TPU v7x, 256 devices: a whole 4x4x8 slice. The times are simulated.
256 devices in a mesh: seg: 8 (over x, core), bond: 32 (over z, y).
Axes of the slice: x: 4, y: 4, z: 8, core: 2. Of those that a mesh axis runs over, the one named last changes fastest.
Arguments:
- state: float32 [8, 32, 256, 256], P('seg', 'bond'), may hold values from -6 to 6
- left_env: bfloat16 [8, 32, 20, 256, 256], P('seg', 'bond'), as said below
- right_env: bfloat16 [8, 32, 20, 256, 256], P('seg', 'bond')
- mpo_mix: float32 [20, 20], replicated, may hold values from -1.25 to 1.25
- block_sizes: int32 [8, 32], P('seg', 'bond'), may hold values from 128 to 256
- ranks: int32 [8, 32], P('seg', 'bond'), may hold values from 64 to 128
Outputs:
- ground: float32 [8, 32, 256, 256], P('seg', 'bond')
- energy: float32 [8], P('seg')
Inputs may be any that keep to these rules, and one draw needn't show every extreme that they name: Every environment matrix left_env[s,b,w] and right_env[s,b,w] is symmetric.
All inputs are finite; a program needn't handle non-finite values.
Results may differ from a plain program's by a relative error of at most 0.014.
Values may be sent and summed in bfloat16 or wider, within the bound.
No kernel may reach another device: no remote copies, remote signals or barrier semaphores. Data moves between devices by JAX's collectives and lax.ppermute only.
A program may use at most 64 MiB of HBM per device.

v0:
```python
import math

import jax
import jax.numpy as jnp
from jax import lax
from jax.experimental import pallas as pl
from jax.experimental.pallas import tpu as pltpu
from jax.sharding import PartitionSpec as P

LANCZOS = 4
POWER = 4


def shifted(value, axis, steps):
    count = lax.axis_size(axis)
    pairs = [(source, (source + steps) % count) for source in range(count)]
    return lax.ppermute(value, axis, pairs)


def bond_sum(value):
    count = lax.axis_size("bond")
    if count & (count - 1):
        return lax.psum(value, "bond")
    step = 1
    while step < count:
        pairs = [(source, source ^ step) for source in range(count)]
        value = value + lax.ppermute(value, "bond", pairs)
        step *= 2
    return value


def apply_ham(vector, left, right, mask):
    rounded = (vector * mask).astype(jnp.bfloat16)
    inner = jnp.einsum("ij,wjk->wik", rounded, right, preferred_element_type=jnp.float32).astype(
        jnp.bfloat16
    )
    outer = jnp.einsum("wij,wjk->ik", left, inner, preferred_element_type=jnp.float32)
    return outer * mask


def gram_kernel(*refs):
    *vec_refs, out_ref = refs
    size = len(vec_refs)
    row = lax.broadcasted_iota(jnp.int32, out_ref.shape, 0)
    lane = lax.broadcasted_iota(jnp.int32, out_ref.shape, 1)
    out = jnp.zeros(out_ref.shape, jnp.float32)
    slot = 0
    for i in range(size):
        for j in range(i, size):
            total = jnp.sum(vec_refs[i][...] * vec_refs[j][...], axis=(0, 1), keepdims=True)
            out = jnp.where((row == 0) & (lane == slot), total, out)
            slot += 1
    out_ref[...] = out


def ritz_kernel(total_ref, out_ref):
    size = LANCZOS + 1
    shape = out_ref.shape
    slots = {}
    slot = 0
    for i in range(size):
        for j in range(i, size):
            slots[i, j] = slots[j, i] = slot
            slot += 1
    entries = {}
    for key in range(slot):
        entries[key] = jnp.full(shape, total_ref[0, key], jnp.float32)
    gram = [[entries[slots[i, j]] for j in range(size)] for i in range(size)]
    zero = jnp.zeros(shape, jnp.float32)

    def quad(first, second):
        acc = zero
        for i in range(size):
            for j in range(size):
                acc = acc + first[i] * gram[i][j] * second[j]
        return acc

    def combine(first, scale_first, second, scale_second):
        return [a * scale_first + b * scale_second for a, b in zip(first, second)]

    vector = [1.0 / jnp.sqrt(gram[0][0])] + [zero] * (size - 1)
    previous = [zero] * size
    beta_prev = zero
    alphas = []
    betas = []
    basis = []
    for step in range(LANCZOS):
        image = [zero] + vector[:-1]
        alpha = quad(image, vector)
        image = [w - alpha * v - beta_prev * p for w, v, p in zip(image, vector, previous)]
        alphas.append(alpha)
        basis.append(vector)
        if step + 1 < LANCZOS:
            beta = jnp.sqrt(quad(image, image))
            betas.append(beta)
            previous = vector
            vector = [w / beta for w in image]
            beta_prev = beta

    def tri_times(weights):
        rows = []
        for i in range(LANCZOS):
            acc = alphas[i] * weights[i]
            if i > 0:
                acc = acc + betas[i - 1] * weights[i - 1]
            if i + 1 < LANCZOS:
                acc = acc + betas[i] * weights[i + 1]
            rows.append(acc)
        return rows

    sigma = None
    for i in range(LANCZOS):
        bound = alphas[i]
        if i > 0:
            bound = bound + jnp.abs(betas[i - 1])
        if i + 1 < LANCZOS:
            bound = bound + jnp.abs(betas[i])
        sigma = bound if sigma is None else jnp.maximum(sigma, bound)
    weights = [zero + 1.0] + [zero] * (LANCZOS - 1)
    for turn in range(POWER):
        product = tri_times(weights)
        weights = [sigma * w - t for w, t in zip(weights, product)]
        norm = zero
        for w in weights:
            norm = norm + w * w
        norm = jnp.sqrt(norm)
        weights = [w / norm for w in weights]
    product = tri_times(weights)
    energy = zero
    for w, t in zip(weights, product):
        energy = energy + w * t
    coef = [c * weights[0] for c in basis[0]]
    for step in range(1, LANCZOS):
        coef = [c + weights[step] * b for c, b in zip(coef, basis[step])]
    lane = lax.broadcasted_iota(jnp.int32, shape, 1)
    out = zero
    for slot in range(LANCZOS):
        out = jnp.where(lane == slot, coef[slot], out)
    out_ref[...] = jnp.where(lane == LANCZOS, energy, out)


def lanczos(start, left, right, mask):
    krylov = [start * mask]
    for step in range(LANCZOS):
        krylov.append(apply_ham(krylov[-1], left, right, mask))
    tile = jax.ShapeDtypeStruct((8, 128), jnp.float32)
    local = pl.pallas_call(gram_kernel, out_shape=tile)(*krylov)
    total = bond_sum(local)
    out = pl.pallas_call(
        ritz_kernel, out_shape=tile, in_specs=[pl.BlockSpec(memory_space=pltpu.SMEM)]
    )(total)
    result = krylov[0] * out[0, 0]
    for step in range(1, LANCZOS):
        result = result + out[0, step] * krylov[step]
    return (result, out[0, LANCZOS])


def env_update(mixed, left_a):
    half_left = jnp.einsum(
        "wij,jk->wik", mixed, left_a, preferred_element_type=jnp.float32
    ).astype(jnp.bfloat16)
    return jnp.einsum(
        "ji,wjk->wik", left_a, half_left, preferred_element_type=jnp.float32
    ).astype(jnp.bfloat16)


def per_device(state, left_env, right_env, mpo_mix, block_sizes, ranks):
    blocks = lax.axis_size("bond")
    width = state.shape[-1]
    start = state[0, 0]
    left = left_env[0, 0]
    right = right_env[0, 0]
    index = jnp.arange(width, dtype=jnp.int32)
    live = (index < block_sizes[0, 0]).astype(jnp.float32)
    mask = live[:, None] * live[None, :]
    kept = (index < ranks[0, 0]).astype(jnp.float32)
    left_mix = jnp.einsum(
        "wu,uij->wij", mpo_mix, left.astype(jnp.float32), precision=lax.Precision.HIGHEST
    ).astype(jnp.bfloat16)
    right_mix = jnp.einsum(
        "wu,uij->wij", mpo_mix, right.astype(jnp.float32), precision=lax.Precision.HIGHEST
    ).astype(jnp.bfloat16)
    left_mix_got = shifted(left_mix, "seg", 1)
    right_mix_got = shifted(right_mix, "seg", -1)
    psi_one, unused = lanczos(start, left, right, mask)
    scaled = psi_one * math.sqrt(blocks * width)
    left_a = (scaled * kept[None, :]).astype(jnp.bfloat16)
    right_a = (scaled * kept[:, None]).astype(jnp.bfloat16)
    left_a_got = shifted(left_a, "seg", 1)
    right_a_got = shifted(right_a, "seg", -1)
    left_in = env_update(left_mix_got, left_a_got)
    right_in = env_update(right_mix_got, right_a_got.T)
    psi_two, energy = lanczos(psi_one, left_in, right_in, mask)
    ground = psi_two * math.sqrt(blocks * width * width)
    return (ground[None, None], jnp.reshape(energy, (1,)))


def solution(mesh):
    in_specs = (
        P("seg", "bond", None, None),
        P("seg", "bond", None, None, None),
        P("seg", "bond", None, None, None),
        P(),
        P("seg", "bond"),
        P("seg", "bond"),
    )
    out_specs = (P("seg", "bond", None, None), P("seg"))
    return jax.shard_map(
        per_device, mesh=mesh, in_specs=in_specs, out_specs=out_specs, check_vma=False
    )
```

profile of v0, /device:TPU:16, one launch (start us, length us, event | category | flops | bytes accessed | tf_op | source)
XLA Modules:
  0.0 140.4 jit_solution(12025516871826509228)
XLA Ops:
  0.6 0.0 copy-start
  0.6 1.7 %copy-done = bf16[1,1,20,256,256]{4,3,2,1,0:T(8,128)(2,1)S(1)} copy-done((bf16[1,1,20,256,256]{4,3,2,1,0:T(8,128)(2,1)S(1)}, bf16[1,1,20,256,256]{4,3,2,1,0:T(8,128)(2,1)}, u32[]{:S(2)}) %copy-start) | copy-done | bytes 2621464
  2.4 4.7 %fusion = bf16[20,256,256]{2,0,1:T(8,128)(2,1)S(1)} fusion(bf16[20,256,256]{2,1,0:T(8,128)(2,1)S(1)} %bitcast.252, f32[20,20]{1,0:T(8,128)} %param.9), kind=kOutput, calls=%fused_computation.2 | convolution fusion | flops 314572800 | bytes 5244480 | tf_op jit(solution)/shard_map/wu,uij->wij/dot_general | solution.py:180
  7.1 0.0 copy-start.1
  7.1 0.0 copy-start.12
  7.1 2.2 %copy.38 = bf16[20,256,256]{2,1,0:T(8,128)(2,1)} copy(bf16[20,256,256]{2,0,1:T(8,128)(2,1)S(1)} %fusion) | data formatting | bytes 5242880 | tf_op jit(solution)/shard_map/wu,uij->wij/dot_general | solution.py:180
  9.3 2.2 %collective-permute-start.7 = (bf16[20,256,256]{2,1,0:T(8,128)(2,1)}, bf16[20,256,256]{2,1,0:T(8,128)(2,1)}, u32[]{:S(2)}, u32[]{:S(2)}) collective-permute-start(bf16[20,256,256]{2,1,0:T(8,128)(2,1)} %copy.38), channel_id=1, source_target_pairs={{0,224},{32,0},{64,32},{96,64},{128,96},{160,128},{192,160},{224,1... | collective-permute-start | bytes 7864328 | tf_op jit(solution)/shard_map/ppermute | solution.py:17
  11.5 0.0 copy-done.1
  11.5 4.2 %fusion.2 = bf16[20,256,256]{2,0,1:T(8,128)(2,1)S(1)} fusion(bf16[20,256,256]{2,1,0:T(8,128)(2,1)S(1)} %bitcast.253, f32[20,20]{1,0:T(8,128)S(1)} %copy-done.12), kind=kOutput, calls=%fused_computation.4 | convolution fusion | flops 314572800 | bytes 5244480 | tf_op jit(solution)/shard_map/wu,uij->wij/dot_general | solution.py:177
  15.6 0.0 copy-start.11
  15.6 2.1 %copy.39 = bf16[20,256,256]{2,1,0:T(8,128)(2,1)} copy(bf16[20,256,256]{2,0,1:T(8,128)(2,1)S(1)} %fusion.2) | data formatting | bytes 5242880 | tf_op jit(solution)/shard_map/wu,uij->wij/dot_general | solution.py:177
  17.7 0.0 collective-permute-start.5
  18.4 4.2 %multiply_multiply_fusion.15.refs_1_ = f32[256,256]{1,0:T(8,128)S(1)} fusion(f32[1,1,256,256]{3,2,1,0:T(8,128)S(1)} %copy-done.11, f32[256]{0:T(256)S(1)} %compare_convert_fusion, bf16[1,1,20,256,256]{4,3,2,1,0:T(8,128)(2,1)} %param.7, bf16[1,1,20,256,256]{4,3,2,1,0:T(8,128)(2,1)S(1)} %copy-done), kind=kOutput, calls=%fused_computation.63 | convolution fusion | flops 1343881216 | bytes 5768192 | tf_op jit(solution)/shard_map/wij,wjk->ik/dot_general | solution.py:37
  22.6 0.8 multiply_multiply_fusion.16.refs_0_
  23.4 4.2 %multiply_multiply_fusion.13.refs_2_ = f32[256,256]{1,0:T(8,128)S(1)} fusion(f32[256,256]{1,0:T(8,128)S(1)} %multiply_multiply_fusion.15.refs_1_, f32[256]{0:T(256)S(1)} %compare_convert_fusion, bf16[1,1,20,256,256]{4,3,2,1,0:T(8,128)(2,1)} %param.7, bf16[1,1,20,256,256]{4,3,2,1,0:T(8,128)(2,1)S(1)} %copy-done), kind=kOutput, calls=%fused_computation.61 | convolution fusion | flops 1343815680 | bytes 5768192 | tf_op jit(solution)/shard_map/wij,wjk->ik/dot_general | solution.py:37
  27.6 4.3 %multiply_multiply_fusion.11.refs_3_ = f32[256,256]{1,0:T(8,128)S(1)} fusion(f32[256,256]{1,0:T(8,128)S(1)} %multiply_multiply_fusion.13.refs_2_, f32[256]{0:T(256)S(1)} %compare_convert_fusion, bf16[1,1,20,256,256]{4,3,2,1,0:T(8,128)(2,1)} %param.7, bf16[1,1,20,256,256]{4,3,2,1,0:T(8,128)(2,1)S(1)} %copy-done), kind=kOutput, calls=%fused_computation.59 | convolution fusion | flops 1343815680 | bytes 5768192 | tf_op jit(solution)/shard_map/wij,wjk->ik/dot_general | solution.py:37
  31.9 0.0 copy-start.10
  32.0 0.0 copy-start.8
  32.0 5.0 %multiply_multiply_fusion.9.refs_4_ = f32[256,256]{1,0:T(8,128)} fusion(f32[256,256]{1,0:T(8,128)S(1)} %multiply_multiply_fusion.11.refs_3_, f32[256]{0:T(256)S(1)} %compare_convert_fusion, bf16[1,1,20,256,256]{4,3,2,1,0:T(8,128)(2,1)} %param.7, bf16[1,1,20,256,256]{4,3,2,1,0:T(8,128)(2,1)S(1)} %copy-done), kind=kOutput, calls=%fused_computation.57 | convolution fusion | flops 1343815680 | bytes 5768192 | tf_op jit(solution)/shard_map/wij,wjk->ik/dot_general | solution.py:37
  37.0 2.3 %shard_map.77 = f32[8,128]{1,0:T(8,128)} custom-call(f32[256,256]{1,0:T(8,128)} %multiply_multiply_fusion.16.refs_0_, f32[256,256]{1,0:T(8,128)} %copy-done.7, f32[256,256]{1,0:T(8,128)} %copy-done.9, f32[256,256]{1,0:T(8,128)} %copy-done.10, f32[256,256]{1,0:T(8,128)} %multiply_multiply_fusion.9.refs_4_), custom_call_target="tpu_custom_call" | custom-call | tf_op jit(solution)/shard_map/pallas_call | solution.py:147
  39.3 1.3 collective-permute-start
  40.6 2.5 %collective-permute-done = f32[8,128]{1,0:T(8,128)S(1)} collective-permute-done((f32[8,128]{1,0:T(8,128)}, f32[8,128]{1,0:T(8,128)S(1)}, u32[]{:S(2)}, u32[]{:S(2)}) %collective-permute-start) | collective-permute-done | bytes 4128 | tf_op jit(solution)/shard_map/ppermute | solution.py:27
  43.1 0.7 add.48
  43.8 0.4 collective-permute-start.1
  44.2 4.7 %collective-permute-done.1 = f32[8,128]{1,0:T(8,128)S(1)} collective-permute-done((f32[8,128]{1,0:T(8,128)S(1)}, f32[8,128]{1,0:T(8,128)S(1)}, u32[]{:S(2)}, u32[]{:S(2)}) %collective-permute-start.1) | collective-permute-done | bytes 4128 | tf_op jit(solution)/shard_map/ppermute | solution.py:27
  48.9 1.9 %collective-permute-start.2 = (f32[8,128]{1,0:T(8,128)S(1)}, f32[8,128]{1,0:T(8,128)S(1)}, u32[]{:S(2)}, u32[]{:S(2)}) collective-permute-start(f32[8,128]{1,0:T(8,128)S(1)} %add.49), channel_id=1, source_target_pairs={{0,4},{1,5},{2,6},{3,7},{4,0},{5,1},{6,2},{7,3},{8,12},{9,13},{10,... | collective-permute-start | bytes 12296 | tf_op jit(solution)/shard_map/ppermute | solution.py:27
  50.8 1.7 %collective-permute-done.2 = f32[8,128]{1,0:T(8,128)S(1)} collective-permute-done((f32[8,128]{1,0:T(8,128)S(1)}, f32[8,128]{1,0:T(8,128)S(1)}, u32[]{:S(2)}, u32[]{:S(2)}) %collective-permute-start.2) | collective-permute-done | bytes 4128 | tf_op jit(solution)/shard_map/ppermute | solution.py:27
  52.5 3.3 %collective-permute-start.3 = (f32[8,128]{1,0:T(8,128)S(1)}, f32[8,128]{1,0:T(8,128)S(1)}, u32[]{:S(2)}, u32[]{:S(2)}) collective-permute-start(f32[8,128]{1,0:T(8,128)S(1)} %add.50), channel_id=1, source_target_pairs={{0,8},{1,9},{2,10},{3,11},{4,12},{5,13},{6,14},{7,15},{8,0},{9,1},... | collective-permute-start | bytes 12296 | tf_op jit(solution)/shard_map/ppermute | solution.py:27
  56.5 0.9 collective-permute-done.3
  57.4 6.8 %collective-permute-start.4 = (f32[8,128]{1,0:T(8,128)S(1)}, f32[8,128]{1,0:T(8,128)S(1)}, u32[]{:S(2)}, u32[]{:S(2)}) collective-permute-start(f32[8,128]{1,0:T(8,128)S(1)} %add.51), channel_id=1, source_target_pairs={{0,16},{1,17},{2,18},{3,19},{4,20},{5,21},{6,22},{7,23},{8,24},{9,... | collective-permute-start | bytes 12296 | tf_op jit(solution)/shard_map/ppermute | solution.py:27
  64.2 1.6 %collective-permute-done.4 = f32[8,128]{1,0:T(8,128)S(1)} collective-permute-done((f32[8,128]{1,0:T(8,128)S(1)}, f32[8,128]{1,0:T(8,128)S(1)}, u32[]{:S(2)}, u32[]{:S(2)}) %collective-permute-start.4) | collective-permute-done | bytes 4128 | tf_op jit(solution)/shard_map/ppermute | solution.py:27
  65.8 0.6 add.52.total_ref
  66.4 1.7 %shard_map.78 = f32[8,128]{1,0:T(8,128)} custom-call(f32[8,128]{1,0:T(8,128)} %add.52.total_ref), custom_call_target="tpu_custom_call" | custom-call | tf_op jit(solution)/shard_map/pallas_call | solution.py:149
  68.1 1.5 %fusion.233 = (f32[1,1]{1,0:T(1,128)}, f32[1,1]{1,0:T(1,128)}, f32[1,1]{1,0:T(1,128)}, f32[1,1]{1,0:T(1,128)}) fusion(f32[8,128]{1,0:T(8,128)} %shard_map.78), kind=kLoop, calls=%fused_computation.131 | loop fusion | bytes 32 | tf_op jit(solution)/shard_map/slice | solution.py:152
  69.6 3.8 %multiply_multiply_fusion.8 = (f32[256,256]{1,0:T(8,128)S(1)}, f32[256,256]{1,0:T(8,128)S(1)}) fusion(f32[256]{0:T(256)S(1)} %compare_convert_fusion, f32[256,256]{1,0:T(8,128)} %copy-done.10, f32[]{:T(128)} %bitcast.24, f32[256,256]{1,0:T(8,128)} %copy-done.9, f32[]{:T(128)} %bitcast.23, f32[256,256]{1,0:T(8,128)S(1)} %copy-done.8, f32[]{:T(128)} %bitcast.22, ...), kind=kLoop, calls=%fused_computation.56 | loop fusion | flops 655360 | bytes 1573904 | tf_op jit(solution)/shard_map/mul | solution.py:143
  73.4 0.1 multiply_convert_fusion.1
  73.5 0.0 collective-permute-start.8
  73.5 0.5 collective-permute-start.6
  74.0 2.0 %collective-permute-done.8 = bf16[256,256]{1,0:T(8,128)(2,1)S(1)} collective-permute-done((bf16[256,256]{1,0:T(8,128)(2,1)S(1)}, bf16[256,256]{1,0:T(8,128)(2,1)S(1)}, u32[]{:S(2)}, u32[]{:S(2)}) %collective-permute-start.8) | collective-permute-done | bytes 131104 | tf_op jit(solution)/shard_map/ppermute | solution.py:17
  76.0 0.0 collective-permute-done.7
  76.0 4.9 %fusion.75 = bf16[20,256,256]{2,1,0:T(8,128)(2,1)} fusion(bf16[20,256,256]{2,1,0:T(8,128)(2,1)} %collective-permute-done.7, bf16[256,256]{1,0:T(8,128)(2,1)S(1)} %collective-permute-done.8), kind=kOutput, calls=%fused_computation.70 | convolution fusion | flops 1344798720 | bytes 5373952 | tf_op jit(solution)/shard_map/ji,wjk->wik/dot_general | solution.py:162
  80.9 0.0 collective-permute-done.6
  80.9 0.0 collective-permute-done.5
  80.9 4.9 %fusion.72 = bf16[20,256,256]{2,1,0:T(8,128)(2,1)} fusion(bf16[20,256,256]{2,1,0:T(8,128)(2,1)} %collective-permute-done.5, bf16[256,256]{1,0:T(8,128)(2,1)S(1)} %collective-permute-done.6), kind=kOutput, calls=%fused_computation.69 | convolution fusion | flops 1344798720 | bytes 5373952 | tf_op jit(solution)/shard_map/ji,wjk->wik/dot_general | solution.py:162
  85.8 4.3 %multiply_multiply_fusion.6.refs_1_ = f32[256,256]{1,0:T(8,128)S(1)} fusion(bf16[20,256,256]{2,1,0:T(8,128)(2,1)} %fusion.75, bf16[20,256,256]{2,1,0:T(8,128)(2,1)} %fusion.72, f32[256,256]{1,0:T(8,128)S(1)} %get-tuple-element.2.refs_0_, f32[256]{0:T(256)S(1)} %compare_convert_fusion), kind=kOutput, calls=%fused_computation.54 | convolution fusion | flops 1343815680 | bytes 5768192 | tf_op jit(solution)/shard_map/wij,wjk->ik/dot_general | solution.py:37
  90.1 4.4 %multiply_multiply_fusion.4.refs_2_ = f32[256,256]{1,0:T(8,128)S(1)} fusion(bf16[20,256,256]{2,1,0:T(8,128)(2,1)} %fusion.75, bf16[20,256,256]{2,1,0:T(8,128)(2,1)} %fusion.72, f32[256,256]{1,0:T(8,128)S(1)} %multiply_multiply_fusion.6.refs_1_, f32[256]{0:T(256)S(1)} %compare_convert_fusion), kind=kOutput, calls=%fused_computation.52 | convolution fusion | flops 1343815680 | bytes 5768192 | tf_op jit(solution)/shard_map/wij,wjk->ik/dot_general | solution.py:37
  94.5 5.1 %multiply_multiply_fusion.2.refs_3_ = f32[256,256]{1,0:T(8,128)} fusion(bf16[20,256,256]{2,1,0:T(8,128)(2,1)} %fusion.75, bf16[20,256,256]{2,1,0:T(8,128)(2,1)} %fusion.72, f32[256,256]{1,0:T(8,128)S(1)} %multiply_multiply_fusion.4.refs_2_, f32[256]{0:T(256)S(1)} %compare_convert_fusion), kind=kOutput, calls=%fused_computation.50 | convolution fusion | flops 1343815680 | bytes 5768192 | tf_op jit(solution)/shard_map/wij,wjk->ik/dot_general | solution.py:37
  99.6 5.1 %multiply_multiply_fusion.refs_4_ = f32[256,256]{1,0:T(8,128)} fusion(bf16[20,256,256]{2,1,0:T(8,128)(2,1)} %fusion.75, bf16[20,256,256]{2,1,0:T(8,128)(2,1)} %fusion.72, f32[256,256]{1,0:T(8,128)} %multiply_multiply_fusion.2.refs_3_, f32[256]{0:T(256)S(1)} %compare_convert_fusion), kind=kOutput, calls=%fused_computation.48 | convolution fusion | flops 1343815680 | bytes 5768192 | tf_op jit(solution)/shard_map/wij,wjk->ik/dot_general | solution.py:37
  104.7 2.3 %shard_map.79 = f32[8,128]{1,0:T(8,128)} custom-call(f32[256,256]{1,0:T(8,128)} %copy-done.2, f32[256,256]{1,0:T(8,128)} %copy-done.4, f32[256,256]{1,0:T(8,128)} %copy-done.6, f32[256,256]{1,0:T(8,128)} %multiply_multiply_fusion.2.refs_3_, f32[256,256]{1,0:T(8,128)} %multiply_multiply_fusion.refs_4_), custom_call_target="tpu_custom_call" | custom-call | tf_op jit(solution)/shard_map/pallas_call | solution.py:147
  107.0 1.3 collective-permute-start.9
  108.3 2.5 %collective-permute-done.9 = f32[8,128]{1,0:T(8,128)S(1)} collective-permute-done((f32[8,128]{1,0:T(8,128)}, f32[8,128]{1,0:T(8,128)S(1)}, u32[]{:S(2)}, u32[]{:S(2)}) %collective-permute-start.9) | collective-permute-done | bytes 4128 | tf_op jit(solution)/shard_map/ppermute | solution.py:27
  110.8 0.7 add.56
  111.5 0.3 collective-permute-start.10
  111.9 4.8 %collective-permute-done.10 = f32[8,128]{1,0:T(8,128)S(1)} collective-permute-done((f32[8,128]{1,0:T(8,128)S(1)}, f32[8,128]{1,0:T(8,128)S(1)}, u32[]{:S(2)}, u32[]{:S(2)}) %collective-permute-start.10) | collective-permute-done | bytes 4128 | tf_op jit(solution)/shard_map/ppermute | solution.py:27
  116.6 1.0 collective-permute-start.11
  117.7 2.6 %collective-permute-done.11 = f32[8,128]{1,0:T(8,128)S(1)} collective-permute-done((f32[8,128]{1,0:T(8,128)S(1)}, f32[8,128]{1,0:T(8,128)S(1)}, u32[]{:S(2)}, u32[]{:S(2)}) %collective-permute-start.11) | collective-permute-done | bytes 4128 | tf_op jit(solution)/shard_map/ppermute | solution.py:27
  120.3 2.0 %collective-permute-start.12 = (f32[8,128]{1,0:T(8,128)S(1)}, f32[8,128]{1,0:T(8,128)S(1)}, u32[]{:S(2)}, u32[]{:S(2)}) collective-permute-start(f32[8,128]{1,0:T(8,128)S(1)} %add.58), channel_id=1, source_target_pairs={{0,8},{1,9},{2,10},{3,11},{4,12},{5,13},{6,14},{7,15},{8,0},{9,1},... | collective-permute-start | bytes 12296 | tf_op jit(solution)/shard_map/ppermute | solution.py:27
  122.3 2.5 %collective-permute-done.12 = f32[8,128]{1,0:T(8,128)S(1)} collective-permute-done((f32[8,128]{1,0:T(8,128)S(1)}, f32[8,128]{1,0:T(8,128)S(1)}, u32[]{:S(2)}, u32[]{:S(2)}) %collective-permute-start.12) | collective-permute-done | bytes 4128 | tf_op jit(solution)/shard_map/ppermute | solution.py:27
  124.8 5.9 %collective-permute-start.13 = (f32[8,128]{1,0:T(8,128)S(1)}, f32[8,128]{1,0:T(8,128)S(1)}, u32[]{:S(2)}, u32[]{:S(2)}) collective-permute-start(f32[8,128]{1,0:T(8,128)S(1)} %add.59), channel_id=1, source_target_pairs={{0,16},{1,17},{2,18},{3,19},{4,20},{5,21},{6,22},{7,23},{8,24},{9,... | collective-permute-start | bytes 12296 | tf_op jit(solution)/shard_map/ppermute | solution.py:27
  130.7 1.6 %collective-permute-done.13 = f32[8,128]{1,0:T(8,128)S(1)} collective-permute-done((f32[8,128]{1,0:T(8,128)S(1)}, f32[8,128]{1,0:T(8,128)S(1)}, u32[]{:S(2)}, u32[]{:S(2)}) %collective-permute-start.13) | collective-permute-done | bytes 4128 | tf_op jit(solution)/shard_map/ppermute | solution.py:27
  132.3 0.6 add.60.total_ref
  132.9 1.7 %shard_map.80 = f32[8,128]{1,0:T(8,128)} custom-call(f32[8,128]{1,0:T(8,128)} %add.60.total_ref), custom_call_target="tpu_custom_call" | custom-call | tf_op jit(solution)/shard_map/pallas_call | solution.py:149
  134.5 1.5 %fusion.232 = (f32[1,1]{1,0:T(1,128)}, f32[1,1]{1,0:T(1,128)}, f32[1,1]{1,0:T(1,128)}, f32[1,1]{1,0:T(1,128)}, f32[1,1]{1,0:T(1,128)}) fusion(f32[8,128]{1,0:T(8,128)} %shard_map.80), kind=kLoop, calls=%fused_computation.130 | loop fusion | bytes 40 | tf_op jit(solution)/shard_map/slice | solution.py:155
  136.1 4.3 %multiply_bitcast_fusion = f32[1,1,256,256]{3,2,1,0:T(8,128)} fusion(f32[256,256]{1,0:T(8,128)} %multiply_multiply_fusion.2.refs_3_, f32[256,256]{1,0:T(8,128)} %copy-done.6, f32[256,256]{1,0:T(8,128)S(1)} %copy-done.5, f32[256,256]{1,0:T(8,128)S(1)} %copy-done.3, f32[]{:T(128)} %bitcast.46, f32[]{:T(128)} %bitcast.45, f32[]{:T(128)} %bitcast.44, f32[]{:T(128)} %bitcast.43), kind=kLoop, calls=%fused_computation.88 | loop fusion | flops 524288 | bytes 1310736 | tf_op jit(solution)/shard_map/broadcast_in_dim | solution.py:195
  (26 shorter events, 0.1 us)
Async XLA Ops:
  0.6 1.7 %copy-start = (bf16[1,1,20,256,256]{4,3,2,1,0:T(8,128)(2,1)S(1)}, bf16[1,1,20,256,256]{4,3,2,1,0:T(8,128)(2,1)}, u32[]{:S(2)}) copy-start(bf16[1,1,20,256,256]{4,3,2,1,0:T(8,128)(2,1)} %param.8) | copy-start | bytes 7864324
  7.1 4.4 %copy-start.1 = (bf16[1,1,20,256,256]{4,3,2,1,0:T(8,128)(2,1)S(1)}, bf16[1,1,20,256,256]{4,3,2,1,0:T(8,128)(2,1)}, u32[]{:S(2)}) copy-start(bf16[1,1,20,256,256]{4,3,2,1,0:T(8,128)(2,1)} %param.7) | copy-start | bytes 7864324
  7.1 4.4 %copy-start.12 = (f32[20,20]{1,0:T(8,128)S(1)}, f32[20,20]{1,0:T(8,128)}, u32[]{:S(2)}) copy-start(f32[20,20]{1,0:T(8,128)} %param.9) | copy-start | bytes 4804
  9.3 66.8 %collective-permute-start.7 = (bf16[20,256,256]{2,1,0:T(8,128)(2,1)}, bf16[20,256,256]{2,1,0:T(8,128)(2,1)}, u32[]{:S(2)}, u32[]{:S(2)}) collective-permute-start(bf16[20,256,256]{2,1,0:T(8,128)(2,1)} %copy.38), channel_id=1, source_target_pairs={{0,224},{32,0},{64,32},{96,64},{128,96},{160,128},{192,160},{224,1... | collective-permute-start | bytes 7864328 | tf_op jit(solution)/shard_map/ppermute | solution.py:17
  15.6 2.8 %copy-start.11 = (f32[1,1,256,256]{3,2,1,0:T(8,128)S(1)}, f32[1,1,256,256]{3,2,1,0:T(8,128)}, u32[]{:S(2)}) copy-start(f32[1,1,256,256]{3,2,1,0:T(8,128)} %param.6) | copy-start | bytes 786436
  17.7 63.2 %collective-permute-start.5 = (bf16[20,256,256]{2,1,0:T(8,128)(2,1)}, bf16[20,256,256]{2,1,0:T(8,128)(2,1)}, u32[]{:S(2)}, u32[]{:S(2)}) collective-permute-start(bf16[20,256,256]{2,1,0:T(8,128)(2,1)} %copy.39), channel_id=1, source_target_pairs={{0,32},{32,64},{64,96},{96,128},{128,160},{160,192},{192,224},{224... | collective-permute-start | bytes 7864328 | tf_op jit(solution)/shard_map/ppermute | solution.py:17
  22.6 5.0 %copy-start.7 = (f32[256,256]{1,0:T(8,128)}, f32[256,256]{1,0:T(8,128)S(1)}, u32[]{:S(2)}) copy-start(f32[256,256]{1,0:T(8,128)S(1)} %multiply_multiply_fusion.15.refs_1_) | copy-start | bytes 786436
  27.6 4.3 %copy-start.9 = (f32[256,256]{1,0:T(8,128)}, f32[256,256]{1,0:T(8,128)S(1)}, u32[]{:S(2)}) copy-start(f32[256,256]{1,0:T(8,128)S(1)} %multiply_multiply_fusion.13.refs_2_) | copy-start | bytes 786436
  31.9 5.0 %copy-start.10 = (f32[256,256]{1,0:T(8,128)}, f32[256,256]{1,0:T(8,128)S(1)}, u32[]{:S(2)}) copy-start(f32[256,256]{1,0:T(8,128)S(1)} %multiply_multiply_fusion.11.refs_3_) | copy-start | bytes 786436
  32.0 37.6 %copy-start.8 = (f32[256,256]{1,0:T(8,128)S(1)}, f32[256,256]{1,0:T(8,128)}, u32[]{:S(2)}) copy-start(f32[256,256]{1,0:T(8,128)} %copy-done.7) | copy-start | bytes 786436
  39.3 3.8 %collective-permute-start = (f32[8,128]{1,0:T(8,128)}, f32[8,128]{1,0:T(8,128)S(1)}, u32[]{:S(2)}, u32[]{:S(2)}) collective-permute-start(f32[8,128]{1,0:T(8,128)} %shard_map.77), channel_id=1, source_target_pairs={{0,1},{1,0},{2,3},{3,2},{4,5},{5,4},{6,7},{7,6},{8,9},{9,8},{10,11... | collective-permute-start | bytes 12296 | tf_op jit(solution)/shard_map/ppermute | solution.py:27
  43.8 5.1 %collective-permute-start.1 = (f32[8,128]{1,0:T(8,128)S(1)}, f32[8,128]{1,0:T(8,128)S(1)}, u32[]{:S(2)}, u32[]{:S(2)}) collective-permute-start(f32[8,128]{1,0:T(8,128)S(1)} %add.48), channel_id=1, source_target_pairs={{0,2},{1,3},{2,0},{3,1},{4,6},{5,7},{6,4},{7,5},{8,10},{9,11},{10,... | collective-permute-start | bytes 12296 | tf_op jit(solution)/shard_map/ppermute | solution.py:27
  48.9 3.6 %collective-permute-start.2 = (f32[8,128]{1,0:T(8,128)S(1)}, f32[8,128]{1,0:T(8,128)S(1)}, u32[]{:S(2)}, u32[]{:S(2)}) collective-permute-start(f32[8,128]{1,0:T(8,128)S(1)} %add.49), channel_id=1, source_target_pairs={{0,4},{1,5},{2,6},{3,7},{4,0},{5,1},{6,2},{7,3},{8,12},{9,13},{10,... | collective-permute-start | bytes 12296 | tf_op jit(solution)/shard_map/ppermute | solution.py:27
  52.5 4.9 %collective-permute-start.3 = (f32[8,128]{1,0:T(8,128)S(1)}, f32[8,128]{1,0:T(8,128)S(1)}, u32[]{:S(2)}, u32[]{:S(2)}) collective-permute-start(f32[8,128]{1,0:T(8,128)S(1)} %add.50), channel_id=1, source_target_pairs={{0,8},{1,9},{2,10},{3,11},{4,12},{5,13},{6,14},{7,15},{8,0},{9,1},... | collective-permute-start | bytes 12296 | tf_op jit(solution)/shard_map/ppermute | solution.py:27
  57.4 8.4 %collective-permute-start.4 = (f32[8,128]{1,0:T(8,128)S(1)}, f32[8,128]{1,0:T(8,128)S(1)}, u32[]{:S(2)}, u32[]{:S(2)}) collective-permute-start(f32[8,128]{1,0:T(8,128)S(1)} %add.51), channel_id=1, source_target_pairs={{0,16},{1,17},{2,18},{3,19},{4,20},{5,21},{6,22},{7,23},{8,24},{9,... | collective-permute-start | bytes 12296 | tf_op jit(solution)/shard_map/ppermute | solution.py:27
  73.4 12.4 %copy-start.2 = (f32[256,256]{1,0:T(8,128)}, f32[256,256]{1,0:T(8,128)S(1)}, u32[]{:S(2)}) copy-start(f32[256,256]{1,0:T(8,128)S(1)} %get-tuple-element.2.refs_0_) | copy-start | bytes 786436
  73.5 2.5 %collective-permute-start.8 = (bf16[256,256]{1,0:T(8,128)(2,1)S(1)}, bf16[256,256]{1,0:T(8,128)(2,1)S(1)}, u32[]{:S(2)}, u32[]{:S(2)}) collective-permute-start(bf16[256,256]{1,0:T(8,128)(2,1)S(1)} %get-tuple-element.5), channel_id=1, source_target_pairs={{0,224},{32,0},{64,32},{96,64},{128,96},{160,128},{192,160},{224,1... | collective-permute-start | bytes 393224 | tf_op jit(solution)/shard_map/ppermute | solution.py:17
  73.5 7.4 %collective-permute-start.6 = (bf16[256,256]{1,0:T(8,128)(2,1)S(1)}, bf16[256,256]{1,0:T(8,128)(2,1)S(1)}, u32[]{:S(2)}, u32[]{:S(2)}) collective-permute-start(bf16[256,256]{1,0:T(8,128)(2,1)S(1)} %get-tuple-element.4), channel_id=1, source_target_pairs={{0,32},{32,64},{64,96},{96,128},{128,160},{160,192},{192,224},{224... | collective-permute-start | bytes 393224 | tf_op jit(solution)/shard_map/ppermute | solution.py:17
  90.1 4.4 %copy-start.4 = (f32[256,256]{1,0:T(8,128)}, f32[256,256]{1,0:T(8,128)S(1)}, u32[]{:S(2)}) copy-start(f32[256,256]{1,0:T(8,128)S(1)} %multiply_multiply_fusion.6.refs_1_) | copy-start | bytes 786436
  94.5 5.1 %copy-start.6 = (f32[256,256]{1,0:T(8,128)}, f32[256,256]{1,0:T(8,128)S(1)}, u32[]{:S(2)}) copy-start(f32[256,256]{1,0:T(8,128)S(1)} %multiply_multiply_fusion.4.refs_2_) | copy-start | bytes 786436
  99.6 36.5 %copy-start.3 = (f32[256,256]{1,0:T(8,128)S(1)}, f32[256,256]{1,0:T(8,128)}, u32[]{:S(2)}) copy-start(f32[256,256]{1,0:T(8,128)} %copy-done.2) | copy-start | bytes 786436
  99.6 36.5 %copy-start.5 = (f32[256,256]{1,0:T(8,128)S(1)}, f32[256,256]{1,0:T(8,128)}, u32[]{:S(2)}) copy-start(f32[256,256]{1,0:T(8,128)} %copy-done.4) | copy-start | bytes 786436
  107.0 3.8 %collective-permute-start.9 = (f32[8,128]{1,0:T(8,128)}, f32[8,128]{1,0:T(8,128)S(1)}, u32[]{:S(2)}, u32[]{:S(2)}) collective-permute-start(f32[8,128]{1,0:T(8,128)} %shard_map.79), channel_id=1, source_target_pairs={{0,1},{1,0},{2,3},{3,2},{4,5},{5,4},{6,7},{7,6},{8,9},{9,8},{10,11... | collective-permute-start | bytes 12296 | tf_op jit(solution)/shard_map/ppermute | solution.py:27
  111.5 5.1 %collective-permute-start.10 = (f32[8,128]{1,0:T(8,128)S(1)}, f32[8,128]{1,0:T(8,128)S(1)}, u32[]{:S(2)}, u32[]{:S(2)}) collective-permute-start(f32[8,128]{1,0:T(8,128)S(1)} %add.56), channel_id=1, source_target_pairs={{0,2},{1,3},{2,0},{3,1},{4,6},{5,7},{6,4},{7,5},{8,10},{9,11},{10,... | collective-permute-start | bytes 12296 | tf_op jit(solution)/shard_map/ppermute | solution.py:27
  116.6 3.6 %collective-permute-start.11 = (f32[8,128]{1,0:T(8,128)S(1)}, f32[8,128]{1,0:T(8,128)S(1)}, u32[]{:S(2)}, u32[]{:S(2)}) collective-permute-start(f32[8,128]{1,0:T(8,128)S(1)} %add.57), channel_id=1, source_target_pairs={{0,4},{1,5},{2,6},{3,7},{4,0},{5,1},{6,2},{7,3},{8,12},{9,13},{10,... | collective-permute-start | bytes 12296 | tf_op jit(solution)/shard_map/ppermute | solution.py:27
  120.3 4.5 %collective-permute-start.12 = (f32[8,128]{1,0:T(8,128)S(1)}, f32[8,128]{1,0:T(8,128)S(1)}, u32[]{:S(2)}, u32[]{:S(2)}) collective-permute-start(f32[8,128]{1,0:T(8,128)S(1)} %add.58), channel_id=1, source_target_pairs={{0,8},{1,9},{2,10},{3,11},{4,12},{5,13},{6,14},{7,15},{8,0},{9,1},... | collective-permute-start | bytes 12296 | tf_op jit(solution)/shard_map/ppermute | solution.py:27
  124.8 7.5 %collective-permute-start.13 = (f32[8,128]{1,0:T(8,128)S(1)}, f32[8,128]{1,0:T(8,128)S(1)}, u32[]{:S(2)}, u32[]{:S(2)}) collective-permute-start(f32[8,128]{1,0:T(8,128)S(1)} %add.59), channel_id=1, source_target_pairs={{0,16},{1,17},{2,18},{3,19},{4,20},{5,21},{6,22},{7,23},{8,24},{9,... | collective-permute-start | bytes 12296 | tf_op jit(solution)/shard_map/ppermute | solution.py:27
where the time goes:
time: 141 us; the launch traced here: 140 us
  matrix products  55.1 us (39%)
  waiting for transfers between devices  27.5 us (20%)
  starting transfers between devices  27 us (19%)
  other arithmetic  11.6 us (8%)
  local copies, waits for them, and re-layouts  9.05 us (6%)
  Pallas kernels  7.99 us (6%)
  between operations  2.17 us (2%)
    dot_general x8, matrix products, apply_ham(): jnp.einsum('wij,wjk->ik', left, inner, preferred_element_type=jnp.float32)  36.5 us
    ppermute x10, waiting for transfers between devices, bond_sum(): value = value + lax.ppermute(value, 'bond', pairs)  25.4 us
    ppermute x10, starting transfers between devices, bond_sum(): value = value + lax.ppermute(value, 'bond', pairs)  24.3 us
    dot_general x2, matrix products, env_update(): jnp.einsum('ji,wjk->wik', left_a, half_left, preferred_element_type=jnp.f...  9.75 us
    dot_general x1, matrix products, per_device(): jnp.einsum('wu,uij->wij', mpo_mix, right.astype(jnp.float32), precision=l...  4.69 us
    pallas_call x2, Pallas kernels, lanczos(): local = pl.pallas_call(gram_kernel, out_shape=tile)(*krylov)  4.65 us
    mul x2, other arithmetic, lanczos(): krylov = [start * mask]  4.61 us
    broadcast_in_dim x1, other arithmetic, per_device(): return (ground[None, None], jnp.reshape(energy, (1,)))  4.31 us
  transfers between devices with their start and end apart: 14, of which 11 were waited for; matrix products, arithmetic and copies ran while one was open for 26% of the time, Pallas kernels for 3%

commit v1 on v0

--- a/solution.py
+++ b/solution.py
@@ -1,3 +1,4 @@
+import functools
 import math
 
 import jax
@@ -139,7 +140,17 @@
     out_ref[...] = jnp.where(lane == LANCZOS, energy, out)
 
 
-def lanczos(start, left, right, mask):
+def combine_kernel(coef_ref, *refs, scale):
+    *vec_refs, out_ref = refs
+    acc = vec_refs[0][...] * coef_ref[0, 0]
+    for step in range(1, len(vec_refs)):
+        acc = acc + coef_ref[0, step] * vec_refs[step][...]
+    if scale is not None:
+        acc = acc * scale
+    out_ref[...] = acc
+
+
+def lanczos(start, left, right, mask, scale=None):
     krylov = [start * mask]
     for step in range(LANCZOS):
         krylov.append(apply_ham(krylov[-1], left, right, mask))
@@ -149,10 +160,13 @@
     out = pl.pallas_call(
         ritz_kernel, out_shape=tile, in_specs=[pl.BlockSpec(memory_space=pltpu.SMEM)]
     )(total)
-    result = krylov[0] * out[0, 0]
-    for step in range(1, LANCZOS):
-        result = result + out[0, step] * krylov[step]
-    return (result, out[0, LANCZOS])
+    vec_spec = pl.BlockSpec(memory_space=pltpu.VMEM)
+    result = pl.pallas_call(
+        functools.partial(combine_kernel, scale=scale),
+        out_shape=jax.ShapeDtypeStruct(start.shape, jnp.float32),
+        in_specs=[pl.BlockSpec(memory_space=pltpu.SMEM)] + [vec_spec] * LANCZOS,
+    )(out, *krylov[:LANCZOS])
+    return (result, krylov[LANCZOS], local, out[0, LANCZOS])
 
 
 def env_update(mixed, left_a):
@@ -174,24 +188,26 @@
     live = (index < block_sizes[0, 0]).astype(jnp.float32)
     mask = live[:, None] * live[None, :]
     kept = (index < ranks[0, 0]).astype(jnp.float32)
+    left_got = shifted(left, "seg", 1)
+    right_got = shifted(right, "seg", -1)
+    psi_one, last, local, unused = lanczos(start, left, right, mask)
+    left_got, right_got, last = lax.optimization_barrier((left_got, right_got, last))
     left_mix = jnp.einsum(
-        "wu,uij->wij", mpo_mix, left.astype(jnp.float32), precision=lax.Precision.HIGHEST
+        "wu,uij->wij", mpo_mix, left_got.astype(jnp.float32), precision=lax.Precision.HIGHEST
     ).astype(jnp.bfloat16)
     right_mix = jnp.einsum(
-        "wu,uij->wij", mpo_mix, right.astype(jnp.float32), precision=lax.Precision.HIGHEST
-    ).astype(jnp.bfloat16)
-    left_mix_got = shifted(left_mix, "seg", 1)
-    right_mix_got = shifted(right_mix, "seg", -1)
-    psi_one, unused = lanczos(start, left, right, mask)
+        "wu,uij->wij", mpo_mix, right_got.astype(jnp.float32), precision=lax.Precision.HIGHEST
+    ).astype(jnp.bfloat16)
     scaled = psi_one * math.sqrt(blocks * width)
     left_a = (scaled * kept[None, :]).astype(jnp.bfloat16)
     right_a = (scaled * kept[:, None]).astype(jnp.bfloat16)
     left_a_got = shifted(left_a, "seg", 1)
     right_a_got = shifted(right_a, "seg", -1)
-    left_in = env_update(left_mix_got, left_a_got)
-    right_in = env_update(right_mix_got, right_a_got.T)
-    psi_two, energy = lanczos(psi_one, left_in, right_in, mask)
-    ground = psi_two * math.sqrt(blocks * width * width)
+    left_in = env_update(left_mix, left_a_got)
+    right_in = env_update(right_mix, right_a_got.T)
+    ground, last, local, energy = lanczos(
+        psi_one, left_in, right_in, mask, math.sqrt(blocks * width * width)
+    )
     return (ground[None, None], jnp.reshape(energy, (1,)))
 
 

time: 141 us -> 136 us (0.965)
  local copies, waits for them, and re-layouts: 9.05 us -> 1.3 us
  other arithmetic: 11.6 us -> 6.11 us
  matrix products: 55.1 us -> 59.1 us
  Pallas kernels: 7.99 us -> 11.9 us
  starting transfers between devices: 27 us -> 29.4 us
  waiting for transfers between devices: 27.5 us -> 25.5 us
    broadcast_in_dim x1 -> x0, other arithmetic: 4.31 us -> none  [per_device(): return (ground[None, None], jnp.reshape(energy, (1,)))]
    dot_general x2 -> x0, local copies, waits for them, and re-layouts: 4.25 us -> none  [the longest x1 2.17 us: per_device(): jnp.einsum('wu,uij->wij', mpo_mix, right.astype(jnp.float32), precision=l...]
    pallas_call x0 -> x2, Pallas kernels: none -> 3.96 us  [lanczos(): pl.pallas_call(functools.partial(combine_kernel, scale=scale), out_shape=...]
    mul x2 -> x1, other arithmetic: 4.61 us -> 1.76 us  [lanczos(): krylov = [start * mask]]
    dot_general x2, matrix products: 8.85 us -> 11.6 us  [the longest x1 6.84 us: per_device(): jnp.einsum('wu,uij->wij', mpo_mix, left_got.astype(jnp.float32), precisio...]
    ppermute x4, starting transfers between devices: 2.71 us -> 5.17 us  [shifted(): return lax.ppermute(value, axis, pairs)]
    ppermute x4, waiting for transfers between devices: 2.02 us -> 0.01 us  [shifted(): return lax.ppermute(value, axis, pairs)]
    unnamed x26 -> x16, local copies, waits for them, and re-layouts: 1.8 us -> 0.04 us
  transfers between devices with their start and end apart: 14 -> 14, of which waited for: 11 -> 10; matrix products, arithmetic and copies ran while one was open for 26% -> 30% of each run, Pallas kernels for 3% -> 4%
where the time goes in v1:
time: 136 us; the launch traced here: 135 us
  matrix products  59.1 us (43%)
  starting transfers between devices  29.4 us (22%)
  waiting for transfers between devices  25.5 us (19%)
  Pallas kernels  11.9 us (9%)
  other arithmetic  6.11 us (4%)
  between operations  2.11 us (2%)
    dot_general x8, matrix products, apply_ham(): jnp.einsum('wij,wjk->ik', left, inner, preferred_element_type=jnp.float32)  36.5 us
    ppermute x10, waiting for transfers between devices, bond_sum(): value = value + lax.ppermute(value, 'bond', pairs)  25.4 us
    ppermute x10, starting transfers between devices, bond_sum(): value = value + lax.ppermute(value, 'bond', pairs)  24.3 us
    dot_general x2, matrix products, env_update(): jnp.einsum('ji,wjk->wik', left_a, half_left, preferred_element_type=jnp.f...  11 us
    dot_general x1, matrix products, per_device(): jnp.einsum('wu,uij->wij', mpo_mix, left_got.astype(jnp.float32), precisio...  6.84 us
    ppermute x4, starting transfers between devices, shifted(): return lax.ppermute(value, axis, pairs)  5.17 us
    dot_general x1, matrix products, per_device(): jnp.einsum('wu,uij->wij', mpo_mix, right_got.astype(jnp.float32), precisi...  4.72 us
    pallas_call x2, Pallas kernels, lanczos(): local = pl.pallas_call(gram_kernel, out_shape=tile)(*krylov)  4.65 us
  transfers between devices with their start and end apart: 14, of which 10 were waited for; matrix products, arithmetic and copies ran while one was open for 30% of the time, Pallas kernels for 4%

profile of v1, /device:TPU:16, one launch (start us, length us, event | category | flops | bytes accessed | tf_op | source)
XLA Modules:
  0.0 135.4 jit_solution(767913650092140152)
XLA Ops:
  0.6 0.0 copy-start
  0.6 2.2 %collective-permute-start.6 = (bf16[20,256,256]{2,1,0:T(8,128)(2,1)}, bf16[20,256,256]{2,1,0:T(8,128)(2,1)S(1)}, u32[]{:S(2)}, u32[]{:S(2)}) collective-permute-start(bf16[20,256,256]{2,1,0:T(8,128)(2,1)} %bitcast.244), channel_id=1, source_target_pairs={{0,224},{32,0},{64,32},{96,64},{128,96},{160,128},{192,160},{224,1... | collective-permute-start | bytes 7864328 | tf_op jit(solution)/shard_map/ppermute | solution.py:18
  2.9 0.0 collective-permute-start.5
  3.5 1.8 %multiply_multiply_fusion.16.refs_0_ = f32[256,256]{1,0:T(8,128)} fusion(f32[1,1,256,256]{3,2,1,0:T(8,128)} %param.6, f32[256]{0:T(256)S(1)} %compare_convert_fusion), kind=kLoop, calls=%fused_computation.66 | loop fusion | flops 131072 | bytes 525312 | tf_op jit(solution)/shard_map/mul | solution.py:154
  5.3 4.4 %multiply_multiply_fusion.15.refs_1_ = f32[256,256]{1,0:T(8,128)S(1)} fusion(f32[1,1,256,256]{3,2,1,0:T(8,128)} %param.6, f32[256]{0:T(256)S(1)} %compare_convert_fusion, bf16[1,1,20,256,256]{4,3,2,1,0:T(8,128)(2,1)} %param.7, bf16[1,1,20,256,256]{4,3,2,1,0:T(8,128)(2,1)} %param.8), kind=kOutput, calls=%fused_computation.65 | convolution fusion | flops 1343881216 | bytes 5768192 | tf_op jit(solution)/shard_map/wij,wjk->ik/dot_general | solution.py:38
  9.6 0.0 copy-start.4
  9.7 4.4 %multiply_multiply_fusion.13.refs_2_ = f32[256,256]{1,0:T(8,128)S(1)} fusion(f32[256,256]{1,0:T(8,128)S(1)} %multiply_multiply_fusion.15.refs_1_, f32[256]{0:T(256)S(1)} %compare_convert_fusion, bf16[1,1,20,256,256]{4,3,2,1,0:T(8,128)(2,1)} %param.7, bf16[1,1,20,256,256]{4,3,2,1,0:T(8,128)(2,1)} %param.8), kind=kOutput, calls=%fused_computation.63 | convolution fusion | flops 1343815680 | bytes 5768192 | tf_op jit(solution)/shard_map/wij,wjk->ik/dot_general | solution.py:38
  14.0 0.0 copy-done.4
  14.0 0.0 copy-start.5
  14.0 4.4 %multiply_multiply_fusion.11.refs_3_ = f32[256,256]{1,0:T(8,128)S(1)} fusion(f32[256,256]{1,0:T(8,128)S(1)} %multiply_multiply_fusion.13.refs_2_, f32[256]{0:T(256)S(1)} %compare_convert_fusion, bf16[1,1,20,256,256]{4,3,2,1,0:T(8,128)(2,1)} %param.7, bf16[1,1,20,256,256]{4,3,2,1,0:T(8,128)(2,1)} %param.8), kind=kOutput, calls=%fused_computation.61 | convolution fusion | flops 1343815680 | bytes 5768192 | tf_op jit(solution)/shard_map/wij,wjk->ik/dot_general | solution.py:38
  18.4 0.0 copy-done.5
  18.4 0.0 copy-start.6
  18.4 5.1 %multiply_multiply_fusion.9.refs_4_ = f32[256,256]{1,0:T(8,128)} fusion(f32[256,256]{1,0:T(8,128)S(1)} %multiply_multiply_fusion.11.refs_3_, f32[256]{0:T(256)S(1)} %compare_convert_fusion, bf16[1,1,20,256,256]{4,3,2,1,0:T(8,128)(2,1)} %param.7, bf16[1,1,20,256,256]{4,3,2,1,0:T(8,128)(2,1)} %param.8), kind=kOutput, calls=%fused_computation.59 | convolution fusion | flops 1343815680 | bytes 5768192 | tf_op jit(solution)/shard_map/wij,wjk->ik/dot_general | solution.py:38
  23.5 0.0 copy-done.6
  23.5 2.3 %shard_map.77 = f32[8,128]{1,0:T(8,128)} custom-call(f32[256,256]{1,0:T(8,128)} %multiply_multiply_fusion.16.refs_0_, f32[256,256]{1,0:T(8,128)} %copy-done.4, f32[256,256]{1,0:T(8,128)} %copy-done.5, f32[256,256]{1,0:T(8,128)} %copy-done.6, f32[256,256]{1,0:T(8,128)} %multiply_multiply_fusion.9.refs_4_), custom_call_target="tpu_custom_call" | custom-call | tf_op jit(solution)/shard_map/pallas_call | solution.py:158
  25.8 1.3 collective-permute-start
  27.1 2.5 %collective-permute-done = f32[8,128]{1,0:T(8,128)S(1)} collective-permute-done((f32[8,128]{1,0:T(8,128)}, f32[8,128]{1,0:T(8,128)S(1)}, u32[]{:S(2)}, u32[]{:S(2)}) %collective-permute-start) | collective-permute-done | bytes 4128 | tf_op jit(solution)/shard_map/ppermute | solution.py:28
  29.6 0.7 add.30
  30.3 0.4 collective-permute-start.1
  30.7 4.7 %collective-permute-done.1 = f32[8,128]{1,0:T(8,128)S(1)} collective-permute-done((f32[8,128]{1,0:T(8,128)S(1)}, f32[8,128]{1,0:T(8,128)S(1)}, u32[]{:S(2)}, u32[]{:S(2)}) %collective-permute-start.1) | collective-permute-done | bytes 4128 | tf_op jit(solution)/shard_map/ppermute | solution.py:28
  35.4 1.9 %collective-permute-start.2 = (f32[8,128]{1,0:T(8,128)S(1)}, f32[8,128]{1,0:T(8,128)S(1)}, u32[]{:S(2)}, u32[]{:S(2)}) collective-permute-start(f32[8,128]{1,0:T(8,128)S(1)} %add.31), channel_id=1, source_target_pairs={{0,4},{1,5},{2,6},{3,7},{4,0},{5,1},{6,2},{7,3},{8,12},{9,13},{10,... | collective-permute-start | bytes 12296 | tf_op jit(solution)/shard_map/ppermute | solution.py:28
  37.4 1.7 %collective-permute-done.2 = f32[8,128]{1,0:T(8,128)S(1)} collective-permute-done((f32[8,128]{1,0:T(8,128)S(1)}, f32[8,128]{1,0:T(8,128)S(1)}, u32[]{:S(2)}, u32[]{:S(2)}) %collective-permute-start.2) | collective-permute-done | bytes 4128 | tf_op jit(solution)/shard_map/ppermute | solution.py:28
  39.0 3.3 %collective-permute-start.3 = (f32[8,128]{1,0:T(8,128)S(1)}, f32[8,128]{1,0:T(8,128)S(1)}, u32[]{:S(2)}, u32[]{:S(2)}) collective-permute-start(f32[8,128]{1,0:T(8,128)S(1)} %add.32), channel_id=1, source_target_pairs={{0,8},{1,9},{2,10},{3,11},{4,12},{5,13},{6,14},{7,15},{8,0},{9,1},... | collective-permute-start | bytes 12296 | tf_op jit(solution)/shard_map/ppermute | solution.py:28
  43.0 0.9 collective-permute-done.3
  43.9 6.8 %collective-permute-start.4 = (f32[8,128]{1,0:T(8,128)S(1)}, f32[8,128]{1,0:T(8,128)S(1)}, u32[]{:S(2)}, u32[]{:S(2)}) collective-permute-start(f32[8,128]{1,0:T(8,128)S(1)} %add.33), channel_id=1, source_target_pairs={{0,16},{1,17},{2,18},{3,19},{4,20},{5,21},{6,22},{7,23},{8,24},{9,... | collective-permute-start | bytes 12296 | tf_op jit(solution)/shard_map/ppermute | solution.py:28
  50.7 1.6 %collective-permute-done.4 = f32[8,128]{1,0:T(8,128)S(1)} collective-permute-done((f32[8,128]{1,0:T(8,128)S(1)}, f32[8,128]{1,0:T(8,128)S(1)}, u32[]{:S(2)}, u32[]{:S(2)}) %collective-permute-start.4) | collective-permute-done | bytes 4128 | tf_op jit(solution)/shard_map/ppermute | solution.py:28
  52.3 0.6 add.34.total_ref
  52.9 1.7 %shard_map.78.coef_ref = f32[8,128]{1,0:T(8,128)} custom-call(f32[8,128]{1,0:T(8,128)} %add.34.total_ref), custom_call_target="tpu_custom_call" | custom-call | tf_op jit(solution)/shard_map/pallas_call | solution.py:160
  54.6 2.0 %shard_map.79 = f32[256,256]{1,0:T(8,128)} custom-call(f32[8,128]{1,0:T(8,128)} %shard_map.78.coef_ref, f32[256,256]{1,0:T(8,128)} %multiply_multiply_fusion.16.refs_0_, f32[256,256]{1,0:T(8,128)} %copy-done.4, f32[256,256]{1,0:T(8,128)} %copy-done.5, f32[256,256]{1,0:T(8,128)} %copy-done.6), custom_call_target="tpu_custom_call" | custom-call | tf_op jit(solution)/shard_map/pallas_call | solution.py:164
  56.6 1.8 %multiply_convert_fusion.1 = (bf16[256,256]{1,0:T(8,128)(2,1)S(1)}, bf16[256,256]{1,0:T(8,128)(2,1)S(1)}, f32[256,256]{1,0:T(8,128)}) fusion(f32[256,256]{1,0:T(8,128)} %shard_map.79, f32[256]{0:T(256)S(1)} %compare_select_fusion, f32[256]{0:T(256)S(1)} %compare_convert_fusion), kind=kLoop, calls=%fused_computation.91 | loop fusion | flops 393216 | bytes 788480 | tf_op jit(solution)/shard_map/convert_element_type | solution.py:202
  58.4 0.0 collective-permute-start.7
  58.4 3.0 %collective-permute-start.8 = (bf16[256,256]{1,0:T(8,128)(2,1)S(1)}, bf16[256,256]{1,0:T(8,128)(2,1)S(1)}, u32[]{:S(2)}, u32[]{:S(2)}) collective-permute-start(bf16[256,256]{1,0:T(8,128)(2,1)S(1)} %get-tuple-element.7), channel_id=1, source_target_pairs={{0,224},{32,0},{64,32},{96,64},{128,96},{160,128},{192,160},{224,1... | collective-permute-start | bytes 393224 | tf_op jit(solution)/shard_map/ppermute | solution.py:18
  61.3 0.0 collective-permute-done.6
  61.3 0.0 collective-permute-done.5
  61.3 0.0 copy-done
  61.3 6.8 %convert_bitcast_fusion.1 = bf16[20,256,256]{2,0,1:T(8,128)(2,1)} fusion(bf16[20,256,256]{2,1,0:T(8,128)(2,1)} %collective-permute-done.5, f32[20,20]{1,0:T(8,128)S(1)} %copy-done), kind=kOutput, calls=%fused_computation.5 | convolution fusion | flops 315883520 | bytes 5244480 | tf_op jit(solution)/shard_map/wu,uij->wij/dot_general | solution.py:195
  68.2 0.0 collective-permute-done.7
  68.2 5.8 %fusion.84 = bf16[20,256,256]{2,1,0:T(8,128)(2,1)} fusion(bf16[20,256,256]{2,0,1:T(8,128)(2,1)} %convert_bitcast_fusion.1, bf16[256,256]{1,0:T(8,128)(2,1)S(1)} %collective-permute-done.7), kind=kOutput, calls=%fused_computation.71 | convolution fusion | flops 1344798720 | bytes 5373952 | tf_op jit(solution)/shard_map/ji,wjk->wik/dot_general | solution.py:176
  74.0 4.7 %convert_bitcast_fusion = bf16[20,256,256]{2,0,1:T(8,128)(2,1)} fusion(bf16[20,256,256]{2,1,0:T(8,128)(2,1)S(1)} %collective-permute-done.6, f32[20,20]{1,0:T(8,128)S(1)} %copy-done), kind=kOutput, calls=%fused_computation.4 | convolution fusion | flops 315883520 | bytes 5244480 | tf_op jit(solution)/shard_map/wu,uij->wij/dot_general | solution.py:198
  78.7 0.0 collective-permute-done.8
  78.7 5.2 %fusion.89 = bf16[20,256,256]{2,1,0:T(8,128)(2,1)} fusion(bf16[20,256,256]{2,0,1:T(8,128)(2,1)} %convert_bitcast_fusion, bf16[256,256]{1,0:T(8,128)(2,1)S(1)} %collective-permute-done.8), kind=kOutput, calls=%fused_computation.72 | convolution fusion | flops 1344798720 | bytes 5373952 | tf_op jit(solution)/shard_map/ji,wjk->wik/dot_general | solution.py:176
  83.9 4.3 %multiply_multiply_fusion.6.refs_1_ = f32[256,256]{1,0:T(8,128)S(1)} fusion(bf16[20,256,256]{2,1,0:T(8,128)(2,1)} %fusion.89, bf16[20,256,256]{2,1,0:T(8,128)(2,1)} %fusion.84, f32[256]{0:T(256)S(1)} %compare_convert_fusion, f32[256,256]{1,0:T(8,128)S(1)} %copy-done.7), kind=kOutput, calls=%fused_computation.56 | convolution fusion | flops 1343881216 | bytes 5768192 | tf_op jit(solution)/shard_map/wij,wjk->ik/dot_general | solution.py:38
  88.3 4.4 %multiply_multiply_fusion.4.refs_2_ = f32[256,256]{1,0:T(8,128)S(1)} fusion(bf16[20,256,256]{2,1,0:T(8,128)(2,1)} %fusion.89, bf16[20,256,256]{2,1,0:T(8,128)(2,1)} %fusion.84, f32[256,256]{1,0:T(8,128)S(1)} %multiply_multiply_fusion.6.refs_1_, f32[256]{0:T(256)S(1)} %compare_convert_fusion), kind=kOutput, calls=%fused_computation.54 | convolution fusion | flops 1343815680 | bytes 5768192 | tf_op jit(solution)/shard_map/wij,wjk->ik/dot_general | solution.py:38
  92.7 4.4 %multiply_multiply_fusion.2.refs_3_ = f32[256,256]{1,0:T(8,128)S(1)} fusion(bf16[20,256,256]{2,1,0:T(8,128)(2,1)} %fusion.89, bf16[20,256,256]{2,1,0:T(8,128)(2,1)} %fusion.84, f32[256,256]{1,0:T(8,128)S(1)} %multiply_multiply_fusion.4.refs_2_, f32[256]{0:T(256)S(1)} %compare_convert_fusion), kind=kOutput, calls=%fused_computation.52 | convolution fusion | flops 1343815680 | bytes 5768192 | tf_op jit(solution)/shard_map/wij,wjk->ik/dot_general | solution.py:38
  97.2 0.0 copy-done.2
  97.2 0.0 copy-start.3
  97.2 5.1 %multiply_multiply_fusion.refs_4_ = f32[256,256]{1,0:T(8,128)} fusion(bf16[20,256,256]{2,1,0:T(8,128)(2,1)} %fusion.89, bf16[20,256,256]{2,1,0:T(8,128)(2,1)} %fusion.84, f32[256,256]{1,0:T(8,128)S(1)} %multiply_multiply_fusion.2.refs_3_, f32[256]{0:T(256)S(1)} %compare_convert_fusion), kind=kOutput, calls=%fused_computation.50 | convolution fusion | flops 1343815680 | bytes 5768192 | tf_op jit(solution)/shard_map/wij,wjk->ik/dot_general | solution.py:38
  102.3 0.0 copy-done.3
  102.3 2.3 %shard_map.80 = f32[8,128]{1,0:T(8,128)} custom-call(f32[256,256]{1,0:T(8,128)} %get-tuple-element.8.refs_0_, f32[256,256]{1,0:T(8,128)} %copy-done.1, f32[256,256]{1,0:T(8,128)} %copy-done.2, f32[256,256]{1,0:T(8,128)} %copy-done.3, f32[256,256]{1,0:T(8,128)} %multiply_multiply_fusion.refs_4_), custom_call_target="tpu_custom_call" | custom-call | tf_op jit(solution)/shard_map/pallas_call | solution.py:158
  104.7 1.3 collective-permute-start.9
  105.9 2.5 %collective-permute-done.9 = f32[8,128]{1,0:T(8,128)S(1)} collective-permute-done((f32[8,128]{1,0:T(8,128)}, f32[8,128]{1,0:T(8,128)S(1)}, u32[]{:S(2)}, u32[]{:S(2)}) %collective-permute-start.9) | collective-permute-done | bytes 4128 | tf_op jit(solution)/shard_map/ppermute | solution.py:28
  108.5 0.7 add.35
  109.2 0.3 collective-permute-start.10
  109.5 4.8 %collective-permute-done.10 = f32[8,128]{1,0:T(8,128)S(1)} collective-permute-done((f32[8,128]{1,0:T(8,128)S(1)}, f32[8,128]{1,0:T(8,128)S(1)}, u32[]{:S(2)}, u32[]{:S(2)}) %collective-permute-start.10) | collective-permute-done | bytes 4128 | tf_op jit(solution)/shard_map/ppermute | solution.py:28
  114.3 1.0 collective-permute-start.11
  115.3 2.6 %collective-permute-done.11 = f32[8,128]{1,0:T(8,128)S(1)} collective-permute-done((f32[8,128]{1,0:T(8,128)S(1)}, f32[8,128]{1,0:T(8,128)S(1)}, u32[]{:S(2)}, u32[]{:S(2)}) %collective-permute-start.11) | collective-permute-done | bytes 4128 | tf_op jit(solution)/shard_map/ppermute | solution.py:28
  117.9 2.0 %collective-permute-start.12 = (f32[8,128]{1,0:T(8,128)S(1)}, f32[8,128]{1,0:T(8,128)S(1)}, u32[]{:S(2)}, u32[]{:S(2)}) collective-permute-start(f32[8,128]{1,0:T(8,128)S(1)} %add.37), channel_id=1, source_target_pairs={{0,8},{1,9},{2,10},{3,11},{4,12},{5,13},{6,14},{7,15},{8,0},{9,1},... | collective-permute-start | bytes 12296 | tf_op jit(solution)/shard_map/ppermute | solution.py:28
  119.9 2.5 %collective-permute-done.12 = f32[8,128]{1,0:T(8,128)S(1)} collective-permute-done((f32[8,128]{1,0:T(8,128)S(1)}, f32[8,128]{1,0:T(8,128)S(1)}, u32[]{:S(2)}, u32[]{:S(2)}) %collective-permute-start.12) | collective-permute-done | bytes 4128 | tf_op jit(solution)/shard_map/ppermute | solution.py:28
  122.4 5.9 %collective-permute-start.13 = (f32[8,128]{1,0:T(8,128)S(1)}, f32[8,128]{1,0:T(8,128)S(1)}, u32[]{:S(2)}, u32[]{:S(2)}) collective-permute-start(f32[8,128]{1,0:T(8,128)S(1)} %add.38), channel_id=1, source_target_pairs={{0,16},{1,17},{2,18},{3,19},{4,20},{5,21},{6,22},{7,23},{8,24},{9,... | collective-permute-start | bytes 12296 | tf_op jit(solution)/shard_map/ppermute | solution.py:28
  128.3 1.6 %collective-permute-done.13 = f32[8,128]{1,0:T(8,128)S(1)} collective-permute-done((f32[8,128]{1,0:T(8,128)S(1)}, f32[8,128]{1,0:T(8,128)S(1)}, u32[]{:S(2)}, u32[]{:S(2)}) %collective-permute-start.13) | collective-permute-done | bytes 4128 | tf_op jit(solution)/shard_map/ppermute | solution.py:28
  129.9 0.6 add.39.total_ref
  130.5 1.7 %shard_map.81.coef_ref = f32[8,128]{1,0:T(8,128)} custom-call(f32[8,128]{1,0:T(8,128)} %add.39.total_ref), custom_call_target="tpu_custom_call" | custom-call | tf_op jit(solution)/shard_map/pallas_call | solution.py:160
  132.2 1.3 slice.3
  133.5 2.0 %shard_map.82 = f32[256,256]{1,0:T(8,128)} custom-call(f32[8,128]{1,0:T(8,128)} %shard_map.81.coef_ref, f32[256,256]{1,0:T(8,128)} %get-tuple-element.8.refs_0_, f32[256,256]{1,0:T(8,128)} %copy-done.1, f32[256,256]{1,0:T(8,128)} %copy-done.2, f32[256,256]{1,0:T(8,128)} %copy-done.3), custom_call_target="tpu_custom_call" | custom-call | tf_op jit(solution)/shard_map/pallas_call | solution.py:164
  (13 shorter events, 0.0 us)
Async XLA Ops:
  0.6 60.7 %copy-start = (f32[20,20]{1,0:T(8,128)S(1)}, f32[20,20]{1,0:T(8,128)}, u32[]{:S(2)}) copy-start(f32[20,20]{1,0:T(8,128)} %param.9) | copy-start | bytes 4804
  0.6 60.7 %collective-permute-start.6 = (bf16[20,256,256]{2,1,0:T(8,128)(2,1)}, bf16[20,256,256]{2,1,0:T(8,128)(2,1)S(1)}, u32[]{:S(2)}, u32[]{:S(2)}) collective-permute-start(bf16[20,256,256]{2,1,0:T(8,128)(2,1)} %bitcast.244), channel_id=1, source_target_pairs={{0,224},{32,0},{64,32},{96,64},{128,96},{160,128},{192,160},{224,1... | collective-permute-start | bytes 7864328 | tf_op jit(solution)/shard_map/ppermute | solution.py:18
  2.9 58.5 %collective-permute-start.5 = (bf16[20,256,256]{2,1,0:T(8,128)(2,1)}, bf16[20,256,256]{2,1,0:T(8,128)(2,1)}, u32[]{:S(2)}, u32[]{:S(2)}) collective-permute-start(bf16[20,256,256]{2,1,0:T(8,128)(2,1)} %bitcast.245), channel_id=1, source_target_pairs={{0,32},{32,64},{64,96},{96,128},{128,160},{160,192},{192,224},{224... | collective-permute-start | bytes 7864328 | tf_op jit(solution)/shard_map/ppermute | solution.py:18
  9.6 4.4 %copy-start.4 = (f32[256,256]{1,0:T(8,128)}, f32[256,256]{1,0:T(8,128)S(1)}, u32[]{:S(2)}) copy-start(f32[256,256]{1,0:T(8,128)S(1)} %multiply_multiply_fusion.15.refs_1_) | copy-start | bytes 786436
  14.0 4.4 %copy-start.5 = (f32[256,256]{1,0:T(8,128)}, f32[256,256]{1,0:T(8,128)S(1)}, u32[]{:S(2)}) copy-start(f32[256,256]{1,0:T(8,128)S(1)} %multiply_multiply_fusion.13.refs_2_) | copy-start | bytes 786436
  18.4 5.1 %copy-start.6 = (f32[256,256]{1,0:T(8,128)}, f32[256,256]{1,0:T(8,128)S(1)}, u32[]{:S(2)}) copy-start(f32[256,256]{1,0:T(8,128)S(1)} %multiply_multiply_fusion.11.refs_3_) | copy-start | bytes 786436
  25.8 3.8 %collective-permute-start = (f32[8,128]{1,0:T(8,128)}, f32[8,128]{1,0:T(8,128)S(1)}, u32[]{:S(2)}, u32[]{:S(2)}) collective-permute-start(f32[8,128]{1,0:T(8,128)} %shard_map.77), channel_id=1, source_target_pairs={{0,1},{1,0},{2,3},{3,2},{4,5},{5,4},{6,7},{7,6},{8,9},{9,8},{10,11... | collective-permute-start | bytes 12296 | tf_op jit(solution)/shard_map/ppermute | solution.py:28
  30.3 5.1 %collective-permute-start.1 = (f32[8,128]{1,0:T(8,128)S(1)}, f32[8,128]{1,0:T(8,128)S(1)}, u32[]{:S(2)}, u32[]{:S(2)}) collective-permute-start(f32[8,128]{1,0:T(8,128)S(1)} %add.30), channel_id=1, source_target_pairs={{0,2},{1,3},{2,0},{3,1},{4,6},{5,7},{6,4},{7,5},{8,10},{9,11},{10,... | collective-permute-start | bytes 12296 | tf_op jit(solution)/shard_map/ppermute | solution.py:28
  35.4 3.6 %collective-permute-start.2 = (f32[8,128]{1,0:T(8,128)S(1)}, f32[8,128]{1,0:T(8,128)S(1)}, u32[]{:S(2)}, u32[]{:S(2)}) collective-permute-start(f32[8,128]{1,0:T(8,128)S(1)} %add.31), channel_id=1, source_target_pairs={{0,4},{1,5},{2,6},{3,7},{4,0},{5,1},{6,2},{7,3},{8,12},{9,13},{10,... | collective-permute-start | bytes 12296 | tf_op jit(solution)/shard_map/ppermute | solution.py:28
  39.0 4.9 %collective-permute-start.3 = (f32[8,128]{1,0:T(8,128)S(1)}, f32[8,128]{1,0:T(8,128)S(1)}, u32[]{:S(2)}, u32[]{:S(2)}) collective-permute-start(f32[8,128]{1,0:T(8,128)S(1)} %add.32), channel_id=1, source_target_pairs={{0,8},{1,9},{2,10},{3,11},{4,12},{5,13},{6,14},{7,15},{8,0},{9,1},... | collective-permute-start | bytes 12296 | tf_op jit(solution)/shard_map/ppermute | solution.py:28
  43.9 8.4 %collective-permute-start.4 = (f32[8,128]{1,0:T(8,128)S(1)}, f32[8,128]{1,0:T(8,128)S(1)}, u32[]{:S(2)}, u32[]{:S(2)}) collective-permute-start(f32[8,128]{1,0:T(8,128)S(1)} %add.33), channel_id=1, source_target_pairs={{0,16},{1,17},{2,18},{3,19},{4,20},{5,21},{6,22},{7,23},{8,24},{9,... | collective-permute-start | bytes 12296 | tf_op jit(solution)/shard_map/ppermute | solution.py:28
  58.4 9.8 %collective-permute-start.7 = (bf16[256,256]{1,0:T(8,128)(2,1)S(1)}, bf16[256,256]{1,0:T(8,128)(2,1)S(1)}, u32[]{:S(2)}, u32[]{:S(2)}) collective-permute-start(bf16[256,256]{1,0:T(8,128)(2,1)S(1)} %get-tuple-element.6), channel_id=1, source_target_pairs={{0,32},{32,64},{64,96},{96,128},{128,160},{160,192},{192,224},{224... | collective-permute-start | bytes 393224 | tf_op jit(solution)/shard_map/ppermute | solution.py:18
  58.4 20.3 %collective-permute-start.8 = (bf16[256,256]{1,0:T(8,128)(2,1)S(1)}, bf16[256,256]{1,0:T(8,128)(2,1)S(1)}, u32[]{:S(2)}, u32[]{:S(2)}) collective-permute-start(bf16[256,256]{1,0:T(8,128)(2,1)S(1)} %get-tuple-element.7), channel_id=1, source_target_pairs={{0,224},{32,0},{64,32},{96,64},{128,96},{160,128},{192,160},{224,1... | collective-permute-start | bytes 393224 | tf_op jit(solution)/shard_map/ppermute | solution.py:18
  78.7 5.2 %copy-start.7 = (f32[256,256]{1,0:T(8,128)S(1)}, f32[256,256]{1,0:T(8,128)}, u32[]{:S(2)}) copy-start(f32[256,256]{1,0:T(8,128)} %shard_map.79) | copy-start | bytes 786436
  88.3 4.4 %copy-start.1 = (f32[256,256]{1,0:T(8,128)}, f32[256,256]{1,0:T(8,128)S(1)}, u32[]{:S(2)}) copy-start(f32[256,256]{1,0:T(8,128)S(1)} %multiply_multiply_fusion.6.refs_1_) | copy-start | bytes 786436
  92.7 4.4 %copy-start.2 = (f32[256,256]{1,0:T(8,128)}, f32[256,256]{1,0:T(8,128)S(1)}, u32[]{:S(2)}) copy-start(f32[256,256]{1,0:T(8,128)S(1)} %multiply_multiply_fusion.4.refs_2_) | copy-start | bytes 786436
  97.2 5.1 %copy-start.3 = (f32[256,256]{1,0:T(8,128)}, f32[256,256]{1,0:T(8,128)S(1)}, u32[]{:S(2)}) copy-start(f32[256,256]{1,0:T(8,128)S(1)} %multiply_multiply_fusion.2.refs_3_) | copy-start | bytes 786436
  104.7 3.8 %collective-permute-start.9 = (f32[8,128]{1,0:T(8,128)}, f32[8,128]{1,0:T(8,128)S(1)}, u32[]{:S(2)}, u32[]{:S(2)}) collective-permute-start(f32[8,128]{1,0:T(8,128)} %shard_map.80), channel_id=1, source_target_pairs={{0,1},{1,0},{2,3},{3,2},{4,5},{5,4},{6,7},{7,6},{8,9},{9,8},{10,11... | collective-permute-start | bytes 12296 | tf_op jit(solution)/shard_map/ppermute | solution.py:28
  109.2 5.1 %collective-permute-start.10 = (f32[8,128]{1,0:T(8,128)S(1)}, f32[8,128]{1,0:T(8,128)S(1)}, u32[]{:S(2)}, u32[]{:S(2)}) collective-permute-start(f32[8,128]{1,0:T(8,128)S(1)} %add.35), channel_id=1, source_target_pairs={{0,2},{1,3},{2,0},{3,1},{4,6},{5,7},{6,4},{7,5},{8,10},{9,11},{10,... | collective-permute-start | bytes 12296 | tf_op jit(solution)/shard_map/ppermute | solution.py:28
  114.3 3.6 %collective-permute-start.11 = (f32[8,128]{1,0:T(8,128)S(1)}, f32[8,128]{1,0:T(8,128)S(1)}, u32[]{:S(2)}, u32[]{:S(2)}) collective-permute-start(f32[8,128]{1,0:T(8,128)S(1)} %add.36), channel_id=1, source_target_pairs={{0,4},{1,5},{2,6},{3,7},{4,0},{5,1},{6,2},{7,3},{8,12},{9,13},{10,... | collective-permute-start | bytes 12296 | tf_op jit(solution)/shard_map/ppermute | solution.py:28
  117.9 4.5 %collective-permute-start.12 = (f32[8,128]{1,0:T(8,128)S(1)}, f32[8,128]{1,0:T(8,128)S(1)}, u32[]{:S(2)}, u32[]{:S(2)}) collective-permute-start(f32[8,128]{1,0:T(8,128)S(1)} %add.37), channel_id=1, source_target_pairs={{0,8},{1,9},{2,10},{3,11},{4,12},{5,13},{6,14},{7,15},{8,0},{9,1},... | collective-permute-start | bytes 12296 | tf_op jit(solution)/shard_map/ppermute | solution.py:28
  122.4 7.5 %collective-permute-start.13 = (f32[8,128]{1,0:T(8,128)S(1)}, f32[8,128]{1,0:T(8,128)S(1)}, u32[]{:S(2)}, u32[]{:S(2)}) collective-permute-start(f32[8,128]{1,0:T(8,128)S(1)} %add.38), channel_id=1, source_target_pairs={{0,16},{1,17},{2,18},{3,19},{4,20},{5,21},{6,22},{7,23},{8,24},{9,... | collective-permute-start | bytes 12296 | tf_op jit(solution)/shard_map/ppermute | solution.py:28

commit v2 on v1

--- a/solution.py
+++ b/solution.py
@@ -39,7 +39,7 @@
     return outer * mask
 
 
-def gram_kernel(*refs):
+def gram_kernel(head_ref, *refs):
     *vec_refs, out_ref = refs
     size = len(vec_refs)
     row = lax.broadcasted_iota(jnp.int32, out_ref.shape, 0)
@@ -48,7 +48,11 @@
     slot = 0
     for i in range(size):
         for j in range(i, size):
-            total = jnp.sum(vec_refs[i][...] * vec_refs[j][...], axis=(0, 1), keepdims=True)
+            if i == 0 and j == 0:
+                head = head_ref[...]
+                total = jnp.sum(head * head, axis=(0, 1), keepdims=True)
+            else:
+                total = jnp.sum(vec_refs[i][...] * vec_refs[j][...], axis=(0, 1), keepdims=True)
             out = jnp.where((row == 0) & (lane == slot), total, out)
             slot += 1
     out_ref[...] = out
@@ -140,22 +144,33 @@
     out_ref[...] = jnp.where(lane == LANCZOS, energy, out)
 
 
-def combine_kernel(coef_ref, *refs, scale):
+def combine_kernel(coef_ref, head_ref, *refs, scale):
     *vec_refs, out_ref = refs
+    rows, cols = vec_refs[0].shape
     acc = vec_refs[0][...] * coef_ref[0, 0]
     for step in range(1, len(vec_refs)):
         acc = acc + coef_ref[0, step] * vec_refs[step][...]
     if scale is not None:
         acc = acc * scale
-    out_ref[...] = acc
-
-
-def lanczos(start, left, right, mask, scale=None):
-    krylov = [start * mask]
+    if head_ref.shape != vec_refs[0].shape:
+        rest = head_ref[...] * coef_ref[0, 0]
+        if scale is not None:
+            rest = rest * scale
+        out_ref[...] = rest
+    out_ref[:rows, :cols] = acc
+
+
+def lanczos(start, left, right, mask, scale=None, cut=None):
+    head = start * mask
+    if cut is None:
+        base, live = head, mask
+    else:
+        base, live = head[:cut, :cut], mask[:cut, :cut]
+    krylov = [base]
     for step in range(LANCZOS):
-        krylov.append(apply_ham(krylov[-1], left, right, mask))
+        krylov.append(apply_ham(krylov[-1], left, right, live))
     tile = jax.ShapeDtypeStruct((8, 128), jnp.float32)
-    local = pl.pallas_call(gram_kernel, out_shape=tile)(*krylov)
+    local = pl.pallas_call(gram_kernel, out_shape=tile)(head, *krylov)
     total = bond_sum(local)
     out = pl.pallas_call(
         ritz_kernel, out_shape=tile, in_specs=[pl.BlockSpec(memory_space=pltpu.SMEM)]
@@ -163,9 +178,9 @@
     vec_spec = pl.BlockSpec(memory_space=pltpu.VMEM)
     result = pl.pallas_call(
         functools.partial(combine_kernel, scale=scale),
-        out_shape=jax.ShapeDtypeStruct(start.shape, jnp.float32),
-        in_specs=[pl.BlockSpec(memory_space=pltpu.SMEM)] + [vec_spec] * LANCZOS,
-    )(out, *krylov[:LANCZOS])
+        out_shape=jax.ShapeDtypeStruct(head.shape, jnp.float32),
+        in_specs=[pl.BlockSpec(memory_space=pltpu.SMEM)] + [vec_spec] * (LANCZOS + 1),
+    )(out, head, *krylov[:LANCZOS])
     return (result, krylov[LANCZOS], local, out[0, LANCZOS])
 
 
@@ -199,14 +214,15 @@
         "wu,uij->wij", mpo_mix, right_got.astype(jnp.float32), precision=lax.Precision.HIGHEST
     ).astype(jnp.bfloat16)
     scaled = psi_one * math.sqrt(blocks * width)
-    left_a = (scaled * kept[None, :]).astype(jnp.bfloat16)
-    right_a = (scaled * kept[:, None]).astype(jnp.bfloat16)
+    cut = width // 2
+    left_a = (scaled[:, :cut] * kept[None, :cut]).astype(jnp.bfloat16)
+    right_a = (scaled[:cut, :] * kept[:cut, None]).astype(jnp.bfloat16)
     left_a_got = shifted(left_a, "seg", 1)
     right_a_got = shifted(right_a, "seg", -1)
     left_in = env_update(left_mix, left_a_got)
     right_in = env_update(right_mix, right_a_got.T)
     ground, last, local, energy = lanczos(
-        psi_one, left_in, right_in, mask, math.sqrt(blocks * width * width)
+        psi_one, left_in, right_in, mask, math.sqrt(blocks * width * width), cut
     )
     return (ground[None, None], jnp.reshape(energy, (1,)))
 

time: 136 us -> 115 us (0.85)
  matrix products: 59.1 us -> 39.9 us
  other arithmetic: 6.11 us -> 4.53 us
    dot_general x8, matrix products: 36.5 us -> 21.4 us  [apply_ham(): jnp.einsum('wij,wjk->ik', left, inner, preferred_element_type=jnp.float32)]
    dot_general x2, matrix products: 11 us -> 6.92 us  [env_update(): jnp.einsum('ji,wjk->wik', left_a, half_left, preferred_element_type=jnp.f...]
    convert_element_type x1 -> x2, other arithmetic: 1.78 us -> 0.1 us  [the longest x1 0.08 us: per_device(): right_a = (scaled[:cut, :] * kept[:cut, None]).astype(jnp.bfloat16)]
  transfers between devices with their start and end apart: 14 -> 14, of which waited for: 10 -> 10; matrix products, arithmetic and copies ran while one was open for 30% -> 32% of each run, Pallas kernels for 4% -> 5%
where the time goes in v2:
time: 115 us
  matrix products  39.9 us (35%)
  starting transfers between devices  29.5 us (26%)
  waiting for transfers between devices  25.4 us (22%)
  Pallas kernels  11.4 us (10%)
  other arithmetic  4.53 us (4%)
  between operations  2.16 us (2%)
  local copies, waits for them, and re-layouts  1.98 us (2%)
    ppermute x10, waiting for transfers between devices, bond_sum(): value = value + lax.ppermute(value, 'bond', pairs)  25.4 us
    ppermute x10, starting transfers between devices, bond_sum(): value = value + lax.ppermute(value, 'bond', pairs)  24.3 us
    dot_general x8, matrix products, apply_ham(): jnp.einsum('wij,wjk->ik', left, inner, preferred_element_type=jnp.float32)  21.4 us
    dot_general x2, matrix products, env_update(): jnp.einsum('ji,wjk->wik', left_a, half_left, preferred_element_type=jnp.f...  6.92 us
    dot_general x1, matrix products, per_device(): jnp.einsum('wu,uij->wij', mpo_mix, left_got.astype(jnp.float32), precisio...  6.84 us
    ppermute x4, starting transfers between devices, shifted(): return lax.ppermute(value, axis, pairs)  5.18 us
    dot_general x1, matrix products, per_device(): jnp.einsum('wu,uij->wij', mpo_mix, right_got.astype(jnp.float32), precisi...  4.79 us
    pallas_call x2, Pallas kernels, lanczos(): local = pl.pallas_call(gram_kernel, out_shape=tile)(head, *krylov)  4.26 us
  transfers between devices with their start and end apart: 14, of which 10 were waited for; matrix products, arithmetic and copies ran while one was open for 32% of the time, Pallas kernels for 5%

profile of v2, /device:TPU:16, one launch (start us, length us, event | category | flops | bytes accessed | tf_op | source)
XLA Modules:
  0.0 114.9 jit_solution(12162076820769142659)
XLA Ops:
  0.6 0.0 copy-start
  0.6 2.2 %collective-permute-start.6 = (bf16[20,256,256]{2,1,0:T(8,128)(2,1)}, bf16[20,256,256]{2,1,0:T(8,128)(2,1)S(1)}, u32[]{:S(2)}, u32[]{:S(2)}) collective-permute-start(bf16[20,256,256]{2,1,0:T(8,128)(2,1)} %bitcast.194), channel_id=1, source_target_pairs={{0,224},{32,0},{64,32},{96,64},{128,96},{160,128},{192,160},{224,1... | collective-permute-start | bytes 7864328 | tf_op jit(solution)/shard_map/ppermute | solution.py:18
  2.9 0.0 collective-permute-start.5
  3.5 0.0 copy-start.8
  3.5 4.4 %fusion.67.refs_1_ = f32[256,256]{1,0:T(8,128)S(1)} fusion(f32[1,1,256,256]{3,2,1,0:T(8,128)} %param.6, f32[256]{0:T(256)S(1)} %compare_convert_fusion, bf16[1,1,20,256,256]{4,3,2,1,0:T(8,128)(2,1)} %param.7, bf16[1,1,20,256,256]{4,3,2,1,0:T(8,128)(2,1)} %param.8), kind=kOutput, calls=%fused_computation.47 | convolution fusion | flops 1343881216 | bytes 5768192 | tf_op jit(solution)/shard_map/wij,wjk->ik/dot_general | solution.py:38
  7.9 0.0 copy-done.8
  7.9 0.0 copy-start.5
  8.0 0.8 multiply_multiply_fusion.4.head_ref.refs_0_
  8.8 4.3 %fusion.73.refs_2_ = f32[256,256]{1,0:T(8,128)S(1)} fusion(f32[256,256]{1,0:T(8,128)S(1)} %fusion.67.refs_1_, f32[256]{0:T(256)S(1)} %compare_convert_fusion, bf16[1,1,20,256,256]{4,3,2,1,0:T(8,128)(2,1)} %param.7, bf16[1,1,20,256,256]{4,3,2,1,0:T(8,128)(2,1)} %param.8), kind=kOutput, calls=%fused_computation.49 | convolution fusion | flops 1343815680 | bytes 5768192 | tf_op jit(solution)/shard_map/wij,wjk->ik/dot_general | solution.py:38
  13.0 0.0 copy-done.5
  13.0 0.0 copy-start.6
  13.1 4.4 %fusion.79.refs_3_ = f32[256,256]{1,0:T(8,128)S(1)} fusion(f32[256,256]{1,0:T(8,128)S(1)} %fusion.73.refs_2_, f32[256]{0:T(256)S(1)} %compare_convert_fusion, bf16[1,1,20,256,256]{4,3,2,1,0:T(8,128)(2,1)} %param.7, bf16[1,1,20,256,256]{4,3,2,1,0:T(8,128)(2,1)} %param.8), kind=kOutput, calls=%fused_computation.51 | convolution fusion | flops 1343815680 | bytes 5768192 | tf_op jit(solution)/shard_map/wij,wjk->ik/dot_general | solution.py:38
  17.4 0.0 copy-done.6
  17.4 0.0 copy-start.7
  17.4 5.1 %fusion.85.refs_4_ = f32[256,256]{1,0:T(8,128)} fusion(f32[256,256]{1,0:T(8,128)S(1)} %fusion.79.refs_3_, f32[256]{0:T(256)S(1)} %compare_convert_fusion, bf16[1,1,20,256,256]{4,3,2,1,0:T(8,128)(2,1)} %param.7, bf16[1,1,20,256,256]{4,3,2,1,0:T(8,128)(2,1)} %param.8), kind=kOutput, calls=%fused_computation.53 | convolution fusion | flops 1343815680 | bytes 5768192 | tf_op jit(solution)/shard_map/wij,wjk->ik/dot_general | solution.py:38
  22.5 2.4 %shard_map.77 = f32[8,128]{1,0:T(8,128)} custom-call(f32[256,256]{1,0:T(8,128)} %multiply_multiply_fusion.4.head_ref.refs_0_, f32[256,256]{1,0:T(8,128)} %multiply_multiply_fusion.4.head_ref.refs_0_, f32[256,256]{1,0:T(8,128)} %copy-done.5, f32[256,256]{1,0:T(8,128)} %copy-done.6, f32[256,256]{1,0:T(8,128)} %copy-done.7, f32[256,256]{1,0:T(8,128)} %fusion.85.refs_4_), custom_call_target="tpu_custom_call" | custom-call | tf_op jit(solution)/shard_map/pallas_call | solution.py:173
  24.9 1.3 %collective-permute-start = (f32[8,128]{1,0:T(8,128)}, f32[8,128]{1,0:T(8,128)S(1)}, u32[]{:S(2)}, u32[]{:S(2)}) collective-permute-start(f32[8,128]{1,0:T(8,128)} %shard_map.77), channel_id=1, source_target_pairs={{0,1},{1,0},{2,3},{3,2},{4,5},{5,4},{6,7},{7,6},{8,9},{9,8},{10,11... | collective-permute-start | bytes 12296 | tf_op jit(solution)/shard_map/ppermute | solution.py:28
  26.2 2.5 %collective-permute-done = f32[8,128]{1,0:T(8,128)S(1)} collective-permute-done((f32[8,128]{1,0:T(8,128)}, f32[8,128]{1,0:T(8,128)S(1)}, u32[]{:S(2)}, u32[]{:S(2)}) %collective-permute-start) | collective-permute-done | bytes 4128 | tf_op jit(solution)/shard_map/ppermute | solution.py:28
  28.7 0.7 add.30
  29.4 0.4 collective-permute-start.1
  29.8 4.7 %collective-permute-done.1 = f32[8,128]{1,0:T(8,128)S(1)} collective-permute-done((f32[8,128]{1,0:T(8,128)S(1)}, f32[8,128]{1,0:T(8,128)S(1)}, u32[]{:S(2)}, u32[]{:S(2)}) %collective-permute-start.1) | collective-permute-done | bytes 4128 | tf_op jit(solution)/shard_map/ppermute | solution.py:28
  34.5 1.9 %collective-permute-start.2 = (f32[8,128]{1,0:T(8,128)S(1)}, f32[8,128]{1,0:T(8,128)S(1)}, u32[]{:S(2)}, u32[]{:S(2)}) collective-permute-start(f32[8,128]{1,0:T(8,128)S(1)} %add.31), channel_id=1, source_target_pairs={{0,4},{1,5},{2,6},{3,7},{4,0},{5,1},{6,2},{7,3},{8,12},{9,13},{10,... | collective-permute-start | bytes 12296 | tf_op jit(solution)/shard_map/ppermute | solution.py:28
  37.1 1.0 collective-permute-done.2
  38.1 3.3 %collective-permute-start.3 = (f32[8,128]{1,0:T(8,128)S(1)}, f32[8,128]{1,0:T(8,128)S(1)}, u32[]{:S(2)}, u32[]{:S(2)}) collective-permute-start(f32[8,128]{1,0:T(8,128)S(1)} %add.32), channel_id=1, source_target_pairs={{0,8},{1,9},{2,10},{3,11},{4,12},{5,13},{6,14},{7,15},{8,0},{9,1},... | collective-permute-start | bytes 12296 | tf_op jit(solution)/shard_map/ppermute | solution.py:28
  41.5 1.6 %collective-permute-done.3 = f32[8,128]{1,0:T(8,128)S(1)} collective-permute-done((f32[8,128]{1,0:T(8,128)S(1)}, f32[8,128]{1,0:T(8,128)S(1)}, u32[]{:S(2)}, u32[]{:S(2)}) %collective-permute-start.3) | collective-permute-done | bytes 4128 | tf_op jit(solution)/shard_map/ppermute | solution.py:28
  43.0 6.8 %collective-permute-start.4 = (f32[8,128]{1,0:T(8,128)S(1)}, f32[8,128]{1,0:T(8,128)S(1)}, u32[]{:S(2)}, u32[]{:S(2)}) collective-permute-start(f32[8,128]{1,0:T(8,128)S(1)} %add.33), channel_id=1, source_target_pairs={{0,16},{1,17},{2,18},{3,19},{4,20},{5,21},{6,22},{7,23},{8,24},{9,... | collective-permute-start | bytes 12296 | tf_op jit(solution)/shard_map/ppermute | solution.py:28
  49.9 1.6 %collective-permute-done.4 = f32[8,128]{1,0:T(8,128)S(1)} collective-permute-done((f32[8,128]{1,0:T(8,128)S(1)}, f32[8,128]{1,0:T(8,128)S(1)}, u32[]{:S(2)}, u32[]{:S(2)}) %collective-permute-start.4) | collective-permute-done | bytes 4128 | tf_op jit(solution)/shard_map/ppermute | solution.py:28
  51.4 0.6 add.34.total_ref
  52.0 1.7 %shard_map.78.coef_ref = f32[8,128]{1,0:T(8,128)} custom-call(f32[8,128]{1,0:T(8,128)} %add.34.total_ref), custom_call_target="tpu_custom_call" | custom-call | tf_op jit(solution)/shard_map/pallas_call | solution.py:175
  53.7 2.0 %shard_map.79 = f32[256,256]{1,0:T(8,128)} custom-call(f32[8,128]{1,0:T(8,128)} %shard_map.78.coef_ref, f32[256,256]{1,0:T(8,128)} %multiply_multiply_fusion.4.head_ref.refs_0_, f32[256,256]{1,0:T(8,128)} %multiply_multiply_fusion.4.head_ref.refs_0_, f32[256,256]{1,0:T(8,128)} %copy-done.5, f32[256,256]{1,0:T(8,128)} %copy-done.6, f32[256,256]{1,0:T(8,128)} %copy-done.7), custom_call_target="tpu_custom_call" | custom-call | tf_op jit(solution)/shard_map/pallas_call | solution.py:179
  55.7 1.0 broadcast_multiply_fusion
  56.8 0.7 slice.29.refs_0_
  57.5 0.0 collective-permute-start.7
  57.5 0.1 fusion.112
  57.6 3.0 %collective-permute-start.8 = (bf16[128,256]{1,0:T(8,128)(2,1)S(1)}, bf16[128,256]{1,0:T(8,128)(2,1)S(1)}, u32[]{:S(2)}, u32[]{:S(2)}) collective-permute-start(bf16[128,256]{1,0:T(8,128)(2,1)S(1)} %fusion.112), channel_id=1, source_target_pairs={{0,224},{32,0},{64,32},{96,64},{128,96},{160,128},{192,160},{224,1... | collective-permute-start | bytes 196616 | tf_op jit(solution)/shard_map/ppermute | solution.py:18
  60.6 0.0 collective-permute-done.6
  60.6 0.0 collective-permute-done.5
  60.6 0.0 copy-done
  60.6 6.8 %convert_bitcast_fusion.1 = bf16[20,256,256]{2,0,1:T(8,128)(2,1)} fusion(bf16[20,256,256]{2,1,0:T(8,128)(2,1)} %collective-permute-done.5, f32[20,20]{1,0:T(8,128)S(1)} %copy-done), kind=kOutput, calls=%fused_computation.5 | convolution fusion | flops 315883520 | bytes 5244480 | tf_op jit(solution)/shard_map/wu,uij->wij/dot_general | solution.py:210
  67.4 4.8 %convert_bitcast_fusion = bf16[20,256,256]{2,0,1:T(8,128)(2,1)} fusion(bf16[20,256,256]{2,1,0:T(8,128)(2,1)S(1)} %collective-permute-done.6, f32[20,20]{1,0:T(8,128)S(1)} %copy-done), kind=kOutput, calls=%fused_computation.4 | convolution fusion | flops 315883520 | bytes 5244480 | tf_op jit(solution)/shard_map/wu,uij->wij/dot_general | solution.py:213
  72.2 0.0 collective-permute-done.7
  72.2 3.5 %fusion.53 = bf16[20,128,128]{1,2,0:T(8,128)(2,1)S(1)} fusion(bf16[20,256,256]{2,0,1:T(8,128)(2,1)} %convert_bitcast_fusion.1, bf16[256,128]{1,0:T(8,128)(2,1)S(1)} %collective-permute-done.7), kind=kOutput, calls=%fused_computation.37 | convolution fusion | flops 504299520 | bytes 3342336 | tf_op jit(solution)/shard_map/ji,wjk->wik/dot_general | solution.py:191
  75.7 0.0 collective-permute-done.8
  75.7 3.5 %fusion.50 = bf16[20,128,128]{1,2,0:T(8,128)(2,1)S(1)} fusion(bf16[20,256,256]{2,0,1:T(8,128)(2,1)} %convert_bitcast_fusion, bf16[128,256]{1,0:T(8,128)(2,1)S(1)} %collective-permute-done.8), kind=kOutput, calls=%fused_computation.36 | convolution fusion | flops 504299520 | bytes 3342336 | tf_op jit(solution)/shard_map/ji,wjk->wik/dot_general | solution.py:191
  79.2 0.7 fusion.95.refs_1_
  79.8 0.7 fusion.94.refs_2_
  80.5 0.7 fusion.93.refs_3_
  81.2 1.3 %fusion.92.refs_4_ = f32[128,128]{1,0:T(8,128)} fusion(bf16[20,128,128]{1,2,0:T(8,128)(2,1)S(1)} %fusion.53, bf16[20,128,128]{1,2,0:T(8,128)(2,1)S(1)} %fusion.50, f32[256,256]{1,0:T(8,128)S(1)} %get-tuple-element.8, f32[128,128]{1,0:T(8,128)S(1)} %fusion.93.refs_3_), kind=kOutput, calls=%fused_computation.58 | convolution fusion | flops 168148992 | bytes 1572864 | tf_op jit(solution)/shard_map/wij,wjk->ik/dot_general | solution.py:38
  82.5 1.9 %shard_map.80 = f32[8,128]{1,0:T(8,128)} custom-call(f32[256,256]{1,0:T(8,128)} %copy-done.1, f32[128,128]{1,0:T(8,128)} %slice.29.refs_0_, f32[128,128]{1,0:T(8,128)} %copy-done.2, f32[128,128]{1,0:T(8,128)} %copy-done.3, f32[128,128]{1,0:T(8,128)} %copy-done.4, f32[128,128]{1,0:T(8,128)} %fusion.92.refs_4_), custom_call_target="tpu_custom_call" | custom-call | tf_op jit(solution)/shard_map/pallas_call | solution.py:173
  84.3 1.3 %collective-permute-start.9 = (f32[8,128]{1,0:T(8,128)}, f32[8,128]{1,0:T(8,128)S(1)}, u32[]{:S(2)}, u32[]{:S(2)}) collective-permute-start(f32[8,128]{1,0:T(8,128)} %shard_map.80), channel_id=1, source_target_pairs={{0,1},{1,0},{2,3},{3,2},{4,5},{5,4},{6,7},{7,6},{8,9},{9,8},{10,11... | collective-permute-start | bytes 12296 | tf_op jit(solution)/shard_map/ppermute | solution.py:28
  85.6 2.5 %collective-permute-done.9 = f32[8,128]{1,0:T(8,128)S(1)} collective-permute-done((f32[8,128]{1,0:T(8,128)}, f32[8,128]{1,0:T(8,128)S(1)}, u32[]{:S(2)}, u32[]{:S(2)}) %collective-permute-start.9) | collective-permute-done | bytes 4128 | tf_op jit(solution)/shard_map/ppermute | solution.py:28
  88.2 0.7 add.35
  88.8 0.3 collective-permute-start.10
  89.2 4.8 %collective-permute-done.10 = f32[8,128]{1,0:T(8,128)S(1)} collective-permute-done((f32[8,128]{1,0:T(8,128)S(1)}, f32[8,128]{1,0:T(8,128)S(1)}, u32[]{:S(2)}, u32[]{:S(2)}) %collective-permute-start.10) | collective-permute-done | bytes 4128 | tf_op jit(solution)/shard_map/ppermute | solution.py:28
  94.0 1.0 collective-permute-start.11
  95.0 2.6 %collective-permute-done.11 = f32[8,128]{1,0:T(8,128)S(1)} collective-permute-done((f32[8,128]{1,0:T(8,128)S(1)}, f32[8,128]{1,0:T(8,128)S(1)}, u32[]{:S(2)}, u32[]{:S(2)}) %collective-permute-start.11) | collective-permute-done | bytes 4128 | tf_op jit(solution)/shard_map/ppermute | solution.py:28
  97.6 2.0 %collective-permute-start.12 = (f32[8,128]{1,0:T(8,128)S(1)}, f32[8,128]{1,0:T(8,128)S(1)}, u32[]{:S(2)}, u32[]{:S(2)}) collective-permute-start(f32[8,128]{1,0:T(8,128)S(1)} %add.37), channel_id=1, source_target_pairs={{0,8},{1,9},{2,10},{3,11},{4,12},{5,13},{6,14},{7,15},{8,0},{9,1},... | collective-permute-start | bytes 12296 | tf_op jit(solution)/shard_map/ppermute | solution.py:28
  99.6 2.5 %collective-permute-done.12 = f32[8,128]{1,0:T(8,128)S(1)} collective-permute-done((f32[8,128]{1,0:T(8,128)S(1)}, f32[8,128]{1,0:T(8,128)S(1)}, u32[]{:S(2)}, u32[]{:S(2)}) %collective-permute-start.12) | collective-permute-done | bytes 4128 | tf_op jit(solution)/shard_map/ppermute | solution.py:28
  102.1 5.9 %collective-permute-start.13 = (f32[8,128]{1,0:T(8,128)S(1)}, f32[8,128]{1,0:T(8,128)S(1)}, u32[]{:S(2)}, u32[]{:S(2)}) collective-permute-start(f32[8,128]{1,0:T(8,128)S(1)} %add.38), channel_id=1, source_target_pairs={{0,16},{1,17},{2,18},{3,19},{4,20},{5,21},{6,22},{7,23},{8,24},{9,... | collective-permute-start | bytes 12296 | tf_op jit(solution)/shard_map/ppermute | solution.py:28
  108.0 1.6 %collective-permute-done.13 = f32[8,128]{1,0:T(8,128)S(1)} collective-permute-done((f32[8,128]{1,0:T(8,128)S(1)}, f32[8,128]{1,0:T(8,128)S(1)}, u32[]{:S(2)}, u32[]{:S(2)}) %collective-permute-start.13) | collective-permute-done | bytes 4128 | tf_op jit(solution)/shard_map/ppermute | solution.py:28
  109.6 0.6 add.39.total_ref
  110.2 1.7 %shard_map.81.coef_ref = f32[8,128]{1,0:T(8,128)} custom-call(f32[8,128]{1,0:T(8,128)} %add.39.total_ref), custom_call_target="tpu_custom_call" | custom-call | tf_op jit(solution)/shard_map/pallas_call | solution.py:175
  111.9 1.3 %slice.28 = f32[1,1]{1,0:T(1,128)} slice(f32[8,128]{1,0:T(8,128)} %shard_map.81.coef_ref), slice={[0:1], [4:5]} | slice | bytes 8 | tf_op jit(solution)/shard_map/slice | solution.py:184
  113.1 1.8 %shard_map.82 = f32[256,256]{1,0:T(8,128)} custom-call(f32[8,128]{1,0:T(8,128)} %shard_map.81.coef_ref, f32[256,256]{1,0:T(8,128)} %copy-done.1, f32[128,128]{1,0:T(8,128)} %slice.29.refs_0_, f32[128,128]{1,0:T(8,128)} %copy-done.2, f32[128,128]{1,0:T(8,128)} %copy-done.3, f32[128,128]{1,0:T(8,128)} %copy-done.4), custom_call_target="tpu_custom_call" | custom-call | tf_op jit(solution)/shard_map/pallas_call | solution.py:179
  (19 shorter events, 0.1 us)
Async XLA Ops:
  0.6 59.9 %copy-start = (f32[20,20]{1,0:T(8,128)S(1)}, f32[20,20]{1,0:T(8,128)}, u32[]{:S(2)}) copy-start(f32[20,20]{1,0:T(8,128)} %param.9) | copy-start | bytes 4804
  0.6 59.9 %collective-permute-start.6 = (bf16[20,256,256]{2,1,0:T(8,128)(2,1)}, bf16[20,256,256]{2,1,0:T(8,128)(2,1)S(1)}, u32[]{:S(2)}, u32[]{:S(2)}) collective-permute-start(bf16[20,256,256]{2,1,0:T(8,128)(2,1)} %bitcast.194), channel_id=1, source_target_pairs={{0,224},{32,0},{64,32},{96,64},{128,96},{160,128},{192,160},{224,1... | collective-permute-start | bytes 7864328 | tf_op jit(solution)/shard_map/ppermute | solution.py:18
  2.9 57.7 %collective-permute-start.5 = (bf16[20,256,256]{2,1,0:T(8,128)(2,1)}, bf16[20,256,256]{2,1,0:T(8,128)(2,1)}, u32[]{:S(2)}, u32[]{:S(2)}) collective-permute-start(bf16[20,256,256]{2,1,0:T(8,128)(2,1)} %bitcast.195), channel_id=1, source_target_pairs={{0,32},{32,64},{64,96},{96,128},{128,160},{160,192},{192,224},{224... | collective-permute-start | bytes 7864328 | tf_op jit(solution)/shard_map/ppermute | solution.py:18
  3.5 4.4 %copy-start.8 = (f32[1,1,256,256]{3,2,1,0:T(8,128)S(1)}, f32[1,1,256,256]{3,2,1,0:T(8,128)}, u32[]{:S(2)}) copy-start(f32[1,1,256,256]{3,2,1,0:T(8,128)} %param.6) | copy-start | bytes 786436
  7.9 5.1 %copy-start.5 = (f32[256,256]{1,0:T(8,128)}, f32[256,256]{1,0:T(8,128)S(1)}, u32[]{:S(2)}) copy-start(f32[256,256]{1,0:T(8,128)S(1)} %fusion.67.refs_1_) | copy-start | bytes 786436
  13.0 4.4 %copy-start.6 = (f32[256,256]{1,0:T(8,128)}, f32[256,256]{1,0:T(8,128)S(1)}, u32[]{:S(2)}) copy-start(f32[256,256]{1,0:T(8,128)S(1)} %fusion.73.refs_2_) | copy-start | bytes 786436
  17.4 5.1 %copy-start.7 = (f32[256,256]{1,0:T(8,128)}, f32[256,256]{1,0:T(8,128)S(1)}, u32[]{:S(2)}) copy-start(f32[256,256]{1,0:T(8,128)S(1)} %fusion.79.refs_3_) | copy-start | bytes 786436
  24.9 3.8 %collective-permute-start = (f32[8,128]{1,0:T(8,128)}, f32[8,128]{1,0:T(8,128)S(1)}, u32[]{:S(2)}, u32[]{:S(2)}) collective-permute-start(f32[8,128]{1,0:T(8,128)} %shard_map.77), channel_id=1, source_target_pairs={{0,1},{1,0},{2,3},{3,2},{4,5},{5,4},{6,7},{7,6},{8,9},{9,8},{10,11... | collective-permute-start | bytes 12296 | tf_op jit(solution)/shard_map/ppermute | solution.py:28
  29.4 5.1 %collective-permute-start.1 = (f32[8,128]{1,0:T(8,128)S(1)}, f32[8,128]{1,0:T(8,128)S(1)}, u32[]{:S(2)}, u32[]{:S(2)}) collective-permute-start(f32[8,128]{1,0:T(8,128)S(1)} %add.30), channel_id=1, source_target_pairs={{0,2},{1,3},{2,0},{3,1},{4,6},{5,7},{6,4},{7,5},{8,10},{9,11},{10,... | collective-permute-start | bytes 12296 | tf_op jit(solution)/shard_map/ppermute | solution.py:28
  34.5 3.6 %collective-permute-start.2 = (f32[8,128]{1,0:T(8,128)S(1)}, f32[8,128]{1,0:T(8,128)S(1)}, u32[]{:S(2)}, u32[]{:S(2)}) collective-permute-start(f32[8,128]{1,0:T(8,128)S(1)} %add.31), channel_id=1, source_target_pairs={{0,4},{1,5},{2,6},{3,7},{4,0},{5,1},{6,2},{7,3},{8,12},{9,13},{10,... | collective-permute-start | bytes 12296 | tf_op jit(solution)/shard_map/ppermute | solution.py:28
  38.1 4.9 %collective-permute-start.3 = (f32[8,128]{1,0:T(8,128)S(1)}, f32[8,128]{1,0:T(8,128)S(1)}, u32[]{:S(2)}, u32[]{:S(2)}) collective-permute-start(f32[8,128]{1,0:T(8,128)S(1)} %add.32), channel_id=1, source_target_pairs={{0,8},{1,9},{2,10},{3,11},{4,12},{5,13},{6,14},{7,15},{8,0},{9,1},... | collective-permute-start | bytes 12296 | tf_op jit(solution)/shard_map/ppermute | solution.py:28
  43.0 8.4 %collective-permute-start.4 = (f32[8,128]{1,0:T(8,128)S(1)}, f32[8,128]{1,0:T(8,128)S(1)}, u32[]{:S(2)}, u32[]{:S(2)}) collective-permute-start(f32[8,128]{1,0:T(8,128)S(1)} %add.33), channel_id=1, source_target_pairs={{0,16},{1,17},{2,18},{3,19},{4,20},{5,21},{6,22},{7,23},{8,24},{9,... | collective-permute-start | bytes 12296 | tf_op jit(solution)/shard_map/ppermute | solution.py:28
  56.8 22.3 %copy-start.1 = (f32[256,256]{1,0:T(8,128)}, f32[256,256]{1,0:T(8,128)S(1)}, u32[]{:S(2)}) copy-start(f32[256,256]{1,0:T(8,128)S(1)} %get-tuple-element.7.head_ref) | copy-start | bytes 786436
  57.5 14.7 %collective-permute-start.7 = (bf16[256,128]{1,0:T(8,128)(2,1)S(1)}, bf16[256,128]{1,0:T(8,128)(2,1)S(1)}, u32[]{:S(2)}, u32[]{:S(2)}) collective-permute-start(bf16[256,128]{1,0:T(8,128)(2,1)S(1)} %fusion.113), channel_id=1, source_target_pairs={{0,32},{32,64},{64,96},{96,128},{128,160},{160,192},{192,224},{224... | collective-permute-start | bytes 196616 | tf_op jit(solution)/shard_map/ppermute | solution.py:18
  57.6 18.1 %collective-permute-start.8 = (bf16[128,256]{1,0:T(8,128)(2,1)S(1)}, bf16[128,256]{1,0:T(8,128)(2,1)S(1)}, u32[]{:S(2)}, u32[]{:S(2)}) collective-permute-start(bf16[128,256]{1,0:T(8,128)(2,1)S(1)} %fusion.112), channel_id=1, source_target_pairs={{0,224},{32,0},{64,32},{96,64},{128,96},{160,128},{192,160},{224,1... | collective-permute-start | bytes 196616 | tf_op jit(solution)/shard_map/ppermute | solution.py:18
  79.8 2.7 %copy-start.2 = (f32[128,128]{1,0:T(8,128)}, f32[128,128]{1,0:T(8,128)S(1)}, u32[]{:S(2)}) copy-start(f32[128,128]{1,0:T(8,128)S(1)} %fusion.95.refs_1_) | copy-start | bytes 196612
  80.5 2.0 %copy-start.3 = (f32[128,128]{1,0:T(8,128)}, f32[128,128]{1,0:T(8,128)S(1)}, u32[]{:S(2)}) copy-start(f32[128,128]{1,0:T(8,128)S(1)} %fusion.94.refs_2_) | copy-start | bytes 196612
  81.2 1.3 %copy-start.4 = (f32[128,128]{1,0:T(8,128)}, f32[128,128]{1,0:T(8,128)S(1)}, u32[]{:S(2)}) copy-start(f32[128,128]{1,0:T(8,128)S(1)} %fusion.93.refs_3_) | copy-start | bytes 196612
  84.3 3.8 %collective-permute-start.9 = (f32[8,128]{1,0:T(8,128)}, f32[8,128]{1,0:T(8,128)S(1)}, u32[]{:S(2)}, u32[]{:S(2)}) collective-permute-start(f32[8,128]{1,0:T(8,128)} %shard_map.80), channel_id=1, source_target_pairs={{0,1},{1,0},{2,3},{3,2},{4,5},{5,4},{6,7},{7,6},{8,9},{9,8},{10,11... | collective-permute-start | bytes 12296 | tf_op jit(solution)/shard_map/ppermute | solution.py:28
  88.8 5.1 %collective-permute-start.10 = (f32[8,128]{1,0:T(8,128)S(1)}, f32[8,128]{1,0:T(8,128)S(1)}, u32[]{:S(2)}, u32[]{:S(2)}) collective-permute-start(f32[8,128]{1,0:T(8,128)S(1)} %add.35), channel_id=1, source_target_pairs={{0,2},{1,3},{2,0},{3,1},{4,6},{5,7},{6,4},{7,5},{8,10},{9,11},{10,... | collective-permute-start | bytes 12296 | tf_op jit(solution)/shard_map/ppermute | solution.py:28
  94.0 3.6 %collective-permute-start.11 = (f32[8,128]{1,0:T(8,128)S(1)}, f32[8,128]{1,0:T(8,128)S(1)}, u32[]{:S(2)}, u32[]{:S(2)}) collective-permute-start(f32[8,128]{1,0:T(8,128)S(1)} %add.36), channel_id=1, source_target_pairs={{0,4},{1,5},{2,6},{3,7},{4,0},{5,1},{6,2},{7,3},{8,12},{9,13},{10,... | collective-permute-start | bytes 12296 | tf_op jit(solution)/shard_map/ppermute | solution.py:28
  97.6 4.5 %collective-permute-start.12 = (f32[8,128]{1,0:T(8,128)S(1)}, f32[8,128]{1,0:T(8,128)S(1)}, u32[]{:S(2)}, u32[]{:S(2)}) collective-permute-start(f32[8,128]{1,0:T(8,128)S(1)} %add.37), channel_id=1, source_target_pairs={{0,8},{1,9},{2,10},{3,11},{4,12},{5,13},{6,14},{7,15},{8,0},{9,1},... | collective-permute-start | bytes 12296 | tf_op jit(solution)/shard_map/ppermute | solution.py:28
  102.1 7.5 %collective-permute-start.13 = (f32[8,128]{1,0:T(8,128)S(1)}, f32[8,128]{1,0:T(8,128)S(1)}, u32[]{:S(2)}, u32[]{:S(2)}) collective-permute-start(f32[8,128]{1,0:T(8,128)S(1)} %add.38), channel_id=1, source_target_pairs={{0,16},{1,17},{2,18},{3,19},{4,20},{5,21},{6,22},{7,23},{8,24},{9,... | collective-permute-start | bytes 12296 | tf_op jit(solution)/shard_map/ppermute | solution.py:28

commit v3 on v2

--- a/solution.py
+++ b/solution.py
@@ -18,15 +18,22 @@
     return lax.ppermute(value, axis, pairs)
 
 
-def bond_sum(value):
+def bond_sum(value, hooks=None):
+    hooks = hooks or {}
     count = lax.axis_size("bond")
     if count & (count - 1):
+        for index in sorted(hooks):
+            value = hooks[index](value)
         return lax.psum(value, "bond")
-    step = 1
-    while step < count:
-        pairs = [(source, source ^ step) for source in range(count)]
+    rounds = count.bit_length() - 1
+    for index in range(rounds):
+        if index in hooks:
+            value = hooks[index](value)
+        pairs = [(source, source ^ (1 << index)) for source in range(count)]
         value = value + lax.ppermute(value, "bond", pairs)
-        step *= 2
+    for index in sorted(hooks):
+        if index >= rounds:
+            value = hooks[index](value)
     return value
 
 
@@ -160,7 +167,7 @@
     out_ref[:rows, :cols] = acc
 
 
-def lanczos(start, left, right, mask, scale=None, cut=None):
+def lanczos(start, left, right, mask, scale=None, cut=None, hooks=None):
     head = start * mask
     if cut is None:
         base, live = head, mask
@@ -171,7 +178,7 @@
         krylov.append(apply_ham(krylov[-1], left, right, live))
     tile = jax.ShapeDtypeStruct((8, 128), jnp.float32)
     local = pl.pallas_call(gram_kernel, out_shape=tile)(head, *krylov)
-    total = bond_sum(local)
+    total = bond_sum(local, hooks)
     out = pl.pallas_call(
         ritz_kernel, out_shape=tile, in_specs=[pl.BlockSpec(memory_space=pltpu.SMEM)]
     )(total)
@@ -181,7 +188,7 @@
         out_shape=jax.ShapeDtypeStruct(head.shape, jnp.float32),
         in_specs=[pl.BlockSpec(memory_space=pltpu.SMEM)] + [vec_spec] * (LANCZOS + 1),
     )(out, head, *krylov[:LANCZOS])
-    return (result, krylov[LANCZOS], local, out[0, LANCZOS])
+    return (result, out[0, LANCZOS])
 
 
 def env_update(mixed, left_a):
@@ -205,14 +212,29 @@
     kept = (index < ranks[0, 0]).astype(jnp.float32)
     left_got = shifted(left, "seg", 1)
     right_got = shifted(right, "seg", -1)
-    psi_one, last, local, unused = lanczos(start, left, right, mask)
-    left_got, right_got, last = lax.optimization_barrier((left_got, right_got, last))
-    left_mix = jnp.einsum(
-        "wu,uij->wij", mpo_mix, left_got.astype(jnp.float32), precision=lax.Precision.HIGHEST
-    ).astype(jnp.bfloat16)
-    right_mix = jnp.einsum(
-        "wu,uij->wij", mpo_mix, right_got.astype(jnp.float32), precision=lax.Precision.HIGHEST
-    ).astype(jnp.bfloat16)
+
+    def mixed(env):
+        return jnp.einsum(
+            "wu,uij->wij", mpo_mix, env.astype(jnp.float32), precision=lax.Precision.HIGHEST
+        ).astype(jnp.bfloat16)
+
+    held = {}
+
+    def take_envs(value):
+        value, held["left"], held["right"] = lax.optimization_barrier((value, left_got, right_got))
+        return value
+
+    def mix_left(value):
+        value, held["left"] = lax.optimization_barrier((value, mixed(held["left"])))
+        return value
+
+    def mix_right(value):
+        value, held["right"] = lax.optimization_barrier((value, mixed(held["right"])))
+        return value
+
+    hooks = {1: take_envs, 3: mix_left, 4: mix_right}
+    psi_one, unused = lanczos(start, left, right, mask, hooks=hooks)
+    left_mix, right_mix = held["left"], held["right"]
     scaled = psi_one * math.sqrt(blocks * width)
     cut = width // 2
     left_a = (scaled[:, :cut] * kept[None, :cut]).astype(jnp.bfloat16)
@@ -221,7 +243,7 @@
     right_a_got = shifted(right_a, "seg", -1)
     left_in = env_update(left_mix, left_a_got)
     right_in = env_update(right_mix, right_a_got.T)
-    ground, last, local, energy = lanczos(
+    ground, energy = lanczos(
         psi_one, left_in, right_in, mask, math.sqrt(blocks * width * width), cut
     )
     return (ground[None, None], jnp.reshape(energy, (1,)))

time: 115 us -> 113 us (0.983)
  starting transfers between devices: 29.5 us -> 22.7 us
  matrix products: 39.9 us -> 41.8 us
  waiting for transfers between devices: 25.4 us -> 27 us
    ppermute x10, starting transfers between devices: 24.3 us -> 19.3 us  [bond_sum(): value = value + lax.ppermute(value, 'bond', pairs)]
    dot_general x8, matrix products: 21.4 us -> 23.7 us  [apply_ham(): jnp.einsum('wij,wjk->ik', left, inner, preferred_element_type=jnp.float32)]
    ppermute x4, starting transfers between devices: 5.18 us -> 3.48 us  [shifted(): return lax.ppermute(value, axis, pairs)]
  transfers between devices with their start and end apart: 14 -> 14, of which waited for: 10 -> 9; matrix products, arithmetic and copies ran while one was open for 32% -> 35% of each run, Pallas kernels for 5% -> 2%
where the time goes in v3:
time: 113 us
  matrix products  41.8 us (37%)
  waiting for transfers between devices  27 us (24%)
  starting transfers between devices  22.7 us (20%)
  Pallas kernels  11.4 us (10%)
  other arithmetic  5.46 us (5%)
  between operations  2.15 us (2%)
  local copies, waits for them, and re-layouts  1.92 us (2%)
    ppermute x10, waiting for transfers between devices, bond_sum(): value = value + lax.ppermute(value, 'bond', pairs)  26.3 us
    dot_general x8, matrix products, apply_ham(): jnp.einsum('wij,wjk->ik', left, inner, preferred_element_type=jnp.float32)  23.7 us
    ppermute x10, starting transfers between devices, bond_sum(): value = value + lax.ppermute(value, 'bond', pairs)  19.3 us
    dot_general x2, matrix products, mixed(): jnp.einsum('wu,uij->wij', mpo_mix, env.astype(jnp.float32), precision=lax...  11.6 us
    dot_general x2, matrix products, env_update(): jnp.einsum('ji,wjk->wik', left_a, half_left, preferred_element_type=jnp.f...  6.49 us
    pallas_call x2, Pallas kernels, lanczos(): local = pl.pallas_call(gram_kernel, out_shape=tile)(head, *krylov)  4.26 us
    pallas_call x2, Pallas kernels, lanczos(): pl.pallas_call(functools.partial(combine_kernel, scale=scale), out_shape=...  3.83 us
    ppermute x4, starting transfers between devices, shifted(): return lax.ppermute(value, axis, pairs)  3.48 us
  transfers between devices with their start and end apart: 14, of which 9 were waited for; matrix products, arithmetic and copies ran while one was open for 35% of the time, Pallas kernels for 2%

profile of v3, /device:TPU:16, one launch (start us, length us, event | category | flops | bytes accessed | tf_op | source)
XLA Modules:
  0.0 112.5 jit_solution(8298676348208861364)
XLA Ops:
  0.6 0.0 copy-start
  0.6 0.0 collective-permute-start.1
  0.7 2.9 %collective-permute-start.2 = (bf16[20,256,256]{2,1,0:T(8,128)(2,1)}, bf16[20,256,256]{2,1,0:T(8,128)(2,1)S(1)}, u32[]{:S(2)}, u32[]{:S(2)}) collective-permute-start(bf16[20,256,256]{2,1,0:T(8,128)(2,1)} %bitcast.195), channel_id=1, source_target_pairs={{0,224},{32,0},{64,32},{96,64},{128,96},{160,128},{192,160},{224,1... | collective-permute-start | bytes 7864328 | tf_op jit(solution)/shard_map/ppermute | solution.py:18
  4.3 1.8 %multiply_multiply_fusion.4.head_ref.refs_0_ = f32[256,256]{1,0:T(8,128)} fusion(f32[1,1,256,256]{3,2,1,0:T(8,128)} %param.6, f32[256]{0:T(256)S(1)} %compare_convert_fusion), kind=kLoop, calls=%fused_computation.66 | loop fusion | flops 131072 | bytes 525312 | tf_op jit(solution)/shard_map/mul | solution.py:171
  6.0 5.1 %fusion.67.refs_1_ = f32[256,256]{1,0:T(8,128)S(1)} fusion(f32[1,1,256,256]{3,2,1,0:T(8,128)} %param.6, f32[256]{0:T(256)S(1)} %compare_convert_fusion, bf16[1,1,20,256,256]{4,3,2,1,0:T(8,128)(2,1)} %param.7, bf16[1,1,20,256,256]{4,3,2,1,0:T(8,128)(2,1)} %param.8), kind=kOutput, calls=%fused_computation.47 | convolution fusion | flops 1343881216 | bytes 5768192 | tf_op jit(solution)/shard_map/wij,wjk->ik/dot_general | solution.py:45
  11.1 0.0 copy-start.5
  11.1 5.1 %fusion.73.refs_2_ = f32[256,256]{1,0:T(8,128)S(1)} fusion(f32[256,256]{1,0:T(8,128)S(1)} %fusion.67.refs_1_, f32[256]{0:T(256)S(1)} %compare_convert_fusion, bf16[1,1,20,256,256]{4,3,2,1,0:T(8,128)(2,1)} %param.7, bf16[1,1,20,256,256]{4,3,2,1,0:T(8,128)(2,1)} %param.8), kind=kOutput, calls=%fused_computation.49 | convolution fusion | flops 1343815680 | bytes 5768192 | tf_op jit(solution)/shard_map/wij,wjk->ik/dot_general | solution.py:45
  16.2 0.0 copy-done.5
  16.2 0.0 copy-start.6
  16.2 5.1 %fusion.79.refs_3_ = f32[256,256]{1,0:T(8,128)S(1)} fusion(f32[256,256]{1,0:T(8,128)S(1)} %fusion.73.refs_2_, f32[256]{0:T(256)S(1)} %compare_convert_fusion, bf16[1,1,20,256,256]{4,3,2,1,0:T(8,128)(2,1)} %param.7, bf16[1,1,20,256,256]{4,3,2,1,0:T(8,128)(2,1)} %param.8), kind=kOutput, calls=%fused_computation.51 | convolution fusion | flops 1343815680 | bytes 5768192 | tf_op jit(solution)/shard_map/wij,wjk->ik/dot_general | solution.py:45
  21.3 0.0 copy-done.6
  21.3 5.8 %fusion.85.refs_4_ = f32[256,256]{1,0:T(8,128)} fusion(f32[256,256]{1,0:T(8,128)S(1)} %fusion.79.refs_3_, f32[256]{0:T(256)S(1)} %compare_convert_fusion, bf16[1,1,20,256,256]{4,3,2,1,0:T(8,128)(2,1)} %param.7, bf16[1,1,20,256,256]{4,3,2,1,0:T(8,128)(2,1)} %param.8), kind=kOutput, calls=%fused_computation.53 | convolution fusion | flops 1343815680 | bytes 5768192 | tf_op jit(solution)/shard_map/wij,wjk->ik/dot_general | solution.py:45
  27.1 0.0 copy-done.7
  27.1 2.4 %shard_map.77 = f32[8,128]{1,0:T(8,128)} custom-call(f32[256,256]{1,0:T(8,128)} %multiply_multiply_fusion.4.head_ref.refs_0_, f32[256,256]{1,0:T(8,128)} %multiply_multiply_fusion.4.head_ref.refs_0_, f32[256,256]{1,0:T(8,128)} %copy-done.5, f32[256,256]{1,0:T(8,128)} %copy-done.6, f32[256,256]{1,0:T(8,128)} %copy-done.7, f32[256,256]{1,0:T(8,128)} %fusion.85.refs_4_), custom_call_target="tpu_custom_call" | custom-call | tf_op jit(solution)/shard_map/pallas_call | solution.py:180
  29.5 1.3 %collective-permute-start = (f32[8,128]{1,0:T(8,128)}, f32[8,128]{1,0:T(8,128)S(1)}, u32[]{:S(2)}, u32[]{:S(2)}) collective-permute-start(f32[8,128]{1,0:T(8,128)} %shard_map.77), channel_id=1, source_target_pairs={{0,1},{1,0},{2,3},{3,2},{4,5},{5,4},{6,7},{7,6},{8,9},{9,8},{10,11... | collective-permute-start | bytes 12296 | tf_op jit(solution)/shard_map/ppermute | solution.py:33
  31.5 1.9 %collective-permute-done = f32[8,128]{1,0:T(8,128)S(1)} collective-permute-done((f32[8,128]{1,0:T(8,128)}, f32[8,128]{1,0:T(8,128)S(1)}, u32[]{:S(2)}, u32[]{:S(2)}) %collective-permute-start) | collective-permute-done | bytes 4128 | tf_op jit(solution)/shard_map/ppermute | solution.py:33
  33.3 0.7 add.30
  34.0 0.0 collective-permute-done.1
  34.0 0.0 collective-permute-done.2
  34.0 2.1 %collective-permute-start.3 = (f32[8,128]{1,0:T(8,128)S(1)}, f32[8,128]{1,0:T(8,128)S(1)}, u32[]{:S(2)}, u32[]{:S(2)}) collective-permute-start(f32[8,128]{1,0:T(8,128)S(1)} %add.30), channel_id=1, source_target_pairs={{0,2},{1,3},{2,0},{3,1},{4,6},{5,7},{6,4},{7,5},{8,10},{9,11},{10,... | collective-permute-start | bytes 12296 | tf_op jit(solution)/shard_map/ppermute | solution.py:33
  36.1 3.0 %collective-permute-done.3 = f32[8,128]{1,0:T(8,128)S(1)} collective-permute-done((f32[8,128]{1,0:T(8,128)S(1)}, f32[8,128]{1,0:T(8,128)S(1)}, u32[]{:S(2)}, u32[]{:S(2)}) %collective-permute-start.3) | collective-permute-done | bytes 4128 | tf_op jit(solution)/shard_map/ppermute | solution.py:33
  39.1 1.9 %collective-permute-start.4 = (f32[8,128]{1,0:T(8,128)S(1)}, f32[8,128]{1,0:T(8,128)S(1)}, u32[]{:S(2)}, u32[]{:S(2)}) collective-permute-start(f32[8,128]{1,0:T(8,128)S(1)} %add.31), channel_id=1, source_target_pairs={{0,4},{1,5},{2,6},{3,7},{4,0},{5,1},{6,2},{7,3},{8,12},{9,13},{10,... | collective-permute-start | bytes 12296 | tf_op jit(solution)/shard_map/ppermute | solution.py:33
  41.0 6.8 %convert_bitcast_fusion.1 = bf16[20,256,256]{2,0,1:T(8,128)(2,1)} fusion(bf16[20,256,256]{2,1,0:T(8,128)(2,1)} %collective-permute-done.1, f32[20,20]{1,0:T(8,128)S(1)} %copy-done), kind=kOutput, calls=%fused_computation.5 | convolution fusion | flops 315883520 | bytes 5244480 | tf_op jit(solution)/shard_map/wu,uij->wij/dot_general | solution.py:217
  47.9 0.0 collective-permute-done.4
  47.9 3.3 %collective-permute-start.5 = (f32[8,128]{1,0:T(8,128)S(1)}, f32[8,128]{1,0:T(8,128)S(1)}, u32[]{:S(2)}, u32[]{:S(2)}) collective-permute-start(f32[8,128]{1,0:T(8,128)S(1)} %add.32), channel_id=1, source_target_pairs={{0,8},{1,9},{2,10},{3,11},{4,12},{5,13},{6,14},{7,15},{8,0},{9,1},... | collective-permute-start | bytes 12296 | tf_op jit(solution)/shard_map/ppermute | solution.py:33
  51.2 4.8 %convert_bitcast_fusion = bf16[20,256,256]{2,0,1:T(8,128)(2,1)} fusion(bf16[20,256,256]{2,1,0:T(8,128)(2,1)S(1)} %collective-permute-done.2, f32[20,20]{1,0:T(8,128)S(1)} %copy-done), kind=kOutput, calls=%fused_computation.4 | convolution fusion | flops 315883520 | bytes 5244480 | tf_op jit(solution)/shard_map/wu,uij->wij/dot_general | solution.py:217
  55.9 0.0 collective-permute-done.5
  56.0 4.5 %collective-permute-start.6 = (f32[8,128]{1,0:T(8,128)S(1)}, f32[8,128]{1,0:T(8,128)S(1)}, u32[]{:S(2)}, u32[]{:S(2)}) collective-permute-start(f32[8,128]{1,0:T(8,128)S(1)} %add.33), channel_id=1, source_target_pairs={{0,16},{1,17},{2,18},{3,19},{4,20},{5,21},{6,22},{7,23},{8,24},{9,... | collective-permute-start | bytes 12296 | tf_op jit(solution)/shard_map/ppermute | solution.py:33
  60.4 3.0 %collective-permute-done.6 = f32[8,128]{1,0:T(8,128)S(1)} collective-permute-done((f32[8,128]{1,0:T(8,128)S(1)}, f32[8,128]{1,0:T(8,128)S(1)}, u32[]{:S(2)}, u32[]{:S(2)}) %collective-permute-start.6) | collective-permute-done | bytes 4128 | tf_op jit(solution)/shard_map/ppermute | solution.py:33
  63.5 0.6 add.34.total_ref
  64.1 1.7 %shard_map.78.coef_ref = f32[8,128]{1,0:T(8,128)} custom-call(f32[8,128]{1,0:T(8,128)} %add.34.total_ref), custom_call_target="tpu_custom_call" | custom-call | tf_op jit(solution)/shard_map/pallas_call | solution.py:182
  65.7 2.0 %shard_map.79 = f32[256,256]{1,0:T(8,128)} custom-call(f32[8,128]{1,0:T(8,128)} %shard_map.78.coef_ref, f32[256,256]{1,0:T(8,128)} %multiply_multiply_fusion.4.head_ref.refs_0_, f32[256,256]{1,0:T(8,128)} %multiply_multiply_fusion.4.head_ref.refs_0_, f32[256,256]{1,0:T(8,128)} %copy-done.5, f32[256,256]{1,0:T(8,128)} %copy-done.6, f32[256,256]{1,0:T(8,128)} %copy-done.7), custom_call_target="tpu_custom_call" | custom-call | tf_op jit(solution)/shard_map/pallas_call | solution.py:186
  67.8 1.0 broadcast_multiply_fusion
  68.8 0.0 copy-start.1
  68.9 0.1 fusion.112
  68.9 0.0 collective-permute-start.8
  69.0 0.5 collective-permute-start.7
  69.5 0.6 slice.29.refs_0_
  70.1 0.7 collective-permute-done.8
  70.9 3.2 %fusion.50 = bf16[20,128,128]{1,2,0:T(8,128)(2,1)S(1)} fusion(bf16[20,256,256]{2,0,1:T(8,128)(2,1)} %convert_bitcast_fusion, bf16[128,256]{1,0:T(8,128)(2,1)S(1)} %collective-permute-done.8), kind=kOutput, calls=%fused_computation.36 | convolution fusion | flops 504299520 | bytes 3342336 | tf_op jit(solution)/shard_map/ji,wjk->wik/dot_general | solution.py:198
  74.1 0.0 collective-permute-done.7
  74.1 3.2 %fusion.53 = bf16[20,128,128]{1,2,0:T(8,128)(2,1)S(1)} fusion(bf16[20,256,256]{2,0,1:T(8,128)(2,1)} %convert_bitcast_fusion.1, bf16[256,128]{1,0:T(8,128)(2,1)S(1)} %collective-permute-done.7), kind=kOutput, calls=%fused_computation.37 | convolution fusion | flops 504299520 | bytes 3342336 | tf_op jit(solution)/shard_map/ji,wjk->wik/dot_general | solution.py:198
  77.4 0.5 fusion.95.refs_1_
  77.9 0.0 copy-start.2
  77.9 0.5 fusion.94.refs_2_
  78.4 0.5 fusion.93.refs_3_
  79.0 1.1 %fusion.92.refs_4_ = f32[128,128]{1,0:T(8,128)} fusion(bf16[20,128,128]{1,2,0:T(8,128)(2,1)S(1)} %fusion.53, bf16[20,128,128]{1,2,0:T(8,128)(2,1)S(1)} %fusion.50, f32[256,256]{1,0:T(8,128)S(1)} %get-tuple-element.18, f32[128,128]{1,0:T(8,128)S(1)} %fusion.93.refs_3_), kind=kOutput, calls=%fused_computation.58 | convolution fusion | flops 168148992 | bytes 1572864 | tf_op jit(solution)/shard_map/wij,wjk->ik/dot_general | solution.py:45
  80.1 0.0 copy-done.3
  80.1 1.8 %shard_map.80 = f32[8,128]{1,0:T(8,128)} custom-call(f32[256,256]{1,0:T(8,128)} %copy-done.1, f32[128,128]{1,0:T(8,128)} %slice.29.refs_0_, f32[128,128]{1,0:T(8,128)} %copy-done.2, f32[128,128]{1,0:T(8,128)} %copy-done.3, f32[128,128]{1,0:T(8,128)} %copy-done.4, f32[128,128]{1,0:T(8,128)} %fusion.92.refs_4_), custom_call_target="tpu_custom_call" | custom-call | tf_op jit(solution)/shard_map/pallas_call | solution.py:180
  82.0 1.3 %collective-permute-start.9 = (f32[8,128]{1,0:T(8,128)}, f32[8,128]{1,0:T(8,128)S(1)}, u32[]{:S(2)}, u32[]{:S(2)}) collective-permute-start(f32[8,128]{1,0:T(8,128)} %shard_map.80), channel_id=1, source_target_pairs={{0,1},{1,0},{2,3},{3,2},{4,5},{5,4},{6,7},{7,6},{8,9},{9,8},{10,11... | collective-permute-start | bytes 12296 | tf_op jit(solution)/shard_map/ppermute | solution.py:33
  83.2 2.5 %collective-permute-done.9 = f32[8,128]{1,0:T(8,128)S(1)} collective-permute-done((f32[8,128]{1,0:T(8,128)}, f32[8,128]{1,0:T(8,128)S(1)}, u32[]{:S(2)}, u32[]{:S(2)}) %collective-permute-start.9) | collective-permute-done | bytes 4128 | tf_op jit(solution)/shard_map/ppermute | solution.py:33
  85.8 0.7 add.35
  86.5 0.3 collective-permute-start.10
  86.8 4.8 %collective-permute-done.10 = f32[8,128]{1,0:T(8,128)S(1)} collective-permute-done((f32[8,128]{1,0:T(8,128)S(1)}, f32[8,128]{1,0:T(8,128)S(1)}, u32[]{:S(2)}, u32[]{:S(2)}) %collective-permute-start.10) | collective-permute-done | bytes 4128 | tf_op jit(solution)/shard_map/ppermute | solution.py:33
  91.6 0.1 collective-permute-start.11
  91.7 3.5 %collective-permute-done.11 = f32[8,128]{1,0:T(8,128)S(1)} collective-permute-done((f32[8,128]{1,0:T(8,128)S(1)}, f32[8,128]{1,0:T(8,128)S(1)}, u32[]{:S(2)}, u32[]{:S(2)}) %collective-permute-start.11) | collective-permute-done | bytes 4128 | tf_op jit(solution)/shard_map/ppermute | solution.py:33
  95.2 0.0 collective-permute-start.12
  95.2 4.5 %collective-permute-done.12 = f32[8,128]{1,0:T(8,128)S(1)} collective-permute-done((f32[8,128]{1,0:T(8,128)S(1)}, f32[8,128]{1,0:T(8,128)S(1)}, u32[]{:S(2)}, u32[]{:S(2)}) %collective-permute-start.12) | collective-permute-done | bytes 4128 | tf_op jit(solution)/shard_map/ppermute | solution.py:33
  99.7 4.5 %collective-permute-start.13 = (f32[8,128]{1,0:T(8,128)S(1)}, f32[8,128]{1,0:T(8,128)S(1)}, u32[]{:S(2)}, u32[]{:S(2)}) collective-permute-start(f32[8,128]{1,0:T(8,128)S(1)} %add.38), channel_id=1, source_target_pairs={{0,16},{1,17},{2,18},{3,19},{4,20},{5,21},{6,22},{7,23},{8,24},{9,... | collective-permute-start | bytes 12296 | tf_op jit(solution)/shard_map/ppermute | solution.py:33
  104.2 3.0 %collective-permute-done.13 = f32[8,128]{1,0:T(8,128)S(1)} collective-permute-done((f32[8,128]{1,0:T(8,128)S(1)}, f32[8,128]{1,0:T(8,128)S(1)}, u32[]{:S(2)}, u32[]{:S(2)}) %collective-permute-start.13) | collective-permute-done | bytes 4128 | tf_op jit(solution)/shard_map/ppermute | solution.py:33
  107.2 0.6 add.39.total_ref
  107.8 1.7 %shard_map.81.coef_ref = f32[8,128]{1,0:T(8,128)} custom-call(f32[8,128]{1,0:T(8,128)} %add.39.total_ref), custom_call_target="tpu_custom_call" | custom-call | tf_op jit(solution)/shard_map/pallas_call | solution.py:182
  109.5 1.8 %shard_map.82 = f32[256,256]{1,0:T(8,128)} custom-call(f32[8,128]{1,0:T(8,128)} %shard_map.81.coef_ref, f32[256,256]{1,0:T(8,128)} %copy-done.1, f32[128,128]{1,0:T(8,128)} %slice.29.refs_0_, f32[128,128]{1,0:T(8,128)} %copy-done.2, f32[128,128]{1,0:T(8,128)} %copy-done.3, f32[128,128]{1,0:T(8,128)} %copy-done.4), custom_call_target="tpu_custom_call" | custom-call | tf_op jit(solution)/shard_map/pallas_call | solution.py:186
  111.3 1.3 %slice.28 = f32[1,1]{1,0:T(1,128)} slice(f32[8,128]{1,0:T(8,128)} %shard_map.81.coef_ref), slice={[0:1], [4:5]} | slice | bytes 8 | tf_op jit(solution)/shard_map/slice | solution.py:191
  (17 shorter events, 0.1 us)
Async XLA Ops:
  0.6 40.4 %copy-start = (f32[20,20]{1,0:T(8,128)S(1)}, f32[20,20]{1,0:T(8,128)}, u32[]{:S(2)}) copy-start(f32[20,20]{1,0:T(8,128)} %param.9) | copy-start | bytes 4804
  0.6 33.4 %collective-permute-start.1 = (bf16[20,256,256]{2,1,0:T(8,128)(2,1)}, bf16[20,256,256]{2,1,0:T(8,128)(2,1)}, u32[]{:S(2)}, u32[]{:S(2)}) collective-permute-start(bf16[20,256,256]{2,1,0:T(8,128)(2,1)} %bitcast.194), channel_id=1, source_target_pairs={{0,32},{32,64},{64,96},{96,128},{128,160},{160,192},{192,224},{224... | collective-permute-start | bytes 7864328 | tf_op jit(solution)/shard_map/ppermute | solution.py:18
  0.7 33.3 %collective-permute-start.2 = (bf16[20,256,256]{2,1,0:T(8,128)(2,1)}, bf16[20,256,256]{2,1,0:T(8,128)(2,1)S(1)}, u32[]{:S(2)}, u32[]{:S(2)}) collective-permute-start(bf16[20,256,256]{2,1,0:T(8,128)(2,1)} %bitcast.195), channel_id=1, source_target_pairs={{0,224},{32,0},{64,32},{96,64},{128,96},{160,128},{192,160},{224,1... | collective-permute-start | bytes 7864328 | tf_op jit(solution)/shard_map/ppermute | solution.py:18
  11.1 5.1 %copy-start.5 = (f32[256,256]{1,0:T(8,128)}, f32[256,256]{1,0:T(8,128)S(1)}, u32[]{:S(2)}) copy-start(f32[256,256]{1,0:T(8,128)S(1)} %fusion.67.refs_1_) | copy-start | bytes 786436
  16.2 5.1 %copy-start.6 = (f32[256,256]{1,0:T(8,128)}, f32[256,256]{1,0:T(8,128)S(1)}, u32[]{:S(2)}) copy-start(f32[256,256]{1,0:T(8,128)S(1)} %fusion.73.refs_2_) | copy-start | bytes 786436
  21.3 5.8 %copy-start.7 = (f32[256,256]{1,0:T(8,128)}, f32[256,256]{1,0:T(8,128)S(1)}, u32[]{:S(2)}) copy-start(f32[256,256]{1,0:T(8,128)S(1)} %fusion.79.refs_3_) | copy-start | bytes 786436
  29.5 3.8 %collective-permute-start = (f32[8,128]{1,0:T(8,128)}, f32[8,128]{1,0:T(8,128)S(1)}, u32[]{:S(2)}, u32[]{:S(2)}) collective-permute-start(f32[8,128]{1,0:T(8,128)} %shard_map.77), channel_id=1, source_target_pairs={{0,1},{1,0},{2,3},{3,2},{4,5},{5,4},{6,7},{7,6},{8,9},{9,8},{10,11... | collective-permute-start | bytes 12296 | tf_op jit(solution)/shard_map/ppermute | solution.py:33
  34.0 5.1 %collective-permute-start.3 = (f32[8,128]{1,0:T(8,128)S(1)}, f32[8,128]{1,0:T(8,128)S(1)}, u32[]{:S(2)}, u32[]{:S(2)}) collective-permute-start(f32[8,128]{1,0:T(8,128)S(1)} %add.30), channel_id=1, source_target_pairs={{0,2},{1,3},{2,0},{3,1},{4,6},{5,7},{6,4},{7,5},{8,10},{9,11},{10,... | collective-permute-start | bytes 12296 | tf_op jit(solution)/shard_map/ppermute | solution.py:33
  39.1 8.8 %collective-permute-start.4 = (f32[8,128]{1,0:T(8,128)S(1)}, f32[8,128]{1,0:T(8,128)S(1)}, u32[]{:S(2)}, u32[]{:S(2)}) collective-permute-start(f32[8,128]{1,0:T(8,128)S(1)} %add.31), channel_id=1, source_target_pairs={{0,4},{1,5},{2,6},{3,7},{4,0},{5,1},{6,2},{7,3},{8,12},{9,13},{10,... | collective-permute-start | bytes 12296 | tf_op jit(solution)/shard_map/ppermute | solution.py:33
  47.9 8.0 %collective-permute-start.5 = (f32[8,128]{1,0:T(8,128)S(1)}, f32[8,128]{1,0:T(8,128)S(1)}, u32[]{:S(2)}, u32[]{:S(2)}) collective-permute-start(f32[8,128]{1,0:T(8,128)S(1)} %add.32), channel_id=1, source_target_pairs={{0,8},{1,9},{2,10},{3,11},{4,12},{5,13},{6,14},{7,15},{8,0},{9,1},... | collective-permute-start | bytes 12296 | tf_op jit(solution)/shard_map/ppermute | solution.py:33
  56.0 7.5 %collective-permute-start.6 = (f32[8,128]{1,0:T(8,128)S(1)}, f32[8,128]{1,0:T(8,128)S(1)}, u32[]{:S(2)}, u32[]{:S(2)}) collective-permute-start(f32[8,128]{1,0:T(8,128)S(1)} %add.33), channel_id=1, source_target_pairs={{0,16},{1,17},{2,18},{3,19},{4,20},{5,21},{6,22},{7,23},{8,24},{9,... | collective-permute-start | bytes 12296 | tf_op jit(solution)/shard_map/ppermute | solution.py:33
  68.8 8.5 %copy-start.1 = (f32[256,256]{1,0:T(8,128)}, f32[256,256]{1,0:T(8,128)S(1)}, u32[]{:S(2)}) copy-start(f32[256,256]{1,0:T(8,128)S(1)} %get-tuple-element.17.head_ref) | copy-start | bytes 786436
  68.9 1.9 %collective-permute-start.8 = (bf16[128,256]{1,0:T(8,128)(2,1)S(1)}, bf16[128,256]{1,0:T(8,128)(2,1)S(1)}, u32[]{:S(2)}, u32[]{:S(2)}) collective-permute-start(bf16[128,256]{1,0:T(8,128)(2,1)S(1)} %fusion.112), channel_id=1, source_target_pairs={{0,224},{32,0},{64,32},{96,64},{128,96},{160,128},{192,160},{224,1... | collective-permute-start | bytes 196616 | tf_op jit(solution)/shard_map/ppermute | solution.py:18
  69.0 5.1 %collective-permute-start.7 = (bf16[256,128]{1,0:T(8,128)(2,1)S(1)}, bf16[256,128]{1,0:T(8,128)(2,1)S(1)}, u32[]{:S(2)}, u32[]{:S(2)}) collective-permute-start(bf16[256,128]{1,0:T(8,128)(2,1)S(1)} %fusion.113), channel_id=1, source_target_pairs={{0,32},{32,64},{64,96},{96,128},{128,160},{160,192},{192,224},{224... | collective-permute-start | bytes 196616 | tf_op jit(solution)/shard_map/ppermute | solution.py:18
  77.9 2.2 %copy-start.2 = (f32[128,128]{1,0:T(8,128)}, f32[128,128]{1,0:T(8,128)S(1)}, u32[]{:S(2)}) copy-start(f32[128,128]{1,0:T(8,128)S(1)} %fusion.95.refs_1_) | copy-start | bytes 196612
  78.4 1.7 %copy-start.3 = (f32[128,128]{1,0:T(8,128)}, f32[128,128]{1,0:T(8,128)S(1)}, u32[]{:S(2)}) copy-start(f32[128,128]{1,0:T(8,128)S(1)} %fusion.94.refs_2_) | copy-start | bytes 196612
  79.0 1.2 %copy-start.4 = (f32[128,128]{1,0:T(8,128)}, f32[128,128]{1,0:T(8,128)S(1)}, u32[]{:S(2)}) copy-start(f32[128,128]{1,0:T(8,128)S(1)} %fusion.93.refs_3_) | copy-start | bytes 196612
  82.0 3.8 %collective-permute-start.9 = (f32[8,128]{1,0:T(8,128)}, f32[8,128]{1,0:T(8,128)S(1)}, u32[]{:S(2)}, u32[]{:S(2)}) collective-permute-start(f32[8,128]{1,0:T(8,128)} %shard_map.80), channel_id=1, source_target_pairs={{0,1},{1,0},{2,3},{3,2},{4,5},{5,4},{6,7},{7,6},{8,9},{9,8},{10,11... | collective-permute-start | bytes 12296 | tf_op jit(solution)/shard_map/ppermute | solution.py:33
  86.5 5.1 %collective-permute-start.10 = (f32[8,128]{1,0:T(8,128)S(1)}, f32[8,128]{1,0:T(8,128)S(1)}, u32[]{:S(2)}, u32[]{:S(2)}) collective-permute-start(f32[8,128]{1,0:T(8,128)S(1)} %add.35), channel_id=1, source_target_pairs={{0,2},{1,3},{2,0},{3,1},{4,6},{5,7},{6,4},{7,5},{8,10},{9,11},{10,... | collective-permute-start | bytes 12296 | tf_op jit(solution)/shard_map/ppermute | solution.py:33
  91.6 3.6 %collective-permute-start.11 = (f32[8,128]{1,0:T(8,128)S(1)}, f32[8,128]{1,0:T(8,128)S(1)}, u32[]{:S(2)}, u32[]{:S(2)}) collective-permute-start(f32[8,128]{1,0:T(8,128)S(1)} %add.36), channel_id=1, source_target_pairs={{0,4},{1,5},{2,6},{3,7},{4,0},{5,1},{6,2},{7,3},{8,12},{9,13},{10,... | collective-permute-start | bytes 12296 | tf_op jit(solution)/shard_map/ppermute | solution.py:33
  95.2 4.5 %collective-permute-start.12 = (f32[8,128]{1,0:T(8,128)S(1)}, f32[8,128]{1,0:T(8,128)S(1)}, u32[]{:S(2)}, u32[]{:S(2)}) collective-permute-start(f32[8,128]{1,0:T(8,128)S(1)} %add.37), channel_id=1, source_target_pairs={{0,8},{1,9},{2,10},{3,11},{4,12},{5,13},{6,14},{7,15},{8,0},{9,1},... | collective-permute-start | bytes 12296 | tf_op jit(solution)/shard_map/ppermute | solution.py:33
  99.7 7.5 %collective-permute-start.13 = (f32[8,128]{1,0:T(8,128)S(1)}, f32[8,128]{1,0:T(8,128)S(1)}, u32[]{:S(2)}, u32[]{:S(2)}) collective-permute-start(f32[8,128]{1,0:T(8,128)S(1)} %add.38), channel_id=1, source_target_pairs={{0,16},{1,17},{2,18},{3,19},{4,20},{5,21},{6,22},{7,23},{8,24},{9,... | collective-permute-start | bytes 12296 | tf_op jit(solution)/shard_map/ppermute | solution.py:33

commit v4 on v3

--- a/solution.py
+++ b/solution.py
@@ -37,32 +37,37 @@
     return value
 
 
-def apply_ham(vector, left, right, mask):
-    rounded = (vector * mask).astype(jnp.bfloat16)
-    inner = jnp.einsum("ij,wjk->wik", rounded, right, preferred_element_type=jnp.float32).astype(
-        jnp.bfloat16
-    )
-    outer = jnp.einsum("wij,wjk->ik", left, inner, preferred_element_type=jnp.float32)
-    return outer * mask
-
-
-def gram_kernel(head_ref, *refs):
-    *vec_refs, out_ref = refs
-    size = len(vec_refs)
-    row = lax.broadcasted_iota(jnp.int32, out_ref.shape, 0)
-    lane = lax.broadcasted_iota(jnp.int32, out_ref.shape, 1)
-    out = jnp.zeros(out_ref.shape, jnp.float32)
+def krylov_kernel(start_ref, mask_ref, left_ref, right_ref, krylov_ref, gram_ref):
+    channels, n = left_ref.shape[0], left_ref.shape[-1]
+    head = start_ref[...] * mask_ref[...]
+    live = mask_ref[:n, :n]
+    krylov_ref[0] = head[:n, :n]
+    for step in range(LANCZOS):
+        rounded = (krylov_ref[step] * live).astype(jnp.bfloat16)
+        krylov_ref[step + 1] = jnp.zeros((n, n), jnp.float32)
+
+        def channel(w, carry, rounded=rounded, step=step):
+            inner = jnp.dot(rounded, right_ref[w], preferred_element_type=jnp.float32)
+            krylov_ref[step + 1] += jnp.dot(
+                left_ref[w], inner.astype(jnp.bfloat16), preferred_element_type=jnp.float32
+            )
+            return carry
+
+        lax.fori_loop(0, channels, channel, 0)
+        krylov_ref[step + 1] = krylov_ref[step + 1] * live
+    row = lax.broadcasted_iota(jnp.int32, gram_ref.shape, 0)
+    lane = lax.broadcasted_iota(jnp.int32, gram_ref.shape, 1)
+    out = jnp.zeros(gram_ref.shape, jnp.float32)
     slot = 0
-    for i in range(size):
-        for j in range(i, size):
+    for i in range(LANCZOS + 1):
+        for j in range(i, LANCZOS + 1):
             if i == 0 and j == 0:
-                head = head_ref[...]
                 total = jnp.sum(head * head, axis=(0, 1), keepdims=True)
             else:
-                total = jnp.sum(vec_refs[i][...] * vec_refs[j][...], axis=(0, 1), keepdims=True)
+                total = jnp.sum(krylov_ref[i] * krylov_ref[j], axis=(0, 1), keepdims=True)
             out = jnp.where((row == 0) & (lane == slot), total, out)
             slot += 1
-    out_ref[...] = out
+    gram_ref[...] = out
 
 
 def ritz_kernel(total_ref, out_ref):
@@ -151,43 +156,38 @@
     out_ref[...] = jnp.where(lane == LANCZOS, energy, out)
 
 
-def combine_kernel(coef_ref, head_ref, *refs, scale):
-    *vec_refs, out_ref = refs
-    rows, cols = vec_refs[0].shape
-    acc = vec_refs[0][...] * coef_ref[0, 0]
-    for step in range(1, len(vec_refs)):
-        acc = acc + coef_ref[0, step] * vec_refs[step][...]
+def combine_kernel(coef_ref, start_ref, mask_ref, krylov_ref, out_ref, *, scale):
+    n = krylov_ref.shape[-1]
+    head = start_ref[...] * mask_ref[...]
+    acc = head[:n, :n] * coef_ref[0, 0]
+    for step in range(1, LANCZOS):
+        acc = acc + coef_ref[0, step] * krylov_ref[step]
     if scale is not None:
         acc = acc * scale
-    if head_ref.shape != vec_refs[0].shape:
-        rest = head_ref[...] * coef_ref[0, 0]
+    if head.shape != (n, n):
+        rest = head * coef_ref[0, 0]
         if scale is not None:
             rest = rest * scale
         out_ref[...] = rest
-    out_ref[:rows, :cols] = acc
-
-
-def lanczos(start, left, right, mask, scale=None, cut=None, hooks=None):
-    head = start * mask
-    if cut is None:
-        base, live = head, mask
-    else:
-        base, live = head[:cut, :cut], mask[:cut, :cut]
-    krylov = [base]
-    for step in range(LANCZOS):
-        krylov.append(apply_ham(krylov[-1], left, right, live))
+    out_ref[:n, :n] = acc
+
+
+def lanczos(start, left, right, mask, scale=None, hooks=None):
+    n = left.shape[-1]
     tile = jax.ShapeDtypeStruct((8, 128), jnp.float32)
-    local = pl.pallas_call(gram_kernel, out_shape=tile)(head, *krylov)
+    krylov, local = pl.pallas_call(
+        krylov_kernel,
+        out_shape=(jax.ShapeDtypeStruct((LANCZOS + 1, n, n), jnp.float32), tile),
+    )(start, mask, left, right)
     total = bond_sum(local, hooks)
-    out = pl.pallas_call(
-        ritz_kernel, out_shape=tile, in_specs=[pl.BlockSpec(memory_space=pltpu.SMEM)]
-    )(total)
+    smem = pl.BlockSpec(memory_space=pltpu.SMEM)
+    out = pl.pallas_call(ritz_kernel, out_shape=tile, in_specs=[smem])(total)
     vec_spec = pl.BlockSpec(memory_space=pltpu.VMEM)
     result = pl.pallas_call(
         functools.partial(combine_kernel, scale=scale),
-        out_shape=jax.ShapeDtypeStruct(head.shape, jnp.float32),
-        in_specs=[pl.BlockSpec(memory_space=pltpu.SMEM)] + [vec_spec] * (LANCZOS + 1),
-    )(out, head, *krylov[:LANCZOS])
+        out_shape=jax.ShapeDtypeStruct(start.shape, jnp.float32),
+        in_specs=[smem, vec_spec, vec_spec, vec_spec],
+    )(out, start, mask, krylov)
     return (result, out[0, LANCZOS])
 
 
@@ -244,7 +244,7 @@
     left_in = env_update(left_mix, left_a_got)
     right_in = env_update(right_mix, right_a_got.T)
     ground, energy = lanczos(
-        psi_one, left_in, right_in, mask, math.sqrt(blocks * width * width), cut
+        psi_one, left_in, right_in, mask, math.sqrt(blocks * width * width)
     )
     return (ground[None, None], jnp.reshape(energy, (1,)))
 

time: 113 us -> 145 us (1.28)
  Pallas kernels: 11.4 us -> 68.4 us
  matrix products: 41.8 us -> 18.1 us
    pallas_call x4, Pallas kernels: 7.61 us -> 64.2 us  [the longest x2 60.8 us: lanczos(): pl.pallas_call(krylov_kernel, out_shape=(jax.ShapeDtypeStruct((LANCZOS +...]
    dot_general x8 -> x0, matrix products: 23.7 us -> none  [apply_ham(): jnp.einsum('wij,wjk->ik', left, inner, preferred_element_type=jnp.float32)]
  transfers between devices with their start and end apart: 14 -> 14, of which waited for: 9 -> 9; matrix products, arithmetic and copies ran while one was open for 35% -> 12% of each run, Pallas kernels for 2% -> 25%
where the time goes in v4:
time: 145 us
  Pallas kernels  68.4 us (47%)
  waiting for transfers between devices  27.6 us (19%)
  starting transfers between devices  22.8 us (16%)
  matrix products  18.1 us (12%)
  other arithmetic  4.62 us (3%)
  between operations  2.01 us (1%)
    pallas_call x2, Pallas kernels, lanczos(): pl.pallas_call(krylov_kernel, out_shape=(jax.ShapeDtypeStruct((LANCZOS +...  60.8 us
    ppermute x10, waiting for transfers between devices, bond_sum(): value = value + lax.ppermute(value, 'bond', pairs)  26.2 us
    ppermute x10, starting transfers between devices, bond_sum(): value = value + lax.ppermute(value, 'bond', pairs)  19.3 us
    dot_general x2, matrix products, mixed(): jnp.einsum('wu,uij->wij', mpo_mix, env.astype(jnp.float32), precision=lax...  11.6 us
    dot_general x2, matrix products, env_update(): jnp.einsum('ji,wjk->wik', left_a, half_left, preferred_element_type=jnp.f...  6.44 us
    pallas_call x2, Pallas kernels, lanczos(): pl.pallas_call(functools.partial(combine_kernel, scale=scale), out_shape=...  4.18 us
    ppermute x4, starting transfers between devices, shifted(): return lax.ppermute(value, axis, pairs)  3.48 us
    pallas_call x2, Pallas kernels, lanczos(): out = pl.pallas_call(ritz_kernel, out_shape=tile, in_specs=[smem])(total)  3.35 us
  transfers between devices with their start and end apart: 14, of which 9 were waited for; matrix products, arithmetic and copies ran while one was open for 12% of the time, Pallas kernels for 25%

profile of v4, /device:TPU:16, one launch (start us, length us, event | category | flops | bytes accessed | tf_op | source)
XLA Modules:
  0.0 144.7 jit_solution(10267597040289780036)
XLA Ops:
  0.6 0.0 copy-start
  0.6 0.0 collective-permute-start.1
  0.7 2.9 %collective-permute-start.2 = (bf16[20,256,256]{2,1,0:T(8,128)(2,1)}, bf16[20,256,256]{2,1,0:T(8,128)(2,1)S(1)}, u32[]{:S(2)}, u32[]{:S(2)}) collective-permute-start(bf16[20,256,256]{2,1,0:T(8,128)(2,1)} %bitcast.32), channel_id=1, source_target_pairs={{0,224},{32,0},{64,32},{96,64},{128,96},{160,128},{192,160},{224,1... | collective-permute-start | bytes 7864328 | tf_op jit(solution)/shard_map/ppermute | solution.py:18
  4.3 0.8 broadcast_multiply_fusion.1.mask_ref
  5.1 36.1 %shard_map.77 = (f32[5,256,256]{2,1,0:T(8,128)}, f32[8,128]{1,0:T(8,128)}) custom-call(f32[256,256]{1,0:T(8,128)} %bitcast.34, f32[256,256]{1,0:T(8,128)} %broadcast_multiply_fusion.1.mask_ref, bf16[20,256,256]{2,1,0:T(8,128)(2,1)} %bitcast.31, bf16[20,256,256]{2,1,0:T(8,128)(2,1)} %bitcast.33), custom_call_target="tpu_custom_call" | custom-call | tf_op jit(solution)/shard_map/pallas_call | solution.py:178
  41.2 1.3 collective-permute-start
  43.1 1.9 %collective-permute-done = f32[8,128]{1,0:T(8,128)S(1)} collective-permute-done((f32[8,128]{1,0:T(8,128)}, f32[8,128]{1,0:T(8,128)S(1)}, u32[]{:S(2)}, u32[]{:S(2)}) %collective-permute-start) | collective-permute-done | bytes 4128 | tf_op jit(solution)/shard_map/ppermute | solution.py:33
  45.0 0.7 add.30
  45.7 0.0 collective-permute-done.1
  45.7 0.0 collective-permute-done.2
  45.7 2.1 %collective-permute-start.3 = (f32[8,128]{1,0:T(8,128)S(1)}, f32[8,128]{1,0:T(8,128)S(1)}, u32[]{:S(2)}, u32[]{:S(2)}) collective-permute-start(f32[8,128]{1,0:T(8,128)S(1)} %add.30), channel_id=1, source_target_pairs={{0,2},{1,3},{2,0},{3,1},{4,6},{5,7},{6,4},{7,5},{8,10},{9,11},{10,... | collective-permute-start | bytes 12296 | tf_op jit(solution)/shard_map/ppermute | solution.py:33
  47.8 3.0 %collective-permute-done.3 = f32[8,128]{1,0:T(8,128)S(1)} collective-permute-done((f32[8,128]{1,0:T(8,128)S(1)}, f32[8,128]{1,0:T(8,128)S(1)}, u32[]{:S(2)}, u32[]{:S(2)}) %collective-permute-start.3) | collective-permute-done | bytes 4128 | tf_op jit(solution)/shard_map/ppermute | solution.py:33
  50.8 1.9 %collective-permute-start.4 = (f32[8,128]{1,0:T(8,128)S(1)}, f32[8,128]{1,0:T(8,128)S(1)}, u32[]{:S(2)}, u32[]{:S(2)}) collective-permute-start(f32[8,128]{1,0:T(8,128)S(1)} %add.31), channel_id=1, source_target_pairs={{0,4},{1,5},{2,6},{3,7},{4,0},{5,1},{6,2},{7,3},{8,12},{9,13},{10,... | collective-permute-start | bytes 12296 | tf_op jit(solution)/shard_map/ppermute | solution.py:33
  52.7 0.0 copy-done
  52.7 6.8 %convert_bitcast_fusion.1 = bf16[20,256,256]{2,0,1:T(8,128)(2,1)} fusion(bf16[20,256,256]{2,1,0:T(8,128)(2,1)} %collective-permute-done.1, f32[20,20]{1,0:T(8,128)S(1)} %copy-done), kind=kOutput, calls=%fused_computation.5 | convolution fusion | flops 315883520 | bytes 5244480 | tf_op jit(solution)/shard_map/wu,uij->wij/dot_general | solution.py:217
  59.6 0.0 collective-permute-done.4
  59.6 3.3 %collective-permute-start.5 = (f32[8,128]{1,0:T(8,128)S(1)}, f32[8,128]{1,0:T(8,128)S(1)}, u32[]{:S(2)}, u32[]{:S(2)}) collective-permute-start(f32[8,128]{1,0:T(8,128)S(1)} %add.32), channel_id=1, source_target_pairs={{0,8},{1,9},{2,10},{3,11},{4,12},{5,13},{6,14},{7,15},{8,0},{9,1},... | collective-permute-start | bytes 12296 | tf_op jit(solution)/shard_map/ppermute | solution.py:33
  62.9 4.8 %convert_bitcast_fusion = bf16[20,256,256]{2,0,1:T(8,128)(2,1)} fusion(bf16[20,256,256]{2,1,0:T(8,128)(2,1)S(1)} %collective-permute-done.2, f32[20,20]{1,0:T(8,128)S(1)} %copy-done), kind=kOutput, calls=%fused_computation.4 | convolution fusion | flops 315883520 | bytes 5244480 | tf_op jit(solution)/shard_map/wu,uij->wij/dot_general | solution.py:217
  67.6 0.0 collective-permute-done.5
  67.6 4.5 %collective-permute-start.6 = (f32[8,128]{1,0:T(8,128)S(1)}, f32[8,128]{1,0:T(8,128)S(1)}, u32[]{:S(2)}, u32[]{:S(2)}) collective-permute-start(f32[8,128]{1,0:T(8,128)S(1)} %add.33), channel_id=1, source_target_pairs={{0,16},{1,17},{2,18},{3,19},{4,20},{5,21},{6,22},{7,23},{8,24},{9,... | collective-permute-start | bytes 12296 | tf_op jit(solution)/shard_map/ppermute | solution.py:33
  72.1 3.0 %collective-permute-done.6 = f32[8,128]{1,0:T(8,128)S(1)} collective-permute-done((f32[8,128]{1,0:T(8,128)S(1)}, f32[8,128]{1,0:T(8,128)S(1)}, u32[]{:S(2)}, u32[]{:S(2)}) %collective-permute-start.6) | collective-permute-done | bytes 4128 | tf_op jit(solution)/shard_map/ppermute | solution.py:33
  75.2 0.6 add.34.total_ref
  75.7 1.7 %shard_map.78.coef_ref = f32[8,128]{1,0:T(8,128)} custom-call(f32[8,128]{1,0:T(8,128)} %add.34.total_ref), custom_call_target="tpu_custom_call" | custom-call | tf_op jit(solution)/shard_map/pallas_call | solution.py:184
  77.4 2.3 %shard_map.79.start_ref = f32[256,256]{1,0:T(8,128)} custom-call(f32[8,128]{1,0:T(8,128)} %shard_map.78.coef_ref, f32[256,256]{1,0:T(8,128)} %bitcast.35, f32[256,256]{1,0:T(8,128)} %broadcast_multiply_fusion.1.mask_ref, f32[5,256,256]{2,1,0:T(8,128)} %get-tuple-element.19.krylov_ref), custom_call_target="tpu_custom_call" | custom-call | tf_op jit(solution)/shard_map/pallas_call | solution.py:186
  79.7 0.0 copy-start.1
  79.7 1.1 broadcast_multiply_fusion
  80.8 0.1 fusion.36
  80.9 0.0 collective-permute-start.8
  81.0 0.5 collective-permute-start.7
  81.5 1.4 collective-permute-done.8
  82.9 4.2 %fusion.30.right_ref = bf16[20,128,128]{2,1,0:T(8,128)(2,1)} fusion(bf16[20,256,256]{2,0,1:T(8,128)(2,1)} %convert_bitcast_fusion, bf16[128,256]{1,0:T(8,128)(2,1)S(1)} %collective-permute-done.8), kind=kOutput, calls=%fused_computation.16 | convolution fusion | flops 504299520 | bytes 3342336 | tf_op jit(solution)/shard_map/ji,wjk->wik/dot_general | solution.py:198
  87.0 0.0 collective-permute-done.7
  87.0 0.0 copy-done.1
  87.0 2.3 %fusion.33.left_ref = bf16[20,128,128]{2,1,0:T(8,128)(2,1)} fusion(bf16[20,256,256]{2,0,1:T(8,128)(2,1)S(1)} %copy-done.1, bf16[256,128]{1,0:T(8,128)(2,1)S(1)} %collective-permute-done.7), kind=kOutput, calls=%fused_computation.17 | convolution fusion | flops 504299520 | bytes 3342336 | tf_op jit(solution)/shard_map/ji,wjk->wik/dot_general | solution.py:198
  89.3 24.7 %shard_map.80 = (f32[5,128,128]{2,1,0:T(8,128)}, f32[8,128]{1,0:T(8,128)}) custom-call(f32[256,256]{1,0:T(8,128)} %shard_map.79.start_ref, f32[256,256]{1,0:T(8,128)} %broadcast_multiply_fusion.1.mask_ref, bf16[20,128,128]{2,1,0:T(8,128)(2,1)} %fusion.33.left_ref, bf16[20,128,128]{2,1,0:T(8,128)(2,1)} %fusion.30.right_ref), custom_call_target="tpu_custom_call" | custom-call | tf_op jit(solution)/shard_map/pallas_call | solution.py:178
  114.0 1.3 collective-permute-start.9
  115.3 2.5 %collective-permute-done.9 = f32[8,128]{1,0:T(8,128)S(1)} collective-permute-done((f32[8,128]{1,0:T(8,128)}, f32[8,128]{1,0:T(8,128)S(1)}, u32[]{:S(2)}, u32[]{:S(2)}) %collective-permute-start.9) | collective-permute-done | bytes 4128 | tf_op jit(solution)/shard_map/ppermute | solution.py:33
  117.8 0.7 add.35
  118.5 0.3 collective-permute-start.10
  118.9 4.8 %collective-permute-done.10 = f32[8,128]{1,0:T(8,128)S(1)} collective-permute-done((f32[8,128]{1,0:T(8,128)S(1)}, f32[8,128]{1,0:T(8,128)S(1)}, u32[]{:S(2)}, u32[]{:S(2)}) %collective-permute-start.10) | collective-permute-done | bytes 4128 | tf_op jit(solution)/shard_map/ppermute | solution.py:33
  123.7 0.1 collective-permute-start.11
  123.8 3.5 %collective-permute-done.11 = f32[8,128]{1,0:T(8,128)S(1)} collective-permute-done((f32[8,128]{1,0:T(8,128)S(1)}, f32[8,128]{1,0:T(8,128)S(1)}, u32[]{:S(2)}, u32[]{:S(2)}) %collective-permute-start.11) | collective-permute-done | bytes 4128 | tf_op jit(solution)/shard_map/ppermute | solution.py:33
  127.3 0.0 collective-permute-start.12
  127.3 4.5 %collective-permute-done.12 = f32[8,128]{1,0:T(8,128)S(1)} collective-permute-done((f32[8,128]{1,0:T(8,128)S(1)}, f32[8,128]{1,0:T(8,128)S(1)}, u32[]{:S(2)}, u32[]{:S(2)}) %collective-permute-start.12) | collective-permute-done | bytes 4128 | tf_op jit(solution)/shard_map/ppermute | solution.py:33
  131.8 4.5 %collective-permute-start.13 = (f32[8,128]{1,0:T(8,128)S(1)}, f32[8,128]{1,0:T(8,128)S(1)}, u32[]{:S(2)}, u32[]{:S(2)}) collective-permute-start(f32[8,128]{1,0:T(8,128)S(1)} %add.38), channel_id=1, source_target_pairs={{0,16},{1,17},{2,18},{3,19},{4,20},{5,21},{6,22},{7,23},{8,24},{9,... | collective-permute-start | bytes 12296 | tf_op jit(solution)/shard_map/ppermute | solution.py:33
  136.3 3.0 %collective-permute-done.13 = f32[8,128]{1,0:T(8,128)S(1)} collective-permute-done((f32[8,128]{1,0:T(8,128)S(1)}, f32[8,128]{1,0:T(8,128)S(1)}, u32[]{:S(2)}, u32[]{:S(2)}) %collective-permute-start.13) | collective-permute-done | bytes 4128 | tf_op jit(solution)/shard_map/ppermute | solution.py:33
  139.3 0.6 add.39.total_ref
  139.9 1.7 %shard_map.81.coef_ref = f32[8,128]{1,0:T(8,128)} custom-call(f32[8,128]{1,0:T(8,128)} %add.39.total_ref), custom_call_target="tpu_custom_call" | custom-call | tf_op jit(solution)/shard_map/pallas_call | solution.py:184
  141.6 1.3 slice.20
  142.8 1.9 %shard_map.82 = f32[256,256]{1,0:T(8,128)} custom-call(f32[8,128]{1,0:T(8,128)} %shard_map.81.coef_ref, f32[256,256]{1,0:T(8,128)} %shard_map.79.start_ref, f32[256,256]{1,0:T(8,128)} %broadcast_multiply_fusion.1.mask_ref, f32[5,128,128]{2,1,0:T(8,128)} %get-tuple-element.23.krylov_ref), custom_call_target="tpu_custom_call" | custom-call | tf_op jit(solution)/shard_map/pallas_call | solution.py:186
  (10 shorter events, 0.0 us)
Async XLA Ops:
  0.6 52.1 %copy-start = (f32[20,20]{1,0:T(8,128)S(1)}, f32[20,20]{1,0:T(8,128)}, u32[]{:S(2)}) copy-start(f32[20,20]{1,0:T(8,128)} %param.9) | copy-start | bytes 4804
  0.6 45.0 %collective-permute-start.1 = (bf16[20,256,256]{2,1,0:T(8,128)(2,1)}, bf16[20,256,256]{2,1,0:T(8,128)(2,1)}, u32[]{:S(2)}, u32[]{:S(2)}) collective-permute-start(bf16[20,256,256]{2,1,0:T(8,128)(2,1)} %bitcast.30), channel_id=1, source_target_pairs={{0,32},{32,64},{64,96},{96,128},{128,160},{160,192},{192,224},{224... | collective-permute-start | bytes 7864328 | tf_op jit(solution)/shard_map/ppermute | solution.py:18
  0.7 45.0 %collective-permute-start.2 = (bf16[20,256,256]{2,1,0:T(8,128)(2,1)}, bf16[20,256,256]{2,1,0:T(8,128)(2,1)S(1)}, u32[]{:S(2)}, u32[]{:S(2)}) collective-permute-start(bf16[20,256,256]{2,1,0:T(8,128)(2,1)} %bitcast.32), channel_id=1, source_target_pairs={{0,224},{32,0},{64,32},{96,64},{128,96},{160,128},{192,160},{224,1... | collective-permute-start | bytes 7864328 | tf_op jit(solution)/shard_map/ppermute | solution.py:18
  41.2 3.8 %collective-permute-start = (f32[8,128]{1,0:T(8,128)}, f32[8,128]{1,0:T(8,128)S(1)}, u32[]{:S(2)}, u32[]{:S(2)}) collective-permute-start(f32[8,128]{1,0:T(8,128)} %get-tuple-element.13), channel_id=1, source_target_pairs={{0,1},{1,0},{2,3},{3,2},{4,5},{5,4},{6,7},{7,6},{8,9},{9,8},{10,11... | collective-permute-start | bytes 12296 | tf_op jit(solution)/shard_map/ppermute | solution.py:33
  45.7 5.1 %collective-permute-start.3 = (f32[8,128]{1,0:T(8,128)S(1)}, f32[8,128]{1,0:T(8,128)S(1)}, u32[]{:S(2)}, u32[]{:S(2)}) collective-permute-start(f32[8,128]{1,0:T(8,128)S(1)} %add.30), channel_id=1, source_target_pairs={{0,2},{1,3},{2,0},{3,1},{4,6},{5,7},{6,4},{7,5},{8,10},{9,11},{10,... | collective-permute-start | bytes 12296 | tf_op jit(solution)/shard_map/ppermute | solution.py:33
  50.8 8.8 %collective-permute-start.4 = (f32[8,128]{1,0:T(8,128)S(1)}, f32[8,128]{1,0:T(8,128)S(1)}, u32[]{:S(2)}, u32[]{:S(2)}) collective-permute-start(f32[8,128]{1,0:T(8,128)S(1)} %add.31), channel_id=1, source_target_pairs={{0,4},{1,5},{2,6},{3,7},{4,0},{5,1},{6,2},{7,3},{8,12},{9,13},{10,... | collective-permute-start | bytes 12296 | tf_op jit(solution)/shard_map/ppermute | solution.py:33
  59.6 8.0 %collective-permute-start.5 = (f32[8,128]{1,0:T(8,128)S(1)}, f32[8,128]{1,0:T(8,128)S(1)}, u32[]{:S(2)}, u32[]{:S(2)}) collective-permute-start(f32[8,128]{1,0:T(8,128)S(1)} %add.32), channel_id=1, source_target_pairs={{0,8},{1,9},{2,10},{3,11},{4,12},{5,13},{6,14},{7,15},{8,0},{9,1},... | collective-permute-start | bytes 12296 | tf_op jit(solution)/shard_map/ppermute | solution.py:33
  67.6 7.5 %collective-permute-start.6 = (f32[8,128]{1,0:T(8,128)S(1)}, f32[8,128]{1,0:T(8,128)S(1)}, u32[]{:S(2)}, u32[]{:S(2)}) collective-permute-start(f32[8,128]{1,0:T(8,128)S(1)} %add.33), channel_id=1, source_target_pairs={{0,16},{1,17},{2,18},{3,19},{4,20},{5,21},{6,22},{7,23},{8,24},{9,... | collective-permute-start | bytes 12296 | tf_op jit(solution)/shard_map/ppermute | solution.py:33
  79.7 7.3 %copy-start.1 = (bf16[20,256,256]{2,0,1:T(8,128)(2,1)S(1)}, bf16[20,256,256]{2,0,1:T(8,128)(2,1)}, u32[]{:S(2)}) copy-start(bf16[20,256,256]{2,0,1:T(8,128)(2,1)} %convert_bitcast_fusion.1) | copy-start | bytes 7864324
  80.9 1.9 %collective-permute-start.8 = (bf16[128,256]{1,0:T(8,128)(2,1)S(1)}, bf16[128,256]{1,0:T(8,128)(2,1)S(1)}, u32[]{:S(2)}, u32[]{:S(2)}) collective-permute-start(bf16[128,256]{1,0:T(8,128)(2,1)S(1)} %fusion.36), channel_id=1, source_target_pairs={{0,224},{32,0},{64,32},{96,64},{128,96},{160,128},{192,160},{224,1... | collective-permute-start | bytes 196616 | tf_op jit(solution)/shard_map/ppermute | solution.py:18
  81.0 6.0 %collective-permute-start.7 = (bf16[256,128]{1,0:T(8,128)(2,1)S(1)}, bf16[256,128]{1,0:T(8,128)(2,1)S(1)}, u32[]{:S(2)}, u32[]{:S(2)}) collective-permute-start(bf16[256,128]{1,0:T(8,128)(2,1)S(1)} %fusion.37), channel_id=1, source_target_pairs={{0,32},{32,64},{64,96},{96,128},{128,160},{160,192},{192,224},{224... | collective-permute-start | bytes 196616 | tf_op jit(solution)/shard_map/ppermute | solution.py:18
  114.0 3.8 %collective-permute-start.9 = (f32[8,128]{1,0:T(8,128)}, f32[8,128]{1,0:T(8,128)S(1)}, u32[]{:S(2)}, u32[]{:S(2)}) collective-permute-start(f32[8,128]{1,0:T(8,128)} %get-tuple-element.22), channel_id=1, source_target_pairs={{0,1},{1,0},{2,3},{3,2},{4,5},{5,4},{6,7},{7,6},{8,9},{9,8},{10,11... | collective-permute-start | bytes 12296 | tf_op jit(solution)/shard_map/ppermute | solution.py:33
  118.5 5.1 %collective-permute-start.10 = (f32[8,128]{1,0:T(8,128)S(1)}, f32[8,128]{1,0:T(8,128)S(1)}, u32[]{:S(2)}, u32[]{:S(2)}) collective-permute-start(f32[8,128]{1,0:T(8,128)S(1)} %add.35), channel_id=1, source_target_pairs={{0,2},{1,3},{2,0},{3,1},{4,6},{5,7},{6,4},{7,5},{8,10},{9,11},{10,... | collective-permute-start | bytes 12296 | tf_op jit(solution)/shard_map/ppermute | solution.py:33
  123.7 3.6 %collective-permute-start.11 = (f32[8,128]{1,0:T(8,128)S(1)}, f32[8,128]{1,0:T(8,128)S(1)}, u32[]{:S(2)}, u32[]{:S(2)}) collective-permute-start(f32[8,128]{1,0:T(8,128)S(1)} %add.36), channel_id=1, source_target_pairs={{0,4},{1,5},{2,6},{3,7},{4,0},{5,1},{6,2},{7,3},{8,12},{9,13},{10,... | collective-permute-start | bytes 12296 | tf_op jit(solution)/shard_map/ppermute | solution.py:33
  127.3 4.5 %collective-permute-start.12 = (f32[8,128]{1,0:T(8,128)S(1)}, f32[8,128]{1,0:T(8,128)S(1)}, u32[]{:S(2)}, u32[]{:S(2)}) collective-permute-start(f32[8,128]{1,0:T(8,128)S(1)} %add.37), channel_id=1, source_target_pairs={{0,8},{1,9},{2,10},{3,11},{4,12},{5,13},{6,14},{7,15},{8,0},{9,1},... | collective-permute-start | bytes 12296 | tf_op jit(solution)/shard_map/ppermute | solution.py:33
  131.8 7.5 %collective-permute-start.13 = (f32[8,128]{1,0:T(8,128)S(1)}, f32[8,128]{1,0:T(8,128)S(1)}, u32[]{:S(2)}, u32[]{:S(2)}) collective-permute-start(f32[8,128]{1,0:T(8,128)S(1)} %add.38), channel_id=1, source_target_pairs={{0,16},{1,17},{2,18},{3,19},{4,20},{5,21},{6,22},{7,23},{8,24},{9,... | collective-permute-start | bytes 12296 | tf_op jit(solution)/shard_map/ppermute | solution.py:33

commit v5 on v3

--- a/solution.py
+++ b/solution.py
@@ -65,9 +65,8 @@
     out_ref[...] = out
 
 
-def ritz_kernel(total_ref, out_ref):
+def ritz_coefficients(total_ref, shape):
     size = LANCZOS + 1
-    shape = out_ref.shape
     slots = {}
     slot = 0
     for i in range(size):
@@ -144,30 +143,41 @@
     coef = [c * weights[0] for c in basis[0]]
     for step in range(1, LANCZOS):
         coef = [c + weights[step] * b for c, b in zip(coef, basis[step])]
-    lane = lax.broadcasted_iota(jnp.int32, shape, 1)
-    out = zero
-    for slot in range(LANCZOS):
-        out = jnp.where(lane == slot, coef[slot], out)
-    out_ref[...] = jnp.where(lane == LANCZOS, energy, out)
-
-
-def combine_kernel(coef_ref, head_ref, *refs, scale):
-    *vec_refs, out_ref = refs
+    return coef, energy
+
+
+def finish_kernel(total_ref, head_ref, *refs, scale, cut, rank_scale):
+    if rank_scale is None:
+        *vec_refs, out_ref, energy_ref = refs
+    else:
+        rank_ref, *vec_refs, out_ref, left_ref, right_ref = refs
+    coef, energy = ritz_coefficients(total_ref, (8, 128))
+    coef = [c[:1, :1] for c in coef]
     rows, cols = vec_refs[0].shape
-    acc = vec_refs[0][...] * coef_ref[0, 0]
+    acc = vec_refs[0][...] * coef[0]
     for step in range(1, len(vec_refs)):
-        acc = acc + coef_ref[0, step] * vec_refs[step][...]
+        acc = acc + coef[step] * vec_refs[step][...]
     if scale is not None:
         acc = acc * scale
     if head_ref.shape != vec_refs[0].shape:
-        rest = head_ref[...] * coef_ref[0, 0]
+        rest = head_ref[...] * coef[0]
         if scale is not None:
             rest = rest * scale
         out_ref[...] = rest
     out_ref[:rows, :cols] = acc
-
-
-def lanczos(start, left, right, mask, scale=None, cut=None, hooks=None):
+    if rank_scale is None:
+        energy_ref[...] = energy[:1, :1]
+    else:
+        rank = rank_ref[0, 0]
+        scaled = out_ref[...] * rank_scale
+        width = scaled.shape[0]
+        col = lax.broadcasted_iota(jnp.int32, (width, cut), 1)
+        left_ref[...] = (scaled[:, :cut] * (col < rank).astype(jnp.float32)).astype(jnp.bfloat16)
+        row = lax.broadcasted_iota(jnp.int32, (cut, width), 0)
+        right_ref[...] = (scaled[:cut, :] * (row < rank).astype(jnp.float32)).astype(jnp.bfloat16)
+
+
+def lanczos(start, left, right, mask, scale=None, cut=None, hooks=None, rank=None):
     head = start * mask
     if cut is None:
         base, live = head, mask
@@ -179,16 +189,31 @@
     tile = jax.ShapeDtypeStruct((8, 128), jnp.float32)
     local = pl.pallas_call(gram_kernel, out_shape=tile)(head, *krylov)
     total = bond_sum(local, hooks)
-    out = pl.pallas_call(
-        ritz_kernel, out_shape=tile, in_specs=[pl.BlockSpec(memory_space=pltpu.SMEM)]
-    )(total)
-    vec_spec = pl.BlockSpec(memory_space=pltpu.VMEM)
-    result = pl.pallas_call(
-        functools.partial(combine_kernel, scale=scale),
-        out_shape=jax.ShapeDtypeStruct(head.shape, jnp.float32),
-        in_specs=[pl.BlockSpec(memory_space=pltpu.SMEM)] + [vec_spec] * (LANCZOS + 1),
-    )(out, head, *krylov[:LANCZOS])
-    return (result, out[0, LANCZOS])
+    smem = pl.BlockSpec(memory_space=pltpu.SMEM)
+    vmem = pl.BlockSpec(memory_space=pltpu.VMEM)
+    width = head.shape[-1]
+    field = jax.ShapeDtypeStruct(head.shape, jnp.float32)
+    if rank is None:
+        in_specs = [smem, vmem] + [vmem] * LANCZOS
+        out_shape = (field, jax.ShapeDtypeStruct((1, 1), jnp.float32))
+        extra = ()
+        rank_scale = None
+    else:
+        in_specs = [smem, vmem, smem] + [vmem] * LANCZOS
+        out_shape = (
+            field,
+            jax.ShapeDtypeStruct((width, width // 2), jnp.bfloat16),
+            jax.ShapeDtypeStruct((width // 2, width), jnp.bfloat16),
+        )
+        extra = (rank,)
+        rank_scale = math.sqrt(lax.axis_size("bond") * width)
+    return pl.pallas_call(
+        functools.partial(
+            finish_kernel, scale=scale, cut=width // 2, rank_scale=rank_scale
+        ),
+        out_shape=out_shape,
+        in_specs=in_specs,
+    )(total, head, *extra, *krylov[:LANCZOS])
 
 
 def env_update(mixed, left_a):
@@ -233,12 +258,9 @@
         return value
 
     hooks = {1: take_envs, 3: mix_left, 4: mix_right}
-    psi_one, unused = lanczos(start, left, right, mask, hooks=hooks)
+    cut = width // 2
+    psi_one, left_a, right_a = lanczos(start, left, right, mask, hooks=hooks, rank=ranks)
     left_mix, right_mix = held["left"], held["right"]
-    scaled = psi_one * math.sqrt(blocks * width)
-    cut = width // 2
-    left_a = (scaled[:, :cut] * kept[None, :cut]).astype(jnp.bfloat16)
-    right_a = (scaled[:cut, :] * kept[:cut, None]).astype(jnp.bfloat16)
     left_a_got = shifted(left_a, "seg", 1)
     right_a_got = shifted(right_a, "seg", -1)
     left_in = env_update(left_mix, left_a_got)

time: 113 us -> 109 us (0.965)
  Pallas kernels: 11.4 us -> 8.86 us
  local copies, waits for them, and re-layouts: 1.92 us -> 0.7 us
    pallas_call x4 -> x2, Pallas kernels: 7.17 us -> 4.6 us  [lanczos(): pl.pallas_call(functools.partial(finish_kernel, scale=scale, cut=width //...]
    slice x1 -> x0, local copies, waits for them, and re-layouts: 1.25 us -> none  [lanczos(): return (result, out[0, LANCZOS])]
  transfers between devices with their start and end apart: 14 -> 14, of which waited for: 9 -> 8; matrix products, arithmetic and copies ran while one was open for 35% -> 37% of each run, Pallas kernels for 2% -> 2%
where the time goes in v5:
time: 109 us
  matrix products  42.5 us (39%)
  waiting for transfers between devices  26.3 us (24%)
  starting transfers between devices  22.8 us (21%)
  Pallas kernels  8.86 us (8%)
  other arithmetic  5.39 us (5%)
  between operations  2.1 us (2%)
    ppermute x10, waiting for transfers between devices, bond_sum(): value = value + lax.ppermute(value, 'bond', pairs)  26.3 us
    dot_general x8, matrix products, apply_ham(): jnp.einsum('wij,wjk->ik', left, inner, preferred_element_type=jnp.float32)  24.4 us
    ppermute x10, starting transfers between devices, bond_sum(): value = value + lax.ppermute(value, 'bond', pairs)  19.3 us
    dot_general x2, matrix products, mixed(): jnp.einsum('wu,uij->wij', mpo_mix, env.astype(jnp.float32), precision=lax...  11.6 us
    dot_general x2, matrix products, env_update(): jnp.einsum('ji,wjk->wik', left_a, half_left, preferred_element_type=jnp.f...  6.49 us
    pallas_call x2, Pallas kernels, lanczos(): pl.pallas_call(functools.partial(finish_kernel, scale=scale, cut=width //...  4.6 us
    pallas_call x2, Pallas kernels, lanczos(): local = pl.pallas_call(gram_kernel, out_shape=tile)(head, *krylov)  4.26 us
    ppermute x4, starting transfers between devices, shifted(): return lax.ppermute(value, axis, pairs)  3.47 us
  transfers between devices with their start and end apart: 14, of which 8 were waited for; matrix products, arithmetic and copies ran while one was open for 37% of the time, Pallas kernels for 2%

profile of v5, /device:TPU:16, one launch (start us, length us, event | category | flops | bytes accessed | tf_op | source)
XLA Modules:
  0.0 108.6 jit_solution(316477631758293577)
XLA Ops:
  0.6 0.0 copy-start
  0.6 0.0 collective-permute-start.1
  0.7 2.9 %collective-permute-start.2 = (bf16[20,256,256]{2,1,0:T(8,128)(2,1)}, bf16[20,256,256]{2,1,0:T(8,128)(2,1)S(1)}, u32[]{:S(2)}, u32[]{:S(2)}) collective-permute-start(bf16[20,256,256]{2,1,0:T(8,128)(2,1)} %bitcast.192), channel_id=1, source_target_pairs={{0,224},{32,0},{64,32},{96,64},{128,96},{160,128},{192,160},{224,1... | collective-permute-start | bytes 7864328 | tf_op jit(solution)/shard_map/ppermute | solution.py:18
  4.3 1.8 %broadcast_multiply_fusion = (f32[256,256]{1,0:T(8,128)S(1)}, f32[256,256]{1,0:T(8,128)}) fusion(f32[256]{0:T(256)S(1)} %compare_convert_fusion, f32[1,1,256,256]{3,2,1,0:T(8,128)} %param.6), kind=kLoop, calls=%fused_computation.81 | loop fusion | flops 131072 | bytes 787456 | tf_op jit(solution)/shard_map/mul | solution.py:236
  6.0 5.1 %fusion.67.refs_1_.refs_2_ = f32[256,256]{1,0:T(8,128)S(1)} fusion(f32[1,1,256,256]{3,2,1,0:T(8,128)} %param.6, f32[256]{0:T(256)S(1)} %compare_convert_fusion, bf16[1,1,20,256,256]{4,3,2,1,0:T(8,128)(2,1)} %param.7, bf16[1,1,20,256,256]{4,3,2,1,0:T(8,128)(2,1)} %param.8), kind=kOutput, calls=%fused_computation.47 | convolution fusion | flops 1343881216 | bytes 5768192 | tf_op jit(solution)/shard_map/wij,wjk->ik/dot_general | solution.py:45
  11.1 0.0 copy-start.2
  11.1 5.1 %fusion.73.refs_2_.refs_3_ = f32[256,256]{1,0:T(8,128)S(1)} fusion(f32[256,256]{1,0:T(8,128)S(1)} %fusion.67.refs_1_.refs_2_, f32[256]{0:T(256)S(1)} %compare_convert_fusion, bf16[1,1,20,256,256]{4,3,2,1,0:T(8,128)(2,1)} %param.7, bf16[1,1,20,256,256]{4,3,2,1,0:T(8,128)(2,1)} %param.8), kind=kOutput, calls=%fused_computation.49 | convolution fusion | flops 1343815680 | bytes 5768192 | tf_op jit(solution)/shard_map/wij,wjk->ik/dot_general | solution.py:45
  16.2 0.0 copy-done.2
  16.2 0.0 copy-start.3
  16.2 5.8 %fusion.79.refs_3_.refs_4_ = f32[256,256]{1,0:T(8,128)} fusion(f32[256,256]{1,0:T(8,128)S(1)} %fusion.73.refs_2_.refs_3_, f32[256]{0:T(256)S(1)} %compare_convert_fusion, bf16[1,1,20,256,256]{4,3,2,1,0:T(8,128)(2,1)} %param.7, bf16[1,1,20,256,256]{4,3,2,1,0:T(8,128)(2,1)} %param.8), kind=kOutput, calls=%fused_computation.51 | convolution fusion | flops 1343815680 | bytes 5768192 | tf_op jit(solution)/shard_map/wij,wjk->ik/dot_general | solution.py:45
  22.0 0.0 copy-done.3
  22.0 5.8 %fusion.85.refs_4_ = f32[256,256]{1,0:T(8,128)} fusion(f32[256,256]{1,0:T(8,128)} %fusion.79.refs_3_.refs_4_, f32[256]{0:T(256)S(1)} %compare_convert_fusion, bf16[1,1,20,256,256]{4,3,2,1,0:T(8,128)(2,1)} %param.7, bf16[1,1,20,256,256]{4,3,2,1,0:T(8,128)(2,1)} %param.8), kind=kOutput, calls=%fused_computation.53 | convolution fusion | flops 1343815680 | bytes 5768192 | tf_op jit(solution)/shard_map/wij,wjk->ik/dot_general | solution.py:45
  27.8 2.4 %shard_map.77 = f32[8,128]{1,0:T(8,128)} custom-call(f32[256,256]{1,0:T(8,128)} %get-tuple-element.27.head_ref.refs_0_.refs_1_, f32[256,256]{1,0:T(8,128)} %get-tuple-element.27.head_ref.refs_0_.refs_1_, f32[256,256]{1,0:T(8,128)} %copy-done.2, f32[256,256]{1,0:T(8,128)} %copy-done.3, f32[256,256]{1,0:T(8,128)} %fusion.79.refs_3_.refs_4_, ...), custom_call_target="tpu_custom_call" | custom-call | tf_op jit(solution)/shard_map/pallas_call | solution.py:190
  30.2 1.3 %collective-permute-start = (f32[8,128]{1,0:T(8,128)}, f32[8,128]{1,0:T(8,128)S(1)}, u32[]{:S(2)}, u32[]{:S(2)}) collective-permute-start(f32[8,128]{1,0:T(8,128)} %shard_map.77), channel_id=1, source_target_pairs={{0,1},{1,0},{2,3},{3,2},{4,5},{5,4},{6,7},{7,6},{8,9},{9,8},{10,11... | collective-permute-start | bytes 12296 | tf_op jit(solution)/shard_map/ppermute | solution.py:33
  31.5 2.5 %collective-permute-done = f32[8,128]{1,0:T(8,128)S(1)} collective-permute-done((f32[8,128]{1,0:T(8,128)}, f32[8,128]{1,0:T(8,128)S(1)}, u32[]{:S(2)}, u32[]{:S(2)}) %collective-permute-start) | collective-permute-done | bytes 4128 | tf_op jit(solution)/shard_map/ppermute | solution.py:33
  34.0 0.7 add.30
  34.7 0.0 collective-permute-done.1
  34.7 0.0 collective-permute-done.2
  34.7 2.1 %collective-permute-start.3 = (f32[8,128]{1,0:T(8,128)S(1)}, f32[8,128]{1,0:T(8,128)S(1)}, u32[]{:S(2)}, u32[]{:S(2)}) collective-permute-start(f32[8,128]{1,0:T(8,128)S(1)} %add.30), channel_id=1, source_target_pairs={{0,2},{1,3},{2,0},{3,1},{4,6},{5,7},{6,4},{7,5},{8,10},{9,11},{10,... | collective-permute-start | bytes 12296 | tf_op jit(solution)/shard_map/ppermute | solution.py:33
  36.8 3.0 %collective-permute-done.3 = f32[8,128]{1,0:T(8,128)S(1)} collective-permute-done((f32[8,128]{1,0:T(8,128)S(1)}, f32[8,128]{1,0:T(8,128)S(1)}, u32[]{:S(2)}, u32[]{:S(2)}) %collective-permute-start.3) | collective-permute-done | bytes 4128 | tf_op jit(solution)/shard_map/ppermute | solution.py:33
  39.8 1.9 %collective-permute-start.4 = (f32[8,128]{1,0:T(8,128)S(1)}, f32[8,128]{1,0:T(8,128)S(1)}, u32[]{:S(2)}, u32[]{:S(2)}) collective-permute-start(f32[8,128]{1,0:T(8,128)S(1)} %add.31), channel_id=1, source_target_pairs={{0,4},{1,5},{2,6},{3,7},{4,0},{5,1},{6,2},{7,3},{8,12},{9,13},{10,... | collective-permute-start | bytes 12296 | tf_op jit(solution)/shard_map/ppermute | solution.py:33
  41.7 0.0 copy-done
  41.7 6.8 %convert_bitcast_fusion.1 = bf16[20,256,256]{2,0,1:T(8,128)(2,1)} fusion(bf16[20,256,256]{2,1,0:T(8,128)(2,1)} %collective-permute-done.1, f32[20,20]{1,0:T(8,128)S(1)} %copy-done), kind=kOutput, calls=%fused_computation.5 | convolution fusion | flops 315883520 | bytes 5244480 | tf_op jit(solution)/shard_map/wu,uij->wij/dot_general | solution.py:242
  48.6 0.0 collective-permute-done.4
  48.6 3.3 %collective-permute-start.5 = (f32[8,128]{1,0:T(8,128)S(1)}, f32[8,128]{1,0:T(8,128)S(1)}, u32[]{:S(2)}, u32[]{:S(2)}) collective-permute-start(f32[8,128]{1,0:T(8,128)S(1)} %add.32), channel_id=1, source_target_pairs={{0,8},{1,9},{2,10},{3,11},{4,12},{5,13},{6,14},{7,15},{8,0},{9,1},... | collective-permute-start | bytes 12296 | tf_op jit(solution)/shard_map/ppermute | solution.py:33
  51.8 4.8 %convert_bitcast_fusion = bf16[20,256,256]{2,0,1:T(8,128)(2,1)} fusion(bf16[20,256,256]{2,1,0:T(8,128)(2,1)S(1)} %collective-permute-done.2, f32[20,20]{1,0:T(8,128)S(1)} %copy-done), kind=kOutput, calls=%fused_computation.4 | convolution fusion | flops 315883520 | bytes 5244480 | tf_op jit(solution)/shard_map/wu,uij->wij/dot_general | solution.py:242
  56.6 0.0 collective-permute-done.5
  56.6 4.5 %collective-permute-start.6 = (f32[8,128]{1,0:T(8,128)S(1)}, f32[8,128]{1,0:T(8,128)S(1)}, u32[]{:S(2)}, u32[]{:S(2)}) collective-permute-start(f32[8,128]{1,0:T(8,128)S(1)} %add.33), channel_id=1, source_target_pairs={{0,16},{1,17},{2,18},{3,19},{4,20},{5,21},{6,22},{7,23},{8,24},{9,... | collective-permute-start | bytes 12296 | tf_op jit(solution)/shard_map/ppermute | solution.py:33
  61.8 2.4 %collective-permute-done.6 = f32[8,128]{1,0:T(8,128)S(1)} collective-permute-done((f32[8,128]{1,0:T(8,128)S(1)}, f32[8,128]{1,0:T(8,128)S(1)}, u32[]{:S(2)}, u32[]{:S(2)}) %collective-permute-start.6) | collective-permute-done | bytes 4128 | tf_op jit(solution)/shard_map/ppermute | solution.py:33
  64.2 0.6 add.34.total_ref
  64.8 2.5 %shard_map.78 = (f32[256,256]{1,0:T(8,128)}, bf16[256,128]{1,0:T(8,128)(2,1)}, bf16[128,256]{1,0:T(8,128)(2,1)}) custom-call(f32[8,128]{1,0:T(8,128)} %add.34.total_ref, f32[256,256]{1,0:T(8,128)} %get-tuple-element.27.head_ref.refs_0_.refs_1_, s32[1,1]{1,0:T(1,128)S(6)} %copy.61.refs_0_, f32[256,256]{1,0:T(8,128)} %get-tuple-element.27.head_ref.refs_0_.refs_1_, ...), custom_call_target="tpu_custom_call" | custom-call | tf_op jit(solution)/shard_map/pallas_call | solution.py:210
  67.2 0.0 collective-permute-start.8
  67.2 0.5 collective-permute-start.7
  67.7 1.0 multiply_multiply_fusion.head_ref
  68.8 0.0 copy-start.1
  68.8 0.7 slice.8.refs_0_
  69.5 0.0 collective-permute-done.8
  69.5 3.2 %fusion.50 = bf16[20,128,128]{1,2,0:T(8,128)(2,1)S(1)} fusion(bf16[20,256,256]{2,0,1:T(8,128)(2,1)} %convert_bitcast_fusion, bf16[128,256]{1,0:T(8,128)(2,1)S(1)} %collective-permute-done.8), kind=kOutput, calls=%fused_computation.36 | convolution fusion | flops 504299520 | bytes 3342336 | tf_op jit(solution)/shard_map/ji,wjk->wik/dot_general | solution.py:223
  72.7 0.0 collective-permute-done.7
  72.7 3.2 %fusion.53 = bf16[20,128,128]{1,2,0:T(8,128)(2,1)S(1)} fusion(bf16[20,256,256]{2,0,1:T(8,128)(2,1)} %convert_bitcast_fusion.1, bf16[256,128]{1,0:T(8,128)(2,1)S(1)} %collective-permute-done.7), kind=kOutput, calls=%fused_computation.37 | convolution fusion | flops 504299520 | bytes 3342336 | tf_op jit(solution)/shard_map/ji,wjk->wik/dot_general | solution.py:223
  76.0 0.0 copy-done.1
  76.0 0.5 fusion.95.refs_1_
  76.5 0.0 copy-start.4
  76.5 0.5 fusion.94.refs_2_
  77.0 0.0 copy-start.5
  77.0 0.5 fusion.93.refs_3_
  77.5 0.0 copy-start.6
  77.6 1.2 %fusion.92.refs_4_ = f32[128,128]{1,0:T(8,128)} fusion(bf16[20,128,128]{1,2,0:T(8,128)(2,1)S(1)} %fusion.53, bf16[20,128,128]{1,2,0:T(8,128)(2,1)S(1)} %fusion.50, f32[256,256]{1,0:T(8,128)S(1)} %get-tuple-element.26, f32[128,128]{1,0:T(8,128)S(1)} %fusion.93.refs_3_), kind=kOutput, calls=%fused_computation.58 | convolution fusion | flops 168148992 | bytes 1572864 | tf_op jit(solution)/shard_map/wij,wjk->ik/dot_general | solution.py:45
  78.7 0.0 copy-done.4
  78.7 0.0 copy-done.5
  78.7 1.9 %shard_map.79 = f32[8,128]{1,0:T(8,128)} custom-call(f32[256,256]{1,0:T(8,128)} %copy-done.1, f32[128,128]{1,0:T(8,128)} %slice.8.refs_0_, f32[128,128]{1,0:T(8,128)} %copy-done.4, f32[128,128]{1,0:T(8,128)} %copy-done.5, f32[128,128]{1,0:T(8,128)} %copy-done.6, f32[128,128]{1,0:T(8,128)} %fusion.92.refs_4_), custom_call_target="tpu_custom_call" | custom-call | tf_op jit(solution)/shard_map/pallas_call | solution.py:190
  80.6 1.3 %collective-permute-start.9 = (f32[8,128]{1,0:T(8,128)}, f32[8,128]{1,0:T(8,128)S(1)}, u32[]{:S(2)}, u32[]{:S(2)}) collective-permute-start(f32[8,128]{1,0:T(8,128)} %shard_map.79), channel_id=1, source_target_pairs={{0,1},{1,0},{2,3},{3,2},{4,5},{5,4},{6,7},{7,6},{8,9},{9,8},{10,11... | collective-permute-start | bytes 12296 | tf_op jit(solution)/shard_map/ppermute | solution.py:33
  81.9 2.5 %collective-permute-done.9 = f32[8,128]{1,0:T(8,128)S(1)} collective-permute-done((f32[8,128]{1,0:T(8,128)}, f32[8,128]{1,0:T(8,128)S(1)}, u32[]{:S(2)}, u32[]{:S(2)}) %collective-permute-start.9) | collective-permute-done | bytes 4128 | tf_op jit(solution)/shard_map/ppermute | solution.py:33
  84.4 0.7 add.35
  85.1 0.3 collective-permute-start.10
  85.4 4.8 %collective-permute-done.10 = f32[8,128]{1,0:T(8,128)S(1)} collective-permute-done((f32[8,128]{1,0:T(8,128)S(1)}, f32[8,128]{1,0:T(8,128)S(1)}, u32[]{:S(2)}, u32[]{:S(2)}) %collective-permute-start.10) | collective-permute-done | bytes 4128 | tf_op jit(solution)/shard_map/ppermute | solution.py:33
  90.2 0.1 collective-permute-start.11
  90.3 3.5 %collective-permute-done.11 = f32[8,128]{1,0:T(8,128)S(1)} collective-permute-done((f32[8,128]{1,0:T(8,128)S(1)}, f32[8,128]{1,0:T(8,128)S(1)}, u32[]{:S(2)}, u32[]{:S(2)}) %collective-permute-start.11) | collective-permute-done | bytes 4128 | tf_op jit(solution)/shard_map/ppermute | solution.py:33
  93.8 0.0 collective-permute-start.12
  93.8 4.5 %collective-permute-done.12 = f32[8,128]{1,0:T(8,128)S(1)} collective-permute-done((f32[8,128]{1,0:T(8,128)S(1)}, f32[8,128]{1,0:T(8,128)S(1)}, u32[]{:S(2)}, u32[]{:S(2)}) %collective-permute-start.12) | collective-permute-done | bytes 4128 | tf_op jit(solution)/shard_map/ppermute | solution.py:33
  98.3 4.5 %collective-permute-start.13 = (f32[8,128]{1,0:T(8,128)S(1)}, f32[8,128]{1,0:T(8,128)S(1)}, u32[]{:S(2)}, u32[]{:S(2)}) collective-permute-start(f32[8,128]{1,0:T(8,128)S(1)} %add.38), channel_id=1, source_target_pairs={{0,16},{1,17},{2,18},{3,19},{4,20},{5,21},{6,22},{7,23},{8,24},{9,... | collective-permute-start | bytes 12296 | tf_op jit(solution)/shard_map/ppermute | solution.py:33
  102.8 3.0 %collective-permute-done.13 = f32[8,128]{1,0:T(8,128)S(1)} collective-permute-done((f32[8,128]{1,0:T(8,128)S(1)}, f32[8,128]{1,0:T(8,128)S(1)}, u32[]{:S(2)}, u32[]{:S(2)}) %collective-permute-start.13) | collective-permute-done | bytes 4128 | tf_op jit(solution)/shard_map/ppermute | solution.py:33
  105.8 0.6 add.39.total_ref
  106.4 2.1 %shard_map.80 = (f32[256,256]{1,0:T(8,128)}, f32[1,1]{1,0:T(1,128)}) custom-call(f32[8,128]{1,0:T(8,128)} %add.39.total_ref, f32[256,256]{1,0:T(8,128)} %copy-done.1, f32[128,128]{1,0:T(8,128)} %slice.8.refs_0_, f32[128,128]{1,0:T(8,128)} %copy-done.4, f32[128,128]{1,0:T(8,128)} %copy-done.5, f32[128,128]{1,0:T(8,128)} %copy-done.6), custom_call_target="tpu_custom_call" | custom-call | tf_op jit(solution)/shard_map/pallas_call | solution.py:210
  (8 shorter events, 0.0 us)
Async XLA Ops:
  0.6 41.1 %copy-start = (f32[20,20]{1,0:T(8,128)S(1)}, f32[20,20]{1,0:T(8,128)}, u32[]{:S(2)}) copy-start(f32[20,20]{1,0:T(8,128)} %param.9) | copy-start | bytes 4804
  0.6 34.0 %collective-permute-start.1 = (bf16[20,256,256]{2,1,0:T(8,128)(2,1)}, bf16[20,256,256]{2,1,0:T(8,128)(2,1)}, u32[]{:S(2)}, u32[]{:S(2)}) collective-permute-start(bf16[20,256,256]{2,1,0:T(8,128)(2,1)} %bitcast.191), channel_id=1, source_target_pairs={{0,32},{32,64},{64,96},{96,128},{128,160},{160,192},{192,224},{224... | collective-permute-start | bytes 7864328 | tf_op jit(solution)/shard_map/ppermute | solution.py:18
  0.7 34.0 %collective-permute-start.2 = (bf16[20,256,256]{2,1,0:T(8,128)(2,1)}, bf16[20,256,256]{2,1,0:T(8,128)(2,1)S(1)}, u32[]{:S(2)}, u32[]{:S(2)}) collective-permute-start(bf16[20,256,256]{2,1,0:T(8,128)(2,1)} %bitcast.192), channel_id=1, source_target_pairs={{0,224},{32,0},{64,32},{96,64},{128,96},{160,128},{192,160},{224,1... | collective-permute-start | bytes 7864328 | tf_op jit(solution)/shard_map/ppermute | solution.py:18
  11.1 5.1 %copy-start.2 = (f32[256,256]{1,0:T(8,128)}, f32[256,256]{1,0:T(8,128)S(1)}, u32[]{:S(2)}) copy-start(f32[256,256]{1,0:T(8,128)S(1)} %fusion.67.refs_1_.refs_2_) | copy-start | bytes 786436
  16.2 5.8 %copy-start.3 = (f32[256,256]{1,0:T(8,128)}, f32[256,256]{1,0:T(8,128)S(1)}, u32[]{:S(2)}) copy-start(f32[256,256]{1,0:T(8,128)S(1)} %fusion.73.refs_2_.refs_3_) | copy-start | bytes 786436
  30.2 3.8 %collective-permute-start = (f32[8,128]{1,0:T(8,128)}, f32[8,128]{1,0:T(8,128)S(1)}, u32[]{:S(2)}, u32[]{:S(2)}) collective-permute-start(f32[8,128]{1,0:T(8,128)} %shard_map.77), channel_id=1, source_target_pairs={{0,1},{1,0},{2,3},{3,2},{4,5},{5,4},{6,7},{7,6},{8,9},{9,8},{10,11... | collective-permute-start | bytes 12296 | tf_op jit(solution)/shard_map/ppermute | solution.py:33
  34.7 5.1 %collective-permute-start.3 = (f32[8,128]{1,0:T(8,128)S(1)}, f32[8,128]{1,0:T(8,128)S(1)}, u32[]{:S(2)}, u32[]{:S(2)}) collective-permute-start(f32[8,128]{1,0:T(8,128)S(1)} %add.30), channel_id=1, source_target_pairs={{0,2},{1,3},{2,0},{3,1},{4,6},{5,7},{6,4},{7,5},{8,10},{9,11},{10,... | collective-permute-start | bytes 12296 | tf_op jit(solution)/shard_map/ppermute | solution.py:33
  39.8 8.8 %collective-permute-start.4 = (f32[8,128]{1,0:T(8,128)S(1)}, f32[8,128]{1,0:T(8,128)S(1)}, u32[]{:S(2)}, u32[]{:S(2)}) collective-permute-start(f32[8,128]{1,0:T(8,128)S(1)} %add.31), channel_id=1, source_target_pairs={{0,4},{1,5},{2,6},{3,7},{4,0},{5,1},{6,2},{7,3},{8,12},{9,13},{10,... | collective-permute-start | bytes 12296 | tf_op jit(solution)/shard_map/ppermute | solution.py:33
  48.6 8.1 %collective-permute-start.5 = (f32[8,128]{1,0:T(8,128)S(1)}, f32[8,128]{1,0:T(8,128)S(1)}, u32[]{:S(2)}, u32[]{:S(2)}) collective-permute-start(f32[8,128]{1,0:T(8,128)S(1)} %add.32), channel_id=1, source_target_pairs={{0,8},{1,9},{2,10},{3,11},{4,12},{5,13},{6,14},{7,15},{8,0},{9,1},... | collective-permute-start | bytes 12296 | tf_op jit(solution)/shard_map/ppermute | solution.py:33
  56.6 7.5 %collective-permute-start.6 = (f32[8,128]{1,0:T(8,128)S(1)}, f32[8,128]{1,0:T(8,128)S(1)}, u32[]{:S(2)}, u32[]{:S(2)}) collective-permute-start(f32[8,128]{1,0:T(8,128)S(1)} %add.33), channel_id=1, source_target_pairs={{0,16},{1,17},{2,18},{3,19},{4,20},{5,21},{6,22},{7,23},{8,24},{9,... | collective-permute-start | bytes 12296 | tf_op jit(solution)/shard_map/ppermute | solution.py:33
  67.2 2.2 %collective-permute-start.8 = (bf16[128,256]{1,0:T(8,128)(2,1)}, bf16[128,256]{1,0:T(8,128)(2,1)S(1)}, u32[]{:S(2)}, u32[]{:S(2)}) collective-permute-start(bf16[128,256]{1,0:T(8,128)(2,1)} %get-tuple-element.23), channel_id=1, source_target_pairs={{0,224},{32,0},{64,32},{96,64},{128,96},{160,128},{192,160},{224,1... | collective-permute-start | bytes 196616 | tf_op jit(solution)/shard_map/ppermute | solution.py:18
  67.2 5.5 %collective-permute-start.7 = (bf16[256,128]{1,0:T(8,128)(2,1)}, bf16[256,128]{1,0:T(8,128)(2,1)S(1)}, u32[]{:S(2)}, u32[]{:S(2)}) collective-permute-start(bf16[256,128]{1,0:T(8,128)(2,1)} %get-tuple-element.21), channel_id=1, source_target_pairs={{0,32},{32,64},{64,96},{96,128},{128,160},{160,192},{192,224},{224... | collective-permute-start | bytes 196616 | tf_op jit(solution)/shard_map/ppermute | solution.py:18
  68.8 7.2 %copy-start.1 = (f32[256,256]{1,0:T(8,128)}, f32[256,256]{1,0:T(8,128)S(1)}, u32[]{:S(2)}) copy-start(f32[256,256]{1,0:T(8,128)S(1)} %multiply_multiply_fusion.head_ref) | copy-start | bytes 786436
  76.5 2.2 %copy-start.4 = (f32[128,128]{1,0:T(8,128)}, f32[128,128]{1,0:T(8,128)S(1)}, u32[]{:S(2)}) copy-start(f32[128,128]{1,0:T(8,128)S(1)} %fusion.95.refs_1_) | copy-start | bytes 196612
  77.0 1.7 %copy-start.5 = (f32[128,128]{1,0:T(8,128)}, f32[128,128]{1,0:T(8,128)S(1)}, u32[]{:S(2)}) copy-start(f32[128,128]{1,0:T(8,128)S(1)} %fusion.94.refs_2_) | copy-start | bytes 196612
  77.5 1.2 %copy-start.6 = (f32[128,128]{1,0:T(8,128)}, f32[128,128]{1,0:T(8,128)S(1)}, u32[]{:S(2)}) copy-start(f32[128,128]{1,0:T(8,128)S(1)} %fusion.93.refs_3_) | copy-start | bytes 196612
  80.6 3.8 %collective-permute-start.9 = (f32[8,128]{1,0:T(8,128)}, f32[8,128]{1,0:T(8,128)S(1)}, u32[]{:S(2)}, u32[]{:S(2)}) collective-permute-start(f32[8,128]{1,0:T(8,128)} %shard_map.79), channel_id=1, source_target_pairs={{0,1},{1,0},{2,3},{3,2},{4,5},{5,4},{6,7},{7,6},{8,9},{9,8},{10,11... | collective-permute-start | bytes 12296 | tf_op jit(solution)/shard_map/ppermute | solution.py:33
  85.1 5.1 %collective-permute-start.10 = (f32[8,128]{1,0:T(8,128)S(1)}, f32[8,128]{1,0:T(8,128)S(1)}, u32[]{:S(2)}, u32[]{:S(2)}) collective-permute-start(f32[8,128]{1,0:T(8,128)S(1)} %add.35), channel_id=1, source_target_pairs={{0,2},{1,3},{2,0},{3,1},{4,6},{5,7},{6,4},{7,5},{8,10},{9,11},{10,... | collective-permute-start | bytes 12296 | tf_op jit(solution)/shard_map/ppermute | solution.py:33
  90.2 3.6 %collective-permute-start.11 = (f32[8,128]{1,0:T(8,128)S(1)}, f32[8,128]{1,0:T(8,128)S(1)}, u32[]{:S(2)}, u32[]{:S(2)}) collective-permute-start(f32[8,128]{1,0:T(8,128)S(1)} %add.36), channel_id=1, source_target_pairs={{0,4},{1,5},{2,6},{3,7},{4,0},{5,1},{6,2},{7,3},{8,12},{9,13},{10,... | collective-permute-start | bytes 12296 | tf_op jit(solution)/shard_map/ppermute | solution.py:33
  93.8 4.5 %collective-permute-start.12 = (f32[8,128]{1,0:T(8,128)S(1)}, f32[8,128]{1,0:T(8,128)S(1)}, u32[]{:S(2)}, u32[]{:S(2)}) collective-permute-start(f32[8,128]{1,0:T(8,128)S(1)} %add.37), channel_id=1, source_target_pairs={{0,8},{1,9},{2,10},{3,11},{4,12},{5,13},{6,14},{7,15},{8,0},{9,1},... | collective-permute-start | bytes 12296 | tf_op jit(solution)/shard_map/ppermute | solution.py:33
  98.3 7.5 %collective-permute-start.13 = (f32[8,128]{1,0:T(8,128)S(1)}, f32[8,128]{1,0:T(8,128)S(1)}, u32[]{:S(2)}, u32[]{:S(2)}) collective-permute-start(f32[8,128]{1,0:T(8,128)S(1)} %add.38), channel_id=1, source_target_pairs={{0,16},{1,17},{2,18},{3,19},{4,20},{5,21},{6,22},{7,23},{8,24},{9,... | collective-permute-start | bytes 12296 | tf_op jit(solution)/shard_map/ppermute | solution.py:33

commit v6 on v5

--- a/solution.py
+++ b/solution.py
@@ -46,9 +46,12 @@
     return outer * mask
 
 
-def gram_kernel(head_ref, *refs):
-    *vec_refs, out_ref = refs
-    size = len(vec_refs)
+def gram_kernel(start_ref, mask_ref, *refs):
+    *later_refs, out_ref = refs
+    head = start_ref[...] * mask_ref[...]
+    n = later_refs[0].shape[-1]
+    vecs = [lambda: head[:n, :n]] + [lambda ref=ref: ref[...] for ref in later_refs]
+    size = len(vecs)
     row = lax.broadcasted_iota(jnp.int32, out_ref.shape, 0)
     lane = lax.broadcasted_iota(jnp.int32, out_ref.shape, 1)
     out = jnp.zeros(out_ref.shape, jnp.float32)
@@ -56,10 +59,9 @@
     for i in range(size):
         for j in range(i, size):
             if i == 0 and j == 0:
-                head = head_ref[...]
                 total = jnp.sum(head * head, axis=(0, 1), keepdims=True)
             else:
-                total = jnp.sum(vec_refs[i][...] * vec_refs[j][...], axis=(0, 1), keepdims=True)
+                total = jnp.sum(vecs[i]() * vecs[j](), axis=(0, 1), keepdims=True)
             out = jnp.where((row == 0) & (lane == slot), total, out)
             slot += 1
     out_ref[...] = out
@@ -146,21 +148,22 @@
     return coef, energy
 
 
-def finish_kernel(total_ref, head_ref, *refs, scale, cut, rank_scale):
+def finish_kernel(total_ref, start_ref, mask_ref, *refs, scale, cut, rank_scale):
     if rank_scale is None:
-        *vec_refs, out_ref, energy_ref = refs
-    else:
-        rank_ref, *vec_refs, out_ref, left_ref, right_ref = refs
+        *later_refs, out_ref, energy_ref = refs
+    else:
+        rank_ref, *later_refs, out_ref, left_ref, right_ref = refs
     coef, energy = ritz_coefficients(total_ref, (8, 128))
     coef = [c[:1, :1] for c in coef]
-    rows, cols = vec_refs[0].shape
-    acc = vec_refs[0][...] * coef[0]
-    for step in range(1, len(vec_refs)):
-        acc = acc + coef[step] * vec_refs[step][...]
+    head = start_ref[...] * mask_ref[...]
+    rows, cols = later_refs[0].shape
+    acc = head[:rows, :cols] * coef[0]
+    for step in range(1, LANCZOS):
+        acc = acc + coef[step] * later_refs[step - 1][...]
     if scale is not None:
         acc = acc * scale
-    if head_ref.shape != vec_refs[0].shape:
-        rest = head_ref[...] * coef[0]
+    if head.shape != (rows, cols):
+        rest = head * coef[0]
         if scale is not None:
             rest = rest * scale
         out_ref[...] = rest
@@ -187,19 +190,19 @@
     for step in range(LANCZOS):
         krylov.append(apply_ham(krylov[-1], left, right, live))
     tile = jax.ShapeDtypeStruct((8, 128), jnp.float32)
-    local = pl.pallas_call(gram_kernel, out_shape=tile)(head, *krylov)
+    local = pl.pallas_call(gram_kernel, out_shape=tile)(start, mask, *krylov[1:])
     total = bond_sum(local, hooks)
     smem = pl.BlockSpec(memory_space=pltpu.SMEM)
     vmem = pl.BlockSpec(memory_space=pltpu.VMEM)
     width = head.shape[-1]
     field = jax.ShapeDtypeStruct(head.shape, jnp.float32)
     if rank is None:
-        in_specs = [smem, vmem] + [vmem] * LANCZOS
+        in_specs = [smem, vmem, vmem] + [vmem] * (LANCZOS - 1)
         out_shape = (field, jax.ShapeDtypeStruct((1, 1), jnp.float32))
         extra = ()
         rank_scale = None
     else:
-        in_specs = [smem, vmem, smem] + [vmem] * LANCZOS
+        in_specs = [smem, vmem, vmem, smem] + [vmem] * (LANCZOS - 1)
         out_shape = (
             field,
             jax.ShapeDtypeStruct((width, width // 2), jnp.bfloat16),
@@ -213,7 +216,7 @@
         ),
         out_shape=out_shape,
         in_specs=in_specs,
-    )(total, head, *extra, *krylov[:LANCZOS])
+    )(total, start, mask, *extra, *krylov[1:LANCZOS])
 
 
 def env_update(mixed, left_a):

time: 109 us -> 108 us (level)
  other arithmetic: 5.39 us -> 3.4 us
  waiting for transfers between devices: 26.3 us -> 27.7 us
    ppermute x4, waiting for transfers between devices: 0.01 us -> 1.87 us  [shifted(): return lax.ppermute(value, axis, pairs)]
  transfers between devices with their start and end apart: 14 -> 14, of which waited for: 8 -> 10; matrix products, arithmetic and copies ran while one was open for 37% -> 35% of each run, Pallas kernels for 2% -> 2%
where the time goes in v6:
time: 108 us
  matrix products  42.7 us (40%)
  waiting for transfers between devices  27.7 us (26%)
  starting transfers between devices  23.2 us (21%)
  Pallas kernels  8.93 us (8%)
  other arithmetic  3.4 us (3%)
  between operations  2.12 us (2%)
    ppermute x10, waiting for transfers between devices, bond_sum(): value = value + lax.ppermute(value, 'bond', pairs)  25.8 us
    dot_general x8, matrix products, apply_ham(): jnp.einsum('wij,wjk->ik', left, inner, preferred_element_type=jnp.float32)  24.6 us
    ppermute x10, starting transfers between devices, bond_sum(): value = value + lax.ppermute(value, 'bond', pairs)  19.7 us
    dot_general x2, matrix products, mixed(): jnp.einsum('wu,uij->wij', mpo_mix, env.astype(jnp.float32), precision=lax...  11.6 us
    dot_general x2, matrix products, env_update(): jnp.einsum('ji,wjk->wik', left_a, half_left, preferred_element_type=jnp.f...  6.53 us
    pallas_call x2, Pallas kernels, lanczos(): pl.pallas_call(functools.partial(finish_kernel, scale=scale, cut=width //...  4.62 us
    pallas_call x2, Pallas kernels, lanczos(): pl.pallas_call(gram_kernel, out_shape=tile)(start, mask, *krylov[1:])  4.31 us
    ppermute x4, starting transfers between devices, shifted(): return lax.ppermute(value, axis, pairs)  3.47 us
  transfers between devices with their start and end apart: 14, of which 10 were waited for; matrix products, arithmetic and copies ran while one was open for 35% of the time, Pallas kernels for 2%

profile of v6, /device:TPU:16, one launch (start us, length us, event | category | flops | bytes accessed | tf_op | source)
XLA Modules:
  0.0 108.1 jit_solution(3195467650192544055)
XLA Ops:
  0.6 0.0 copy-start
  0.6 0.0 collective-permute-start.1
  0.7 2.9 %collective-permute-start.2 = (bf16[20,256,256]{2,1,0:T(8,128)(2,1)}, bf16[20,256,256]{2,1,0:T(8,128)(2,1)S(1)}, u32[]{:S(2)}, u32[]{:S(2)}) collective-permute-start(bf16[20,256,256]{2,1,0:T(8,128)(2,1)} %bitcast.193), channel_id=1, source_target_pairs={{0,224},{32,0},{64,32},{96,64},{128,96},{160,128},{192,160},{224,1... | collective-permute-start | bytes 7864328 | tf_op jit(solution)/shard_map/ppermute | solution.py:18
  4.3 0.8 broadcast_multiply_fusion.mask_ref
  5.1 5.1 %fusion.67.refs_0_.refs_1_ = f32[256,256]{1,0:T(8,128)S(1)} fusion(f32[1,1,256,256]{3,2,1,0:T(8,128)} %param.6, f32[256]{0:T(256)S(1)} %compare_convert_fusion, bf16[1,1,20,256,256]{4,3,2,1,0:T(8,128)(2,1)} %param.7, bf16[1,1,20,256,256]{4,3,2,1,0:T(8,128)(2,1)} %param.8), kind=kOutput, calls=%fused_computation.47 | convolution fusion | flops 1343881216 | bytes 5768192 | tf_op jit(solution)/shard_map/wij,wjk->ik/dot_general | solution.py:45
  10.2 0.0 copy-start.2
  10.2 5.1 %fusion.73.refs_1_.refs_2_ = f32[256,256]{1,0:T(8,128)S(1)} fusion(f32[256,256]{1,0:T(8,128)S(1)} %fusion.67.refs_0_.refs_1_, f32[256]{0:T(256)S(1)} %compare_convert_fusion, bf16[1,1,20,256,256]{4,3,2,1,0:T(8,128)(2,1)} %param.7, bf16[1,1,20,256,256]{4,3,2,1,0:T(8,128)(2,1)} %param.8), kind=kOutput, calls=%fused_computation.49 | convolution fusion | flops 1343815680 | bytes 5768192 | tf_op jit(solution)/shard_map/wij,wjk->ik/dot_general | solution.py:45
  15.3 0.0 copy-done.2
  15.3 0.0 copy-start.3
  15.3 5.1 %fusion.79.refs_2_.refs_3_ = f32[256,256]{1,0:T(8,128)S(1)} fusion(f32[256,256]{1,0:T(8,128)S(1)} %fusion.73.refs_1_.refs_2_, f32[256]{0:T(256)S(1)} %compare_convert_fusion, bf16[1,1,20,256,256]{4,3,2,1,0:T(8,128)(2,1)} %param.7, bf16[1,1,20,256,256]{4,3,2,1,0:T(8,128)(2,1)} %param.8), kind=kOutput, calls=%fused_computation.51 | convolution fusion | flops 1343815680 | bytes 5768192 | tf_op jit(solution)/shard_map/wij,wjk->ik/dot_general | solution.py:45
  20.4 0.0 copy-done.3
  20.4 0.0 copy-start.4
  20.4 5.8 %fusion.85.refs_3_ = f32[256,256]{1,0:T(8,128)} fusion(f32[256,256]{1,0:T(8,128)S(1)} %fusion.79.refs_2_.refs_3_, f32[256]{0:T(256)S(1)} %compare_convert_fusion, bf16[1,1,20,256,256]{4,3,2,1,0:T(8,128)(2,1)} %param.7, bf16[1,1,20,256,256]{4,3,2,1,0:T(8,128)(2,1)} %param.8), kind=kOutput, calls=%fused_computation.53 | convolution fusion | flops 1343815680 | bytes 5768192 | tf_op jit(solution)/shard_map/wij,wjk->ik/dot_general | solution.py:45
  26.2 0.0 copy-done.4
  26.2 2.4 %shard_map.77 = f32[8,128]{1,0:T(8,128)} custom-call(f32[256,256]{1,0:T(8,128)} %bitcast.190, f32[256,256]{1,0:T(8,128)} %broadcast_multiply_fusion.mask_ref, f32[256,256]{1,0:T(8,128)} %copy-done.2, f32[256,256]{1,0:T(8,128)} %copy-done.3, f32[256,256]{1,0:T(8,128)} %copy-done.4, f32[256,256]{1,0:T(8,128)} %fusion.85.refs_3_), custom_call_target="tpu_custom_call" | custom-call | tf_op jit(solution)/shard_map/pallas_call | solution.py:193
  28.6 1.3 %collective-permute-start = (f32[8,128]{1,0:T(8,128)}, f32[8,128]{1,0:T(8,128)S(1)}, u32[]{:S(2)}, u32[]{:S(2)}) collective-permute-start(f32[8,128]{1,0:T(8,128)} %shard_map.77), channel_id=1, source_target_pairs={{0,1},{1,0},{2,3},{3,2},{4,5},{5,4},{6,7},{7,6},{8,9},{9,8},{10,11... | collective-permute-start | bytes 12296 | tf_op jit(solution)/shard_map/ppermute | solution.py:33
  29.9 2.5 %collective-permute-done = f32[8,128]{1,0:T(8,128)S(1)} collective-permute-done((f32[8,128]{1,0:T(8,128)}, f32[8,128]{1,0:T(8,128)S(1)}, u32[]{:S(2)}, u32[]{:S(2)}) %collective-permute-start) | collective-permute-done | bytes 4128 | tf_op jit(solution)/shard_map/ppermute | solution.py:33
  32.4 0.7 add.30
  33.1 0.2 collective-permute-done.1
  33.3 0.0 collective-permute-done.2
  33.3 2.1 %collective-permute-start.3 = (f32[8,128]{1,0:T(8,128)S(1)}, f32[8,128]{1,0:T(8,128)S(1)}, u32[]{:S(2)}, u32[]{:S(2)}) collective-permute-start(f32[8,128]{1,0:T(8,128)S(1)} %add.30), channel_id=1, source_target_pairs={{0,2},{1,3},{2,0},{3,1},{4,6},{5,7},{6,4},{7,5},{8,10},{9,11},{10,... | collective-permute-start | bytes 12296 | tf_op jit(solution)/shard_map/ppermute | solution.py:33
  35.3 3.0 %collective-permute-done.3 = f32[8,128]{1,0:T(8,128)S(1)} collective-permute-done((f32[8,128]{1,0:T(8,128)S(1)}, f32[8,128]{1,0:T(8,128)S(1)}, u32[]{:S(2)}, u32[]{:S(2)}) %collective-permute-start.3) | collective-permute-done | bytes 4128 | tf_op jit(solution)/shard_map/ppermute | solution.py:33
  38.4 1.9 %collective-permute-start.4 = (f32[8,128]{1,0:T(8,128)S(1)}, f32[8,128]{1,0:T(8,128)S(1)}, u32[]{:S(2)}, u32[]{:S(2)}) collective-permute-start(f32[8,128]{1,0:T(8,128)S(1)} %add.31), channel_id=1, source_target_pairs={{0,4},{1,5},{2,6},{3,7},{4,0},{5,1},{6,2},{7,3},{8,12},{9,13},{10,... | collective-permute-start | bytes 12296 | tf_op jit(solution)/shard_map/ppermute | solution.py:33
  40.3 0.0 copy-done
  40.3 6.8 %convert_bitcast_fusion.1 = bf16[20,256,256]{2,0,1:T(8,128)(2,1)} fusion(bf16[20,256,256]{2,1,0:T(8,128)(2,1)} %collective-permute-done.1, f32[20,20]{1,0:T(8,128)S(1)} %copy-done), kind=kOutput, calls=%fused_computation.5 | convolution fusion | flops 315883520 | bytes 5244480 | tf_op jit(solution)/shard_map/wu,uij->wij/dot_general | solution.py:245
  47.1 0.0 collective-permute-done.4
  47.1 3.3 %collective-permute-start.5 = (f32[8,128]{1,0:T(8,128)S(1)}, f32[8,128]{1,0:T(8,128)S(1)}, u32[]{:S(2)}, u32[]{:S(2)}) collective-permute-start(f32[8,128]{1,0:T(8,128)S(1)} %add.32), channel_id=1, source_target_pairs={{0,8},{1,9},{2,10},{3,11},{4,12},{5,13},{6,14},{7,15},{8,0},{9,1},... | collective-permute-start | bytes 12296 | tf_op jit(solution)/shard_map/ppermute | solution.py:33
  50.4 4.8 %convert_bitcast_fusion = bf16[20,256,256]{2,0,1:T(8,128)(2,1)} fusion(bf16[20,256,256]{2,1,0:T(8,128)(2,1)S(1)} %collective-permute-done.2, f32[20,20]{1,0:T(8,128)S(1)} %copy-done), kind=kOutput, calls=%fused_computation.4 | convolution fusion | flops 315883520 | bytes 5244480 | tf_op jit(solution)/shard_map/wu,uij->wij/dot_general | solution.py:245
  55.2 0.0 collective-permute-done.5
  55.2 4.5 %collective-permute-start.6 = (f32[8,128]{1,0:T(8,128)S(1)}, f32[8,128]{1,0:T(8,128)S(1)}, u32[]{:S(2)}, u32[]{:S(2)}) collective-permute-start(f32[8,128]{1,0:T(8,128)S(1)} %add.33), channel_id=1, source_target_pairs={{0,16},{1,17},{2,18},{3,19},{4,20},{5,21},{6,22},{7,23},{8,24},{9,... | collective-permute-start | bytes 12296 | tf_op jit(solution)/shard_map/ppermute | solution.py:33
  60.4 2.4 %collective-permute-done.6 = f32[8,128]{1,0:T(8,128)S(1)} collective-permute-done((f32[8,128]{1,0:T(8,128)S(1)}, f32[8,128]{1,0:T(8,128)S(1)}, u32[]{:S(2)}, u32[]{:S(2)}) %collective-permute-start.6) | collective-permute-done | bytes 4128 | tf_op jit(solution)/shard_map/ppermute | solution.py:33
  62.7 0.6 add.34.total_ref
  63.3 2.5 %shard_map.78 = (f32[256,256]{1,0:T(8,128)}, bf16[256,128]{1,0:T(8,128)(2,1)}, bf16[128,256]{1,0:T(8,128)(2,1)}) custom-call(f32[8,128]{1,0:T(8,128)} %add.34.total_ref, f32[256,256]{1,0:T(8,128)} %bitcast.191, f32[256,256]{1,0:T(8,128)} %broadcast_multiply_fusion.mask_ref, s32[1,1]{1,0:T(1,128)S(6)} %copy.61.refs_0_, f32[256,256]{1,0:T(8,128)} %copy-done.2, ...), custom_call_target="tpu_custom_call" | custom-call | tf_op jit(solution)/shard_map/pallas_call | solution.py:213
  65.8 0.0 collective-permute-start.8
  65.8 0.5 collective-permute-start.7
  66.3 1.7 %collective-permute-done.8 = bf16[128,256]{1,0:T(8,128)(2,1)S(1)} collective-permute-done((bf16[128,256]{1,0:T(8,128)(2,1)}, bf16[128,256]{1,0:T(8,128)(2,1)S(1)}, u32[]{:S(2)}, u32[]{:S(2)}) %collective-permute-start.8) | collective-permute-done | bytes 65568 | tf_op jit(solution)/shard_map/ppermute | solution.py:18
  68.0 3.2 %fusion.50 = bf16[20,128,128]{1,2,0:T(8,128)(2,1)S(1)} fusion(bf16[20,256,256]{2,0,1:T(8,128)(2,1)} %convert_bitcast_fusion, bf16[128,256]{1,0:T(8,128)(2,1)S(1)} %collective-permute-done.8), kind=kOutput, calls=%fused_computation.36 | convolution fusion | flops 504299520 | bytes 3342336 | tf_op jit(solution)/shard_map/ji,wjk->wik/dot_general | solution.py:226
  71.3 0.0 copy-start.1
  71.3 0.0 collective-permute-done.7
  71.3 3.3 %fusion.53 = bf16[20,128,128]{1,2,0:T(8,128)(2,1)S(1)} fusion(bf16[20,256,256]{2,0,1:T(8,128)(2,1)} %convert_bitcast_fusion.1, bf16[256,128]{1,0:T(8,128)(2,1)S(1)} %collective-permute-done.7), kind=kOutput, calls=%fused_computation.37 | convolution fusion | flops 504299520 | bytes 3342336 | tf_op jit(solution)/shard_map/ji,wjk->wik/dot_general | solution.py:226
  74.6 0.0 copy-done.1
  74.6 1.4 %fusion.95.refs_0_ = f32[128,128]{1,0:T(8,128)S(1)} fusion(bf16[20,128,128]{1,2,0:T(8,128)(2,1)S(1)} %fusion.53, bf16[20,128,128]{1,2,0:T(8,128)(2,1)S(1)} %fusion.50, f32[256,256]{1,0:T(8,128)S(1)} %copy-done.1, f32[256,256]{1,0:T(8,128)} %get-tuple-element.19.start_ref), kind=kOutput, calls=%fused_computation.61 | convolution fusion | flops 168165376 | bytes 1572864 | tf_op jit(solution)/shard_map/wij,wjk->ik/dot_general | solution.py:45
  75.9 0.0 copy-start.5
  75.9 0.5 fusion.94.refs_1_
  76.5 0.0 copy-start.6
  76.5 0.5 fusion.93.refs_2_
  77.0 0.0 copy-start.7
  77.0 1.1 %fusion.92.refs_3_ = f32[128,128]{1,0:T(8,128)} fusion(bf16[20,128,128]{1,2,0:T(8,128)(2,1)S(1)} %fusion.53, bf16[20,128,128]{1,2,0:T(8,128)(2,1)S(1)} %fusion.50, f32[256,256]{1,0:T(8,128)S(1)} %copy-done.1, f32[128,128]{1,0:T(8,128)S(1)} %fusion.93.refs_2_), kind=kOutput, calls=%fused_computation.58 | convolution fusion | flops 168148992 | bytes 1572864 | tf_op jit(solution)/shard_map/wij,wjk->ik/dot_general | solution.py:45
  78.2 0.0 copy-done.5
  78.2 0.0 copy-done.7
  78.2 1.9 %shard_map.79 = f32[8,128]{1,0:T(8,128)} custom-call(f32[256,256]{1,0:T(8,128)} %get-tuple-element.19.start_ref, f32[256,256]{1,0:T(8,128)} %broadcast_multiply_fusion.mask_ref, f32[128,128]{1,0:T(8,128)} %copy-done.5, f32[128,128]{1,0:T(8,128)} %copy-done.6, f32[128,128]{1,0:T(8,128)} %copy-done.7, f32[128,128]{1,0:T(8,128)} %fusion.92.refs_3_), custom_call_target="tpu_custom_call" | custom-call | tf_op jit(solution)/shard_map/pallas_call | solution.py:193
  80.1 1.3 %collective-permute-start.9 = (f32[8,128]{1,0:T(8,128)}, f32[8,128]{1,0:T(8,128)S(1)}, u32[]{:S(2)}, u32[]{:S(2)}) collective-permute-start(f32[8,128]{1,0:T(8,128)} %shard_map.79), channel_id=1, source_target_pairs={{0,1},{1,0},{2,3},{3,2},{4,5},{5,4},{6,7},{7,6},{8,9},{9,8},{10,11... | collective-permute-start | bytes 12296 | tf_op jit(solution)/shard_map/ppermute | solution.py:33
  81.3 2.5 %collective-permute-done.9 = f32[8,128]{1,0:T(8,128)S(1)} collective-permute-done((f32[8,128]{1,0:T(8,128)}, f32[8,128]{1,0:T(8,128)S(1)}, u32[]{:S(2)}, u32[]{:S(2)}) %collective-permute-start.9) | collective-permute-done | bytes 4128 | tf_op jit(solution)/shard_map/ppermute | solution.py:33
  83.9 0.7 add.35
  84.6 0.3 collective-permute-start.10
  84.9 4.8 %collective-permute-done.10 = f32[8,128]{1,0:T(8,128)S(1)} collective-permute-done((f32[8,128]{1,0:T(8,128)S(1)}, f32[8,128]{1,0:T(8,128)S(1)}, u32[]{:S(2)}, u32[]{:S(2)}) %collective-permute-start.10) | collective-permute-done | bytes 4128 | tf_op jit(solution)/shard_map/ppermute | solution.py:33
  89.7 0.3 collective-permute-start.11
  90.0 3.3 %collective-permute-done.11 = f32[8,128]{1,0:T(8,128)S(1)} collective-permute-done((f32[8,128]{1,0:T(8,128)S(1)}, f32[8,128]{1,0:T(8,128)S(1)}, u32[]{:S(2)}, u32[]{:S(2)}) %collective-permute-start.11) | collective-permute-done | bytes 4128 | tf_op jit(solution)/shard_map/ppermute | solution.py:33
  93.3 0.3 collective-permute-start.12
  93.6 4.2 %collective-permute-done.12 = f32[8,128]{1,0:T(8,128)S(1)} collective-permute-done((f32[8,128]{1,0:T(8,128)S(1)}, f32[8,128]{1,0:T(8,128)S(1)}, u32[]{:S(2)}, u32[]{:S(2)}) %collective-permute-start.12) | collective-permute-done | bytes 4128 | tf_op jit(solution)/shard_map/ppermute | solution.py:33
  97.8 4.5 %collective-permute-start.13 = (f32[8,128]{1,0:T(8,128)S(1)}, f32[8,128]{1,0:T(8,128)S(1)}, u32[]{:S(2)}, u32[]{:S(2)}) collective-permute-start(f32[8,128]{1,0:T(8,128)S(1)} %add.38), channel_id=1, source_target_pairs={{0,16},{1,17},{2,18},{3,19},{4,20},{5,21},{6,22},{7,23},{8,24},{9,... | collective-permute-start | bytes 12296 | tf_op jit(solution)/shard_map/ppermute | solution.py:33
  102.3 3.0 %collective-permute-done.13 = f32[8,128]{1,0:T(8,128)S(1)} collective-permute-done((f32[8,128]{1,0:T(8,128)S(1)}, f32[8,128]{1,0:T(8,128)S(1)}, u32[]{:S(2)}, u32[]{:S(2)}) %collective-permute-start.13) | collective-permute-done | bytes 4128 | tf_op jit(solution)/shard_map/ppermute | solution.py:33
  105.3 0.6 add.39.total_ref
  105.9 2.2 %shard_map.80 = (f32[256,256]{1,0:T(8,128)}, f32[1,1]{1,0:T(1,128)}) custom-call(f32[8,128]{1,0:T(8,128)} %add.39.total_ref, f32[256,256]{1,0:T(8,128)} %get-tuple-element.19.start_ref, f32[256,256]{1,0:T(8,128)} %broadcast_multiply_fusion.mask_ref, f32[128,128]{1,0:T(8,128)} %copy-done.5, f32[128,128]{1,0:T(8,128)} %copy-done.6, f32[128,128]{1,0:T(8,128)} %copy-done.7), custom_call_target="tpu_custom_call" | custom-call | tf_op jit(solution)/shard_map/pallas_call | solution.py:213
  (8 shorter events, 0.0 us)
Async XLA Ops:
  0.6 39.7 %copy-start = (f32[20,20]{1,0:T(8,128)S(1)}, f32[20,20]{1,0:T(8,128)}, u32[]{:S(2)}) copy-start(f32[20,20]{1,0:T(8,128)} %param.9) | copy-start | bytes 4804
  0.6 32.6 %collective-permute-start.1 = (bf16[20,256,256]{2,1,0:T(8,128)(2,1)}, bf16[20,256,256]{2,1,0:T(8,128)(2,1)}, u32[]{:S(2)}, u32[]{:S(2)}) collective-permute-start(bf16[20,256,256]{2,1,0:T(8,128)(2,1)} %bitcast.192), channel_id=1, source_target_pairs={{0,32},{32,64},{64,96},{96,128},{128,160},{160,192},{192,224},{224... | collective-permute-start | bytes 7864328 | tf_op jit(solution)/shard_map/ppermute | solution.py:18
  0.7 32.6 %collective-permute-start.2 = (bf16[20,256,256]{2,1,0:T(8,128)(2,1)}, bf16[20,256,256]{2,1,0:T(8,128)(2,1)S(1)}, u32[]{:S(2)}, u32[]{:S(2)}) collective-permute-start(bf16[20,256,256]{2,1,0:T(8,128)(2,1)} %bitcast.193), channel_id=1, source_target_pairs={{0,224},{32,0},{64,32},{96,64},{128,96},{160,128},{192,160},{224,1... | collective-permute-start | bytes 7864328 | tf_op jit(solution)/shard_map/ppermute | solution.py:18
  10.2 5.1 %copy-start.2 = (f32[256,256]{1,0:T(8,128)}, f32[256,256]{1,0:T(8,128)S(1)}, u32[]{:S(2)}) copy-start(f32[256,256]{1,0:T(8,128)S(1)} %fusion.67.refs_0_.refs_1_) | copy-start | bytes 786436
  15.3 5.1 %copy-start.3 = (f32[256,256]{1,0:T(8,128)}, f32[256,256]{1,0:T(8,128)S(1)}, u32[]{:S(2)}) copy-start(f32[256,256]{1,0:T(8,128)S(1)} %fusion.73.refs_1_.refs_2_) | copy-start | bytes 786436
  20.4 5.8 %copy-start.4 = (f32[256,256]{1,0:T(8,128)}, f32[256,256]{1,0:T(8,128)S(1)}, u32[]{:S(2)}) copy-start(f32[256,256]{1,0:T(8,128)S(1)} %fusion.79.refs_2_.refs_3_) | copy-start | bytes 786436
  28.6 3.8 %collective-permute-start = (f32[8,128]{1,0:T(8,128)}, f32[8,128]{1,0:T(8,128)S(1)}, u32[]{:S(2)}, u32[]{:S(2)}) collective-permute-start(f32[8,128]{1,0:T(8,128)} %shard_map.77), channel_id=1, source_target_pairs={{0,1},{1,0},{2,3},{3,2},{4,5},{5,4},{6,7},{7,6},{8,9},{9,8},{10,11... | collective-permute-start | bytes 12296 | tf_op jit(solution)/shard_map/ppermute | solution.py:33
  33.3 5.1 %collective-permute-start.3 = (f32[8,128]{1,0:T(8,128)S(1)}, f32[8,128]{1,0:T(8,128)S(1)}, u32[]{:S(2)}, u32[]{:S(2)}) collective-permute-start(f32[8,128]{1,0:T(8,128)S(1)} %add.30), channel_id=1, source_target_pairs={{0,2},{1,3},{2,0},{3,1},{4,6},{5,7},{6,4},{7,5},{8,10},{9,11},{10,... | collective-permute-start | bytes 12296 | tf_op jit(solution)/shard_map/ppermute | solution.py:33
  38.4 8.8 %collective-permute-start.4 = (f32[8,128]{1,0:T(8,128)S(1)}, f32[8,128]{1,0:T(8,128)S(1)}, u32[]{:S(2)}, u32[]{:S(2)}) collective-permute-start(f32[8,128]{1,0:T(8,128)S(1)} %add.31), channel_id=1, source_target_pairs={{0,4},{1,5},{2,6},{3,7},{4,0},{5,1},{6,2},{7,3},{8,12},{9,13},{10,... | collective-permute-start | bytes 12296 | tf_op jit(solution)/shard_map/ppermute | solution.py:33
  47.1 8.1 %collective-permute-start.5 = (f32[8,128]{1,0:T(8,128)S(1)}, f32[8,128]{1,0:T(8,128)S(1)}, u32[]{:S(2)}, u32[]{:S(2)}) collective-permute-start(f32[8,128]{1,0:T(8,128)S(1)} %add.32), channel_id=1, source_target_pairs={{0,8},{1,9},{2,10},{3,11},{4,12},{5,13},{6,14},{7,15},{8,0},{9,1},... | collective-permute-start | bytes 12296 | tf_op jit(solution)/shard_map/ppermute | solution.py:33
  55.2 7.5 %collective-permute-start.6 = (f32[8,128]{1,0:T(8,128)S(1)}, f32[8,128]{1,0:T(8,128)S(1)}, u32[]{:S(2)}, u32[]{:S(2)}) collective-permute-start(f32[8,128]{1,0:T(8,128)S(1)} %add.33), channel_id=1, source_target_pairs={{0,16},{1,17},{2,18},{3,19},{4,20},{5,21},{6,22},{7,23},{8,24},{9,... | collective-permute-start | bytes 12296 | tf_op jit(solution)/shard_map/ppermute | solution.py:33
  65.8 2.2 %collective-permute-start.8 = (bf16[128,256]{1,0:T(8,128)(2,1)}, bf16[128,256]{1,0:T(8,128)(2,1)S(1)}, u32[]{:S(2)}, u32[]{:S(2)}) collective-permute-start(bf16[128,256]{1,0:T(8,128)(2,1)} %get-tuple-element.23), channel_id=1, source_target_pairs={{0,224},{32,0},{64,32},{96,64},{128,96},{160,128},{192,160},{224,1... | collective-permute-start | bytes 196616 | tf_op jit(solution)/shard_map/ppermute | solution.py:18
  65.8 5.5 %collective-permute-start.7 = (bf16[256,128]{1,0:T(8,128)(2,1)}, bf16[256,128]{1,0:T(8,128)(2,1)S(1)}, u32[]{:S(2)}, u32[]{:S(2)}) collective-permute-start(bf16[256,128]{1,0:T(8,128)(2,1)} %get-tuple-element.21), channel_id=1, source_target_pairs={{0,32},{32,64},{64,96},{96,128},{128,160},{160,192},{192,224},{224... | collective-permute-start | bytes 196616 | tf_op jit(solution)/shard_map/ppermute | solution.py:18
  71.3 3.3 %copy-start.1 = (f32[256,256]{1,0:T(8,128)S(1)}, f32[256,256]{1,0:T(8,128)}, u32[]{:S(2)}) copy-start(f32[256,256]{1,0:T(8,128)} %broadcast_multiply_fusion.mask_ref) | copy-start | bytes 786436
  75.9 2.2 %copy-start.5 = (f32[128,128]{1,0:T(8,128)}, f32[128,128]{1,0:T(8,128)S(1)}, u32[]{:S(2)}) copy-start(f32[128,128]{1,0:T(8,128)S(1)} %fusion.95.refs_0_) | copy-start | bytes 196612
  76.5 1.7 %copy-start.6 = (f32[128,128]{1,0:T(8,128)}, f32[128,128]{1,0:T(8,128)S(1)}, u32[]{:S(2)}) copy-start(f32[128,128]{1,0:T(8,128)S(1)} %fusion.94.refs_1_) | copy-start | bytes 196612
  77.0 1.2 %copy-start.7 = (f32[128,128]{1,0:T(8,128)}, f32[128,128]{1,0:T(8,128)S(1)}, u32[]{:S(2)}) copy-start(f32[128,128]{1,0:T(8,128)S(1)} %fusion.93.refs_2_) | copy-start | bytes 196612
  80.1 3.8 %collective-permute-start.9 = (f32[8,128]{1,0:T(8,128)}, f32[8,128]{1,0:T(8,128)S(1)}, u32[]{:S(2)}, u32[]{:S(2)}) collective-permute-start(f32[8,128]{1,0:T(8,128)} %shard_map.79), channel_id=1, source_target_pairs={{0,1},{1,0},{2,3},{3,2},{4,5},{5,4},{6,7},{7,6},{8,9},{9,8},{10,11... | collective-permute-start | bytes 12296 | tf_op jit(solution)/shard_map/ppermute | solution.py:33
  84.6 5.1 %collective-permute-start.10 = (f32[8,128]{1,0:T(8,128)S(1)}, f32[8,128]{1,0:T(8,128)S(1)}, u32[]{:S(2)}, u32[]{:S(2)}) collective-permute-start(f32[8,128]{1,0:T(8,128)S(1)} %add.35), channel_id=1, source_target_pairs={{0,2},{1,3},{2,0},{3,1},{4,6},{5,7},{6,4},{7,5},{8,10},{9,11},{10,... | collective-permute-start | bytes 12296 | tf_op jit(solution)/shard_map/ppermute | solution.py:33
  89.7 3.6 %collective-permute-start.11 = (f32[8,128]{1,0:T(8,128)S(1)}, f32[8,128]{1,0:T(8,128)S(1)}, u32[]{:S(2)}, u32[]{:S(2)}) collective-permute-start(f32[8,128]{1,0:T(8,128)S(1)} %add.36), channel_id=1, source_target_pairs={{0,4},{1,5},{2,6},{3,7},{4,0},{5,1},{6,2},{7,3},{8,12},{9,13},{10,... | collective-permute-start | bytes 12296 | tf_op jit(solution)/shard_map/ppermute | solution.py:33
  93.3 4.5 %collective-permute-start.12 = (f32[8,128]{1,0:T(8,128)S(1)}, f32[8,128]{1,0:T(8,128)S(1)}, u32[]{:S(2)}, u32[]{:S(2)}) collective-permute-start(f32[8,128]{1,0:T(8,128)S(1)} %add.37), channel_id=1, source_target_pairs={{0,8},{1,9},{2,10},{3,11},{4,12},{5,13},{6,14},{7,15},{8,0},{9,1},... | collective-permute-start | bytes 12296 | tf_op jit(solution)/shard_map/ppermute | solution.py:33
  97.8 7.5 %collective-permute-start.13 = (f32[8,128]{1,0:T(8,128)S(1)}, f32[8,128]{1,0:T(8,128)S(1)}, u32[]{:S(2)}, u32[]{:S(2)}) collective-permute-start(f32[8,128]{1,0:T(8,128)S(1)} %add.38), channel_id=1, source_target_pairs={{0,16},{1,17},{2,18},{3,19},{4,20},{5,21},{6,22},{7,23},{8,24},{9,... | collective-permute-start | bytes 12296 | tf_op jit(solution)/shard_map/ppermute | solution.py:33
